TPU v7x, 128 devices: a whole 4x4x4 slice. The times are simulated.
128 devices in a mesh: grp: 8 (over x, core), seq: 16 (over z, y).
Axes of the slice: x: 4, y: 4, z: 4, core: 2. Of those that a mesh axis runs over, the one named last changes fastest.
Arguments:
- queries: bfloat16 [16384, 4096], P(('grp', 'seq')), may hold values from -6 to 6
- kv_pairs: bfloat16 [2, 16384, 256], P(None, ('grp', 'seq')), may hold values from -6 to 6
- residual: bfloat16 [16384, 4096], P(('grp', 'seq')), may hold values from -30 to 30
- norm_gain: bfloat16 [4096], replicated, may hold values from 0.099609375 to 1.8984375
- o_weight: bfloat16 [4096, 4096], P('seq'), may hold values from -0.09375 to 0.09375
- w_in: bfloat16 [128, 4096, 1536], P(('grp', 'seq')), may hold values from -0.09375 to 0.09375
- w_down: bfloat16 [128, 768, 4096], P(('grp', 'seq')), may hold values from -0.21875 to 0.21875
- expert_ids: int32 [16384, 4], P(('grp', 'seq')), may hold values from 0 to 127, all different within a row; in each aligned block of 128 rows (0 to 127, 128 to 255, ...) at most 8 rows name the same one
- route_weights: float32 [16384, 4], P(('grp', 'seq')), may hold values from 0.1 to 0.6
Outputs:
- layer_out: bfloat16 [16384, 4096], P(('grp', 'seq'))
Inputs may be any that keep to these rules, and one draw needn't show every extreme that they name: `expert_ids`: within the rows of one device (aligned blocks of 128 rows) no expert is named by more than 8 rows, a bound that some block reaches; each row names 4 different experts, and every expert is named somewhere.
All inputs are finite; a program needn't handle non-finite values.
Results may differ from a plain program's by a relative error of at most 0.01.
Values may be sent and summed in bfloat16 or wider, within the bound.
No kernel may reach another device: no remote copies, remote signals or barrier semaphores. Data moves between devices by JAX's collectives and lax.ppermute only.
A program may use at most 128 MiB of HBM per device.

v0:
```python
import jax
import jax.numpy as jnp
from jax import lax
from jax.sharding import PartitionSpec as P

HD = 128


def shards(
    queries, kv_pairs, residual, norm_gain, o_weight, w_in, w_down, expert_ids, route_weights
):
    tok_dev = queries.shape[0]
    width = residual.shape[1]
    n_seq = lax.axis_size("seq")
    n_grp = lax.axis_size("grp")
    devices = n_seq * n_grp
    head_size = HD
    heads_all = queries.shape[1] // head_size
    per_device = heads_all // n_seq
    key_heads = kv_pairs.shape[2] // head_size
    sharing = heads_all // key_heads
    head_queries = lax.all_to_all(queries, "seq", split_axis=1, concat_axis=0, tiled=True)
    seq_len = head_queries.shape[0]
    kv_all = lax.all_gather(kv_pairs, "seq", axis=1, tiled=True)
    first_col = lax.axis_index("seq") * per_device // sharing * head_size
    kv_mine = lax.dynamic_slice_in_dim(kv_all, first_col, head_size, 2)
    key_rows = kv_mine[0]
    value_rows = kv_mine[1]
    block = min(512, seq_len)
    num_blocks = seq_len // block
    query_blocks = head_queries.reshape(num_blocks, block, per_device, head_size)
    key_positions = jnp.arange(seq_len, dtype=jnp.int32)
    scale = 1.0 / head_size**0.5

    def attend(operands):
        query_block, block_index = operands
        scores = (
            jnp.einsum("qhd,kd->hqk", query_block, key_rows, preferred_element_type=jnp.float32)
            * scale
        )
        query_positions = block_index * block + jnp.arange(block, dtype=jnp.int32)
        allowed = key_positions[None, :] <= query_positions[:, None]
        scores = jnp.where(allowed[None], scores, jnp.float32(-1e30))
        top_score = jnp.max(scores, axis=2, keepdims=True)
        weights = jnp.exp(scores - top_score)
        probs = (weights / jnp.sum(weights, axis=2, keepdims=True)).astype(jnp.bfloat16)
        result = jnp.einsum("hqk,kd->qhd", probs, value_rows, preferred_element_type=jnp.float32)
        return result.astype(jnp.bfloat16).reshape(block, per_device * head_size)

    attended = lax.map(attend, (query_blocks, jnp.arange(num_blocks, dtype=jnp.int32)))
    attended = attended.reshape(seq_len, per_device * head_size)
    attn_out = lax.psum_scatter(
        jnp.dot(attended, o_weight, preferred_element_type=jnp.float32).astype(jnp.bfloat16),
        "seq",
        scatter_dimension=0,
        tiled=True,
    ).astype(jnp.float32)
    mixed = residual.astype(jnp.float32) + attn_out
    mean_square = jnp.mean(mixed * mixed, axis=1, keepdims=True)
    normed = (mixed * lax.rsqrt(mean_square + 1e-06) * norm_gain.astype(jnp.float32)).astype(
        jnp.bfloat16
    )
    top_count = expert_ids.shape[1]
    capacity = 2 * tok_dev * top_count // devices
    flat_ids = expert_ids.reshape(-1)
    flat_weights = route_weights.reshape(-1)
    onehot = (flat_ids[:, None] == jnp.arange(devices, dtype=jnp.int32)[None, :]).astype(jnp.int32)
    earlier = jnp.cumsum(onehot, axis=0) - onehot
    rank = jnp.sum(earlier * onehot, axis=1)
    slot_index = flat_ids * capacity + rank
    source_rows = jnp.arange(flat_ids.shape[0], dtype=jnp.int32) // top_count
    outgoing_rows = (
        jnp.zeros((devices * capacity, width), jnp.bfloat16).at[slot_index].set(normed[source_rows])
    )
    outgoing_rows = outgoing_rows.reshape(devices, capacity, width)
    ffe_width = w_down.shape[1]
    arrived = lax.all_to_all(outgoing_rows, ("grp", "seq"), split_axis=0, concat_axis=0, tiled=True)
    flat_rows = arrived.reshape(-1, width)
    projected = jnp.dot(flat_rows, w_in[0], preferred_element_type=jnp.float32)
    hidden = (jax.nn.silu(projected[:, :ffe_width]) * projected[:, ffe_width:]).astype(jnp.bfloat16)
    produced = jnp.dot(hidden, w_down[0], preferred_element_type=jnp.float32).astype(jnp.bfloat16)
    returned = lax.all_to_all(
        produced.reshape(arrived.shape), ("grp", "seq"), split_axis=0, concat_axis=0, tiled=True
    )
    returned = returned.reshape(devices * capacity, width)
    picked = returned[slot_index].astype(jnp.float32) * flat_weights[:, None]
    combined = jnp.sum(picked.reshape(tok_dev, top_count, width), axis=1)
    return (mixed + combined).astype(jnp.bfloat16)


def solution(mesh):
    return jax.shard_map(
        shards,
        mesh=mesh,
        in_specs=(
            P(("grp", "seq"), None),
            P(None, ("grp", "seq"), None),
            P(("grp", "seq"), None),
            P(),
            P("seq", None),
            P(("grp", "seq"), None, None),
            P(("grp", "seq"), None, None),
            P(("grp", "seq"), None),
            P(("grp", "seq"), None),
        ),
        out_specs=P(("grp", "seq"), None),
        check_vma=False,
    )
```

profile of v0, /device:TPU:7, one launch (start us, length us, event | category | flops | bytes accessed | tf_op | source)
XLA Modules:
  0.0 554.3 jit_solution(18190887373898614392)
XLA Ops:
  6.5 0.7 all-gather.2.cloned.1.call-update
  7.3 2.3 copy.36
  9.6 7.8 %all-to-all-start = ((bf16[128,16,256]{2,0,1:T(8,128)(2,1)}), bf16[128,16,256]{2,0,1:T(8,128)(2,1)S(1)}, u32[]{:S(2)}, u32[]{:S(2)}) async-start(bf16[128,16,256]{2,0,1:T(8,128)(2,1)} %bitcast.97), calls=%async_computation | async-start | bytes 2097152 | tf_op jit(solution)/shard_map/all_to_all | solution.py:22
  17.4 17.2 %all-to-all-done = bf16[128,16,256]{2,0,1:T(8,128)(2,1)S(1)} async-done(((bf16[128,16,256]{2,0,1:T(8,128)(2,1)}), bf16[128,16,256]{2,0,1:T(8,128)(2,1)S(1)}, u32[]{:S(2)}, u32[]{:S(2)}) %all-to-all-start) | async-done | bytes 1048608 | tf_op jit(solution)/shard_map/all_to_all | solution.py:22
  34.6 1.2 reshape.168
  35.8 24.4 %all-gather.2.cloned.1.call-done = bf16[2,2048,256]{2,1,0:T(8,128)(2,1)} async-done(((bf16[2,128,256]{2,1,0:T(8,128)(2,1)}), bf16[2,2048,256]{2,1,0:T(8,128)(2,1)}) %all-gather.2.cloned.1.call-update) | async-done | bytes 2097168 | tf_op jit(solution)/shard_map/all_gather | solution.py:24
  60.2 2.1 dynamic-slice_bitcast_fusion
  62.3 1.0 copy.14
  63.3 66.1 %while.11 = (s32[]{:T(128)}, bf16[4,512,256]{2,1,0:T(8,128)(2,1)}, s32[4]{0:T(128)S(1)}, bf16[4,512,2,128]{3,2,1,0:T(2,128)(2,1)}, bf16[2048,128]{1,0:T(8,128)(2...) while((s32[]{:T(128)}, bf16[4,512,256]{2,1,0:T(8,128)(2,1)}, s32[4]{0:T(128)S(1)}, ...), condition=%wide.region_3.4_spmd.clone, body=%wide.region_0.3_spmd.clone.sunk | while | flops 1087506944 | bytes 22033012 | solution.py:50
  63.3 0.7 dynamic_slice.18
  64.7 0.7 iota_compare_fusion.5
  65.3 1.1 constant_dynamic-slice_fusion.2
  66.5 7.5 %fusion.52 = (f32[2,512]{1,0:T(2,128)S(1)}, f32[2,512,2048]{2,1,0:T(8,128)}) fusion(pred[512,2048]{1,0:T(8,128)(4,1)S(1)} %iota_compare_fusion.5, bf16[2048,128]{1,0:T(8,128)(2,1)} %get-tuple-element.140, bf16[1,512,2,128]{3,2,1,0:T(2,128)(2,1)S(1)} %constant_dynamic-slice_fusion.2), kind=kOutput, calls=%fused_computation.68.clone.1 | convolution fusion | flops 545261568 | bytes 10227712 | tf_op jit(solution)/shard_map/while/body/eval_jaxpr/sub | solution.py:45
  73.9 5.0 fusion.53
  79.1 0.7 constant_dynamic-update-slice_fusion.2
  79.8 0.7 dynamic_slice.18
  81.9 1.1 constant_dynamic-slice_fusion.2
  83.0 7.5 %fusion.52 = (f32[2,512]{1,0:T(2,128)S(1)}, f32[2,512,2048]{2,1,0:T(8,128)}) fusion(pred[512,2048]{1,0:T(8,128)(4,1)S(1)} %iota_compare_fusion.5, bf16[2048,128]{1,0:T(8,128)(2,1)} %get-tuple-element.140, bf16[1,512,2,128]{3,2,1,0:T(2,128)(2,1)S(1)} %constant_dynamic-slice_fusion.2), kind=kOutput, calls=%fused_computation.68.clone.1 | convolution fusion | flops 545261568 | bytes 10227712 | tf_op jit(solution)/shard_map/while/body/eval_jaxpr/sub | solution.py:45
  90.5 5.0 fusion.53
  95.6 0.7 constant_dynamic-update-slice_fusion.2
  96.4 0.7 dynamic_slice.18
  97.7 0.7 iota_compare_fusion.5
  98.4 1.1 constant_dynamic-slice_fusion.2
  99.5 7.5 %fusion.52 = (f32[2,512]{1,0:T(2,128)S(1)}, f32[2,512,2048]{2,1,0:T(8,128)}) fusion(pred[512,2048]{1,0:T(8,128)(4,1)S(1)} %iota_compare_fusion.5, bf16[2048,128]{1,0:T(8,128)(2,1)} %get-tuple-element.140, bf16[1,512,2,128]{3,2,1,0:T(2,128)(2,1)S(1)} %constant_dynamic-slice_fusion.2), kind=kOutput, calls=%fused_computation.68.clone.1 | convolution fusion | flops 545261568 | bytes 10227712 | tf_op jit(solution)/shard_map/while/body/eval_jaxpr/sub | solution.py:45
  107.0 5.0 fusion.53
  112.2 0.7 constant_dynamic-update-slice_fusion.2
  112.9 0.7 dynamic_slice.18
  114.2 0.7 iota_compare_fusion.5
  114.9 1.1 constant_dynamic-slice_fusion.2
  116.0 7.5 %fusion.52 = (f32[2,512]{1,0:T(2,128)S(1)}, f32[2,512,2048]{2,1,0:T(8,128)}) fusion(pred[512,2048]{1,0:T(8,128)(4,1)S(1)} %iota_compare_fusion.5, bf16[2048,128]{1,0:T(8,128)(2,1)} %get-tuple-element.140, bf16[1,512,2,128]{3,2,1,0:T(2,128)(2,1)S(1)} %constant_dynamic-slice_fusion.2), kind=kOutput, calls=%fused_computation.68.clone.1 | convolution fusion | flops 545261568 | bytes 10227712 | tf_op jit(solution)/shard_map/while/body/eval_jaxpr/sub | solution.py:45
  123.5 5.0 fusion.53
  128.7 0.7 constant_dynamic-update-slice_fusion.2
  129.4 9.3 %convolution_convert_fusion = bf16[2048,4096]{1,0:T(8,128)(2,1)} fusion(bf16[2048,256]{1,0:T(8,128)(2,1)} %bitcast.98, bf16[256,4096]{1,0:T(8,128)(2,1)S(1)} %copy-done), kind=kOutput, calls=%fused_computation.28 | convolution fusion | flops 4303355904 | bytes 19922944 | tf_op jit(solution)/shard_map/dot_general | solution.py:53
  138.7 0.7 copy-done.4
  140.6 109.5 %reduce-scatter.2.cloned.1.call-done = bf16[128,4096]{1,0:T(8,128)(2,1)} async-done(((bf16[2048,4096]{1,0:T(8,128)(2,1)}), bf16[128,4096]{1,0:T(8,128)(2,1)}) %reduce-scatter.2.cloned.1.call-update) | async-done | bytes 1048592 | tf_op jit(solution)/shard_map/reduce_scatter | solution.py:52
  250.1 1.6 multiply_reduce_fusion.1
  251.8 1.6 multiply_convert_fusion
  253.4 4.8 gather_fusion
  258.2 12.4 %scatter_custom_fusion = bf16[1024,4096]{1,0:T(8,128)(2,1)} fusion(s32[512]{0:T(512)S(1)} %bitcast.104, bf16[512,4096]{1,0:T(8,128)(2,1)} %gather_fusion, bf16[]{:T(256)} %constant.68.clone.1), kind=kCustom, calls=%fused_computation.35 | custom fusion | bytes 8389120 | tf_op jit(solution)/shard_map/scatter | solution.py:73
  270.7 106.3 %all_to_all.26 = bf16[128,8,4096]{2,1,0:T(8,128)(2,1)S(1)} all-to-all(bf16[128,8,4096]{2,1,0:T(8,128)(2,1)} %bitcast.94), channel_id=1, replica_groups=mesh['grp'=8,'seq'=16] {'grp','seq'}, dimensions={0} | all-to-all | bytes 16777216 | tf_op jit(solution)/shard_map/all_to_all | solution.py:77
  377.0 15.8 %fusion.24 = f32[1024,1536]{1,0:T(8,128)S(1)} fusion(bf16[1,4096,1536]{2,1,0:T(8,128)(2,1)} %param.16, bf16[128,8,4096]{2,1,0:T(8,128)(2,1)S(1)} %all_to_all.26), kind=kOutput, calls=%fused_computation.29 | convolution fusion | flops 12884901888 | bytes 27262976 | tf_op jit(solution)/shard_map/dot_general | solution.py:79
  392.8 8.9 %convert_bitcast_fusion = bf16[128,8,4096]{2,1,0:T(8,128)(2,1)} fusion(bf16[1,768,4096]{2,1,0:T(8,128)(2,1)S(1)} %bitcast.108, f32[1024,1536]{1,0:T(8,128)S(1)} %fusion.24), kind=kOutput, calls=%fused_computation.33 | convolution fusion | flops 6451363840 | bytes 20971520 | tf_op jit(solution)/shard_map/dot_general | solution.py:81
  401.7 5.6 %all-to-all-start.2 = ((bf16[128,8,4096]{2,1,0:T(8,128)(2,1)}), bf16[128,8,4096]{2,1,0:T(8,128)(2,1)}, u32[]{:S(2)}, u32[]{:S(2)}) async-start(bf16[128,8,4096]{2,1,0:T(8,128)(2,1)} %convert_bitcast_fusion), calls=%async_computation.3 | async-start | bytes 16777216 | tf_op jit(solution)/shard_map/all_to_all | solution.py:82
  407.5 103.8 %all-to-all-done.2 = bf16[128,8,4096]{2,1,0:T(8,128)(2,1)} async-done(((bf16[128,8,4096]{2,1,0:T(8,128)(2,1)}), bf16[128,8,4096]{2,1,0:T(8,128)(2,1)}, u32[]{:S(2)}, u32[]{:S(2)}) %all-to-all-start.2) | async-done | bytes 8388640 | tf_op jit(solution)/shard_map/all_to_all | solution.py:82
  511.3 13.0 %gather_fusion.1 = bf16[512,4096]{1,0:T(8,128)(2,1)} fusion(bf16[1024,4096]{1,0:T(8,128)(2,1)} %bitcast.15, s32[1024]{0:T(1024)S(1)} %pad_clamp_fusion), kind=kCustom, calls=%fused_computation.1 | custom fusion | bytes 8390656 | tf_op jit(solution)/shard_map/gather | solution.py:86
  524.3 8.5 %reshape.175 = f32[128,4,4096]{2,1,0:T(4,128)} reshape(bf16[512,4096]{1,0:T(8,128)(2,1)} %gather_fusion.1) | data formatting | bytes 12582912 | tf_op jit(solution)/shard_map/convert_element_type | solution.py:86
  532.8 11.3 %multiply_reduce_fusion = f32[128,4096]{1,0:T(8,128)} fusion(f32[128,4,4096]{2,1,0:T(4,128)} %reshape.175, f32[128,4]{1,0:T(8,128)S(1)} %copy.21), kind=kLoop, calls=%fused_computation.32 | loop fusion | flops 3670016 | bytes 10487808 | tf_op jit(solution)/shard_map/reduce_sum | solution.py:87
  544.1 3.2 add_convert_fusion
  (52 shorter events, 2.6 us)
Async XLA Ops:
  6.5 122.9 %copy-start = (bf16[256,4096]{1,0:T(8,128)(2,1)S(1)}, bf16[256,4096]{1,0:T(8,128)(2,1)}, u32[]{:S(2)}) copy-start(bf16[256,4096]{1,0:T(8,128)(2,1)} %param.15) | copy-start | bytes 6291460
  6.5 53.7 %all-gather.2.cloned.1.call-start = ((), (), s32[]{:S(2)}) async-start(), calls=%async_computation.4 | async-start | bytes 2228224 | tf_op jit(solution)/shard_map/all_gather | solution.py:24
  9.6 25.0 %all-to-all-start = ((bf16[128,16,256]{2,0,1:T(8,128)(2,1)}), bf16[128,16,256]{2,0,1:T(8,128)(2,1)S(1)}, u32[]{:S(2)}, u32[]{:S(2)}) async-start(bf16[128,16,256]{2,0,1:T(8,128)(2,1)} %bitcast.97), calls=%async_computation | async-start | bytes 2097152 | tf_op jit(solution)/shard_map/all_to_all | solution.py:22
  17.4 232.8 %reduce-scatter.2.cloned.1.call-start = ((), (), s32[]{:S(2)}) async-start(), calls=%async_computation.5 | async-start | bytes 17825792 | tf_op jit(solution)/shard_map/reduce_scatter | solution.py:52
  138.7 0.7 copy-start.4
  138.7 1.0 copy-start.3
  138.7 111.5 %copy-start.2 = (bf16[128,4096]{1,0:T(8,128)(2,1)S(1)}, bf16[128,4096]{1,0:T(8,128)(2,1)}, u32[]{:S(2)}) copy-start(bf16[128,4096]{1,0:T(8,128)(2,1)} %param.13) | copy-start | bytes 3145732
  270.7 122.1 %slice-start = ((s8[6291456]{0:T(1024)(128)(4,1)}), s8[4194304]{0:T(1024)(128)(4,1)S(1)}, s32[]{:S(2)}) async-start(s8[6291456]{0:T(1024)(128)(4,1)} %bitcast.107), calls=%async_computation.6 | async-start | bytes 8388608
  377.0 15.8 %slice-start.1 = ((s8[6291456]{0:T(1024)(128)(4,1)}), s8[2097152]{0:T(1024)(128)(4,1)S(1)}, s32[]{:S(2)}) async-start(s8[6291456]{0:T(1024)(128)(4,1)} %bitcast.107), calls=%async_computation.7 | async-start | bytes 4194304
  401.7 5.6 %copy-start.5 = (f32[128,4]{0,1:T(4,128)S(1)}, f32[128,4]{0,1:T(4,128)}, u32[]{:S(2)}) copy-start(f32[128,4]{0,1:T(4,128)} %param.19) | copy-start | bytes 6148
  401.7 109.5 %all-to-all-start.2 = ((bf16[128,8,4096]{2,1,0:T(8,128)(2,1)}), bf16[128,8,4096]{2,1,0:T(8,128)(2,1)}, u32[]{:S(2)}, u32[]{:S(2)}) async-start(bf16[128,8,4096]{2,1,0:T(8,128)(2,1)} %convert_bitcast_fusion), calls=%async_computation.3 | async-start | bytes 16777216 | tf_op jit(solution)/shard_map/all_to_all | solution.py:82
  532.8 14.5 %copy-start.1 = (bf16[256,4096]{1,0:T(8,128)(2,1)S(1)}, bf16[256,4096]{1,0:T(8,128)(2,1)}, u32[]{:S(2)}) copy-start(bf16[256,4096]{1,0:T(8,128)(2,1)} %param.15) | copy-start | bytes 6291460
Sparse Core Ops, SparseCore 0:
  9.5 50.7 all-gather.1
  138.8 111.2 reduce-scatter.1
where the time goes:
time: 565 us; the launch traced here: 554 us
  waiting for transfers between devices  256 us (45%)
  blocking collectives  106 us (19%)
  matrix products  83.9 us (15%)
  local copies, waits for them, and re-layouts  57.4 us (10%)
  other arithmetic  20.9 us (4%)
  between operations  13.8 us (2%)
  starting transfers between devices  13.4 us (2%)
    reduce_scatter x1, waiting for transfers between devices, shards(): lax.psum_scatter(jnp.dot(attended, o_weight, preferred_element_type=jnp.f...  109 us
    all_to_all x1, blocking collectives, shards(): lax.all_to_all(outgoing_rows, ('grp', 'seq'), split_axis=0, concat_axis=0...  106 us
    all_to_all x1, waiting for transfers between devices, shards(): lax.all_to_all(produced.reshape(arrived.shape), ('grp', 'seq'), split_axi...  104 us
    sub x4, matrix products, attend(): weights = jnp.exp(scores - top_score)  29.8 us
    all_gather x1, waiting for transfers between devices, shards(): kv_all = lax.all_gather(kv_pairs, 'seq', axis=1, tiled=True)  24.4 us
    dot_general x4, matrix products, attend(): jnp.einsum('hqk,kd->qhd', probs, value_rows, preferred_element_type=jnp.f...  20.1 us
    all_to_all x1, waiting for transfers between devices, shards(): lax.all_to_all(queries, 'seq', split_axis=1, concat_axis=0, tiled=True)  17.2 us
    dot_general x1, matrix products, shards(): projected = jnp.dot(flat_rows, w_in[0], preferred_element_type=jnp.float32)  15.8 us
  transfers between devices with their start and end apart: 4, of which 4 were waited for; matrix products, arithmetic and copies ran while one was open for 1% of the time, Pallas kernels for 0%

commit v1 on v0

v1 whole, which is shorter than its diff:
```python
import functools

import jax
import jax.numpy as jnp
from jax import lax
from jax.experimental import pallas as pl
from jax.experimental.pallas import tpu as pltpu
from jax.sharding import PartitionSpec as P

HD = 128
Q_BLOCK = 256


def _attend_kernel(q_ref, k_ref, v_ref, o_ref, *, block, scale):
    qi = pl.program_id(1)
    q = q_ref[...]
    k = k_ref[...]
    length = k.shape[0]
    scores = lax.dot_general(
        q, k, (((1,), (1,)), ((), ())), preferred_element_type=jnp.float32
    ) * scale
    q_pos = qi * block + lax.broadcasted_iota(jnp.int32, (block, length), 0)
    k_pos = lax.broadcasted_iota(jnp.int32, (block, length), 1)
    scores = jnp.where(k_pos <= q_pos, scores, jnp.float32(-1e30))
    top = jnp.max(scores, axis=1, keepdims=True)
    weights = jnp.exp(scores - top)
    total = jnp.sum(weights, axis=1, keepdims=True)
    probs = (weights / total).astype(jnp.bfloat16)
    o_ref[...] = jnp.dot(probs, v_ref[...], preferred_element_type=jnp.float32).astype(
        o_ref.dtype
    )


def attention(packed, heads, head_size):
    seq_len = packed.shape[0]
    block = min(Q_BLOCK, seq_len)
    kernel = functools.partial(_attend_kernel, block=block, scale=1.0 / head_size**0.5)
    return pl.pallas_call(
        kernel,
        out_shape=jax.ShapeDtypeStruct((seq_len, heads * head_size), jnp.bfloat16),
        grid=(heads, seq_len // block),
        in_specs=[
            pl.BlockSpec((block, head_size), lambda h, i: (i, h)),
            pl.BlockSpec((seq_len, head_size), lambda h, i: (0, heads)),
            pl.BlockSpec((seq_len, head_size), lambda h, i: (0, heads + 1)),
        ],
        out_specs=pl.BlockSpec((block, head_size), lambda h, i: (i, h)),
        compiler_params=pltpu.CompilerParams(
            dimension_semantics=("arbitrary", "arbitrary"),
            vmem_limit_bytes=48 * 1024 * 1024,
        ),
    )(packed, packed, packed)


def shards(
    queries, kv_pairs, residual, norm_gain, o_weight, w_in, w_down, expert_ids, route_weights
):
    tok_dev = queries.shape[0]
    width = residual.shape[1]
    n_seq = lax.axis_size("seq")
    n_grp = lax.axis_size("grp")
    devices = n_seq * n_grp
    head_size = HD
    heads_all = queries.shape[1] // head_size
    per_device = heads_all // n_seq
    key_heads = kv_pairs.shape[2] // head_size
    sharing = heads_all // key_heads
    assert sharing % per_device == 0

    q_send = queries.reshape(tok_dev, n_seq, per_device * head_size).transpose(1, 0, 2)
    kv_heads = kv_pairs.reshape(2, tok_dev, key_heads, head_size)
    head_of_dest = (jnp.arange(n_seq) * per_device) // sharing
    kv_send = jnp.take(kv_heads, head_of_dest, axis=2)
    kv_send = kv_send.transpose(2, 1, 0, 3).reshape(n_seq, tok_dev, 2 * head_size)
    send = jnp.concatenate([q_send, kv_send], axis=2)
    packed = lax.all_to_all(send, "seq", split_axis=0, concat_axis=0, tiled=True)
    seq_len = n_seq * tok_dev
    packed = packed.reshape(seq_len, (per_device + 2) * head_size)

    attended = attention(packed, per_device, head_size)
    attn_out = lax.psum_scatter(
        jnp.dot(attended, o_weight, preferred_element_type=jnp.float32).astype(jnp.bfloat16),
        "seq",
        scatter_dimension=0,
        tiled=True,
    ).astype(jnp.float32)
    mixed = residual.astype(jnp.float32) + attn_out
    mean_square = jnp.mean(mixed * mixed, axis=1, keepdims=True)
    normed = (mixed * lax.rsqrt(mean_square + 1e-06) * norm_gain.astype(jnp.float32)).astype(
        jnp.bfloat16
    )

    top_count = expert_ids.shape[1]
    capacity = 2 * tok_dev * top_count // devices
    slots = devices * capacity
    flat_ids = expert_ids.reshape(-1)
    flat_weights = route_weights.reshape(-1)
    n_flat = flat_ids.shape[0]
    onehot = (flat_ids[:, None] == jnp.arange(devices, dtype=jnp.int32)[None, :]).astype(
        jnp.bfloat16
    )
    row = lax.broadcasted_iota(jnp.int32, (n_flat, n_flat), 0)
    col = lax.broadcasted_iota(jnp.int32, (n_flat, n_flat), 1)
    before = (col < row).astype(jnp.bfloat16)
    earlier = jnp.dot(before, onehot, preferred_element_type=jnp.float32)
    rank = jnp.sum(earlier * onehot.astype(jnp.float32), axis=1).astype(jnp.int32)
    slot_index = flat_ids * capacity + rank
    picks = slot_index[:, None] == jnp.arange(slots, dtype=jnp.int32)[None, :]
    token_slots = jnp.any(picks.reshape(tok_dev, top_count, slots), axis=1).astype(jnp.bfloat16)
    outgoing_rows = lax.dot_general(
        token_slots, normed, (((0,), (0,)), ((), ())), preferred_element_type=jnp.float32
    ).astype(jnp.bfloat16)
    outgoing_rows = outgoing_rows.reshape(devices, capacity, width)
    ffe_width = w_down.shape[1]
    arrived = lax.all_to_all(outgoing_rows, ("grp", "seq"), split_axis=0, concat_axis=0, tiled=True)
    flat_rows = arrived.reshape(-1, width)
    projected = jnp.dot(flat_rows, w_in[0], preferred_element_type=jnp.float32)
    hidden = (jax.nn.silu(projected[:, :ffe_width]) * projected[:, ffe_width:]).astype(jnp.bfloat16)
    produced = jnp.dot(hidden, w_down[0], preferred_element_type=jnp.float32).astype(jnp.bfloat16)
    returned = lax.all_to_all(
        produced.reshape(arrived.shape), ("grp", "seq"), split_axis=0, concat_axis=0, tiled=True
    )
    returned = returned.reshape(slots, width)
    picked = jnp.dot(picks.astype(jnp.bfloat16), returned, preferred_element_type=jnp.float32)
    picked = picked * flat_weights[:, None]
    combined = jnp.sum(picked.reshape(tok_dev, top_count, width), axis=1)
    return (mixed + combined).astype(jnp.bfloat16)


def solution(mesh):
    return jax.shard_map(
        shards,
        mesh=mesh,
        in_specs=(
            P(("grp", "seq"), None),
            P(None, ("grp", "seq"), None),
            P(("grp", "seq"), None),
            P(),
            P("seq", None),
            P(("grp", "seq"), None, None),
            P(("grp", "seq"), None, None),
            P(("grp", "seq"), None),
            P(("grp", "seq"), None),
        ),
        out_specs=P(("grp", "seq"), None),
        check_vma=False,
    )
```

time: 565 us -> 484 us (0.86); the launches traced: 554 us -> 481 us
  waiting for transfers between devices: 256 us -> 211 us
  matrix products: 83.9 us -> 46.9 us
  local copies, waits for them, and re-layouts: 57.4 us -> 22.4 us
  blocking collectives: 106 us -> 141 us
  Pallas kernels: 0 us -> 22.6 us
  starting transfers between devices: 13.4 us -> 5.62 us
    all_to_all x0 -> x1, blocking collectives: none -> 35 us  [shards(): lax.all_to_all(send, 'seq', split_axis=0, concat_axis=0, tiled=True)]
    sub x4 -> x0, matrix products: 29.8 us -> none  [attend(): weights = jnp.exp(scores - top_score)]
    all_gather x1 -> x0, waiting for transfers between devices: 24.4 us -> none  [shards(): kv_all = lax.all_gather(kv_pairs, 'seq', axis=1, tiled=True)]
    pallas_call x0 -> x1, Pallas kernels: none -> 22.6 us  [attention(): pl.pallas_call(kernel, out_shape=jax.ShapeDtypeStruct((seq_len, heads * h...]
    all_to_all x1 -> x0, waiting for transfers between devices: 17.2 us -> none  [shards(): lax.all_to_all(queries, 'seq', split_axis=1, concat_axis=0, tiled=True)]
    gather x2 -> x1, local copies, waits for them, and re-layouts: 17.8 us -> 1.65 us  [shards(): kv_send = jnp.take(kv_heads, head_of_dest, axis=2)]
    scatter x1 -> x0, local copies, waits for them, and re-layouts: 12.4 us -> none  [shards(): jnp.zeros((devices * capacity, width), jnp.bfloat16).at[slot_index]]
    reshape x1 -> x3, local copies, waits for them, and re-layouts: 1.2 us -> 10 us  [the longest x1 9.76 us: shards(): combined = jnp.sum(picked.reshape(tok_dev, top_count, width), axis=1)]
  transfers between devices with their start and end apart: 4 -> 2, of which waited for: 4 -> 2; matrix products, arithmetic and copies ran while one was open for 1% -> 0% of each run, Pallas kernels for 0% -> 0%
where the time goes in v1:
time: 484 us; the launch traced here: 481 us
  waiting for transfers between devices  211 us (44%)
  blocking collectives  141 us (29%)
  matrix products  46.9 us (10%)
  Pallas kernels  22.6 us (5%)
  local copies, waits for them, and re-layouts  22.4 us (5%)
  other arithmetic  18.3 us (4%)
  between operations  13.6 us (3%)
  starting transfers between devices  5.62 us (1%)
    reduce_scatter x1, waiting for transfers between devices, shards(): lax.psum_scatter(jnp.dot(attended, o_weight, preferred_element_type=jnp.f...  108 us
    all_to_all x1, blocking collectives, shards(): lax.all_to_all(outgoing_rows, ('grp', 'seq'), split_axis=0, concat_axis=0...  106 us
    all_to_all x1, waiting for transfers between devices, shards(): lax.all_to_all(produced.reshape(arrived.shape), ('grp', 'seq'), split_axi...  103 us
    all_to_all x1, blocking collectives, shards(): lax.all_to_all(send, 'seq', split_axis=0, concat_axis=0, tiled=True)  35 us
    pallas_call x1, Pallas kernels, attention(): pl.pallas_call(kernel, out_shape=jax.ShapeDtypeStruct((seq_len, heads * h...  22.6 us
    dot_general x1, matrix products, shards(): projected = jnp.dot(flat_rows, w_in[0], preferred_element_type=jnp.float32)  15.8 us
    dot_general x1, matrix products, shards(): jnp.dot(picks.astype(jnp.bfloat16), returned, preferred_element_type=jnp....  10.2 us
    reduce_sum x1, other arithmetic, shards(): combined = jnp.sum(picked.reshape(tok_dev, top_count, width), axis=1)  10.2 us
  transfers between devices with their start and end apart: 2, of which 2 were waited for; matrix products, arithmetic and copies ran while one was open for 0% of the time, Pallas kernels for 0%

profile of v1, /device:TPU:7, one launch (start us, length us, event | category | flops | bytes accessed | tf_op | source)
XLA Modules:
  0.0 480.8 jit_solution(1168316395557426771)
XLA Ops:
  6.5 0.0 copy-start
  6.5 0.0 reduce-scatter.2.cloned.1.call-start
  6.6 1.2 copy.38
  7.7 0.1 copy.39
  7.9 1.7 gather_fusion
  9.5 1.4 select_bitcast_fusion
  10.9 1.3 copy.40
  12.2 1.6 copy.37
  13.9 1.4 pad_maximum_fusion
  15.3 35.0 %all_to_all.15 = bf16[16,128,512]{1,2,0:T(8,128)(2,1)} all-to-all(bf16[16,128,512]{1,2,0:T(8,128)(2,1)S(1)} %pad_maximum_fusion), channel_id=1, replica_groups=mesh['grp'=8,'seq'=16] {'seq'}, dimensions={0} | all-to-all | bytes 4194304 | tf_op jit(solution)/shard_map/all_to_all | solution.py:76
  50.2 3.9 copy.41
  54.2 0.0 copy-start.2
  54.2 1.6 copy-done.2
  55.7 22.6 %shard_map.91 = bf16[2048,256]{1,0:T(8,128)(2,1)S(1)} custom-call(bf16[2048,512]{1,0:T(8,128)(2,1)S(1)} %bitcast.31, bf16[2048,512]{1,0:T(8,128)(2,1)S(1)} %bitcast.32, bf16[2048,512]{1,0:T(8,128)(2,1)S(1)} %bitcast.33), custom_call_target="tpu_custom_call" | custom-call | tf_op jit(solution)/shard_map/pallas_call | solution.py:38
  78.3 0.0 copy-done
  78.3 8.1 %convolution_convert_fusion = bf16[2048,4096]{1,0:T(8,128)(2,1)} fusion(bf16[2048,256]{1,0:T(8,128)(2,1)S(1)} %shard_map.91, bf16[256,4096]{1,0:T(8,128)(2,1)S(1)} %copy-done), kind=kOutput, calls=%fused_computation.1 | convolution fusion | flops 4303355904 | bytes 19922944 | tf_op jit(solution)/shard_map/dot_general | solution.py:82
  86.4 0.0 copy-start.5
  86.4 0.0 copy-start.4
  86.4 0.0 copy-start.3
  86.4 0.0 reduce-scatter.2.cloned.1.call-update
  86.4 0.7 copy-done.5
  87.1 0.1 copy.42
  87.2 0.1 reshape.131
  87.3 0.3 fusion.13
  87.6 0.1 convert_element_type.53
  87.7 0.1 copy.43
  87.8 0.0 copy-done.4
  87.8 0.4 fusion.10
  88.2 107.7 %reduce-scatter.2.cloned.1.call-done = bf16[128,4096]{1,0:T(8,128)(2,1)} async-done(((bf16[2048,4096]{1,0:T(8,128)(2,1)}), bf16[128,4096]{1,0:T(8,128)(2,1)}) %reduce-scatter.2.cloned.1.call-update) | async-done | bytes 1048592 | tf_op jit(solution)/shard_map/reduce_scatter | solution.py:81
  195.9 0.0 copy-done.3
  195.9 1.6 multiply_reduce_fusion
  197.6 3.7 convert_bitcast_fusion.1
  201.2 0.0 slice-start
  201.2 105.8 %all_to_all.16 = bf16[128,8,4096]{2,1,0:T(8,128)(2,1)S(1)} all-to-all(bf16[128,8,4096]{2,1,0:T(8,128)(2,1)S(1)} %convert_bitcast_fusion.1), channel_id=1, replica_groups=mesh['grp'=8,'seq'=16] {'grp','seq'}, dimensions={0} | all-to-all | bytes 16777216 | tf_op jit(solution)/shard_map/all_to_all | solution.py:115
  307.0 15.8 %fusion = f32[1024,1536]{1,0:T(8,128)S(1)} fusion(bf16[1,4096,1536]{2,1,0:T(8,128)(2,1)} %param.14, bf16[128,8,4096]{2,1,0:T(8,128)(2,1)S(1)} %all_to_all.16), kind=kOutput, calls=%fused_computation.2 | convolution fusion | flops 12884901888 | bytes 27262976 | tf_op jit(solution)/shard_map/dot_general | solution.py:117
  322.8 0.0 slice-done
  322.9 0.0 slice-done.1
  322.9 8.9 %convert_bitcast_fusion = bf16[128,8,4096]{2,1,0:T(8,128)(2,1)} fusion(bf16[1,768,4096]{2,1,0:T(8,128)(2,1)S(1)} %bitcast.38, f32[1024,1536]{1,0:T(8,128)S(1)} %fusion), kind=kOutput, calls=%fused_computation.7 | convolution fusion | flops 6451363840 | bytes 20971520 | tf_op jit(solution)/shard_map/dot_general | solution.py:119
  331.7 5.6 %all-to-all-start.2 = ((bf16[128,8,4096]{2,1,0:T(8,128)(2,1)}), bf16[128,8,4096]{2,1,0:T(8,128)(2,1)}, u32[]{:S(2)}, u32[]{:S(2)}) async-start(bf16[128,8,4096]{2,1,0:T(8,128)(2,1)} %convert_bitcast_fusion), calls=%async_computation.3 | async-start | bytes 16777216 | tf_op jit(solution)/shard_map/all_to_all | solution.py:120
  337.4 0.0 copy-done.6
  337.4 0.1 copy.44
  337.5 0.1 mul.82
  337.6 103.0 %all-to-all-done.2 = bf16[128,8,4096]{2,1,0:T(8,128)(2,1)} async-done(((bf16[128,8,4096]{2,1,0:T(8,128)(2,1)}), bf16[128,8,4096]{2,1,0:T(8,128)(2,1)}, u32[]{:S(2)}, u32[]{:S(2)}) %all-to-all-start.2) | async-done | bytes 8388640 | tf_op jit(solution)/shard_map/all_to_all | solution.py:120
  440.6 10.2 %fusion.5 = f32[512,4096]{1,0:T(8,128)} fusion(bf16[128,8,4096]{2,1,0:T(8,128)(2,1)} %all-to-all-done.2, f32[512]{0:T(512)S(1)} %mul.82, s32[512]{0:T(512)S(1)} %multiply_add_fusion.1), kind=kOutput, calls=%fused_computation.9 | convolution fusion | flops 4297588736 | bytes 16781312 | tf_op jit(solution)/shard_map/dot_general | solution.py:124
  450.8 9.8 %reshape.136 = f32[128,4,4096]{2,1,0:T(4,128)} reshape(f32[512,4096]{1,0:T(8,128)} %fusion.5) | data formatting | bytes 16777216 | tf_op jit(solution)/shard_map/reshape | solution.py:126
  460.6 10.2 %reduce_sum.29 = f32[128,4096]{1,0:T(8,128)} reduce(f32[128,4,4096]{2,1,0:T(4,128)} %reshape.136, f32[]{:T(128)} %constant.40.clone.1), dimensions={1}, to_apply=%region_4.5 | reduce | flops 1572864 | bytes 10485764 | tf_op jit(solution)/shard_map/reduce_sum | solution.py:126
  470.8 3.2 add_convert_fusion
  473.9 0.0 copy-done.1
  (12 shorter events, 0.1 us)
Async XLA Ops:
  6.5 71.8 %copy-start = (bf16[256,4096]{1,0:T(8,128)(2,1)S(1)}, bf16[256,4096]{1,0:T(8,128)(2,1)}, u32[]{:S(2)}) copy-start(bf16[256,4096]{1,0:T(8,128)(2,1)} %param.13) | copy-start | bytes 6291460
  6.5 189.4 %reduce-scatter.2.cloned.1.call-start = ((), (), s32[]{:S(2)}) async-start(), calls=%async_computation.4 | async-start | bytes 17825792 | tf_op jit(solution)/shard_map/reduce_scatter | solution.py:81
  54.2 1.6 copy-start.2
  86.4 0.7 copy-start.5
  86.4 1.4 copy-start.4
  86.4 109.5 %copy-start.3 = (bf16[128,4096]{1,0:T(8,128)(2,1)S(1)}, bf16[128,4096]{1,0:T(8,128)(2,1)}, u32[]{:S(2)}) copy-start(bf16[128,4096]{1,0:T(8,128)(2,1)} %param.11) | copy-start | bytes 3145732
  201.2 121.6 %slice-start = ((s8[6291456]{0:T(1024)(128)(4,1)}), s8[4194304]{0:T(1024)(128)(4,1)S(1)}, s32[]{:S(2)}) async-start(s8[6291456]{0:T(1024)(128)(4,1)} %bitcast.37), calls=%async_computation.5 | async-start | bytes 8388608
  307.0 15.8 %slice-start.1 = ((s8[6291456]{0:T(1024)(128)(4,1)}), s8[2097152]{0:T(1024)(128)(4,1)S(1)}, s32[]{:S(2)}) async-start(s8[6291456]{0:T(1024)(128)(4,1)} %bitcast.37), calls=%async_computation.6 | async-start | bytes 4194304
  331.7 5.6 %copy-start.6 = (f32[128,4]{0,1:T(4,128)S(1)}, f32[128,4]{0,1:T(4,128)}, u32[]{:S(2)}) copy-start(f32[128,4]{0,1:T(4,128)} %param.17) | copy-start | bytes 6148
  331.7 108.9 %all-to-all-start.2 = ((bf16[128,8,4096]{2,1,0:T(8,128)(2,1)}), bf16[128,8,4096]{2,1,0:T(8,128)(2,1)}, u32[]{:S(2)}, u32[]{:S(2)}) async-start(bf16[128,8,4096]{2,1,0:T(8,128)(2,1)} %convert_bitcast_fusion), calls=%async_computation.3 | async-start | bytes 16777216 | tf_op jit(solution)/shard_map/all_to_all | solution.py:120
  460.6 13.4 %copy-start.1 = (bf16[256,4096]{1,0:T(8,128)(2,1)S(1)}, bf16[256,4096]{1,0:T(8,128)(2,1)}, u32[]{:S(2)}) copy-start(bf16[256,4096]{1,0:T(8,128)(2,1)} %param.13) | copy-start | bytes 6291460
Sparse Core Ops, SparseCore 0:
  86.5 109.3 reduce-scatter.1

commit v2 on v1

--- a/solution.py
+++ b/solution.py
@@ -121,9 +121,14 @@
         produced.reshape(arrived.shape), ("grp", "seq"), split_axis=0, concat_axis=0, tiled=True
     )
     returned = returned.reshape(slots, width)
-    picked = jnp.dot(picks.astype(jnp.bfloat16), returned, preferred_element_type=jnp.float32)
-    picked = picked * flat_weights[:, None]
-    combined = jnp.sum(picked.reshape(tok_dev, top_count, width), axis=1)
+    picks_by_choice = picks.reshape(tok_dev, top_count, slots).transpose(1, 0, 2)
+    picked = jnp.dot(
+        picks_by_choice.reshape(n_flat, slots).astype(jnp.bfloat16),
+        returned,
+        preferred_element_type=jnp.float32,
+    ).reshape(top_count, tok_dev, width)
+    weights_by_choice = route_weights.T.reshape(top_count, tok_dev, 1)
+    combined = jnp.sum(picked * weights_by_choice, axis=0)
     return (mixed + combined).astype(jnp.bfloat16)
 
 

time: 484 us -> 451 us (0.932)
  blocking collectives: 141 us -> 244 us
  waiting for transfers between devices: 211 us -> 108 us
  other arithmetic: 18.3 us -> 5.96 us
  local copies, waits for them, and re-layouts: 22.4 us -> 12.5 us
  starting transfers between devices: 5.62 us -> 0.01 us
    all_to_all x1 -> x0, waiting for transfers between devices: 103 us -> none  [shards(): lax.all_to_all(produced.reshape(arrived.shape), ('grp', 'seq'), split_axi...]
    all_to_all x0 -> x1, blocking collectives: none -> 103 us  [shards(): lax.all_to_all(produced.reshape(arrived.shape), ('grp', 'seq'), split_axi...]
    reduce_sum x1 -> x0, other arithmetic: 10.2 us -> none  [shards(): combined = jnp.sum(picked.reshape(tok_dev, top_count, width), axis=1)]
    reshape x2 -> x0, local copies, waits for them, and re-layouts: 9.87 us -> none  [the longest x1 9.76 us: shards(): combined = jnp.sum(picked.reshape(tok_dev, top_count, width), axis=1)]
    all_to_all x1 -> x0, starting transfers between devices: 5.62 us -> none  [shards(): lax.all_to_all(produced.reshape(arrived.shape), ('grp', 'seq'), split_axi...]
    dot_general x1, matrix products: 10.2 us -> 5.11 us  [shards(): jnp.dot(picks_by_choice.reshape(n_flat, slots).astype(jnp.bfloat16), retu...]
  transfers between devices with their start and end apart: 2 -> 1, of which waited for: 2 -> 1; matrix products, arithmetic and copies ran while one was open for 0% -> 0% of each run, Pallas kernels for 0% -> 0%
where the time goes in v2:
time: 451 us; the launch traced here: 450 us
  blocking collectives  244 us (54%)
  waiting for transfers between devices  108 us (24%)
  matrix products  44.3 us (10%)
  Pallas kernels  22.6 us (5%)
  between operations  13.5 us (3%)
  local copies, waits for them, and re-layouts  12.5 us (3%)
  other arithmetic  5.96 us (1%)
    reduce_scatter x1, waiting for transfers between devices, shards(): lax.psum_scatter(jnp.dot(attended, o_weight, preferred_element_type=jnp.f...  108 us
    all_to_all x1, blocking collectives, shards(): lax.all_to_all(outgoing_rows, ('grp', 'seq'), split_axis=0, concat_axis=0...  106 us
    all_to_all x1, blocking collectives, shards(): lax.all_to_all(produced.reshape(arrived.shape), ('grp', 'seq'), split_axi...  103 us
    all_to_all x1, blocking collectives, shards(): lax.all_to_all(send, 'seq', split_axis=0, concat_axis=0, tiled=True)  35 us
    pallas_call x1, Pallas kernels, attention(): pl.pallas_call(kernel, out_shape=jax.ShapeDtypeStruct((seq_len, heads * h...  22.6 us
    dot_general x1, matrix products, shards(): projected = jnp.dot(flat_rows, w_in[0], preferred_element_type=jnp.float32)  17.2 us
    dot_general x1, matrix products, shards(): jnp.dot(hidden, w_down[0], preferred_element_type=jnp.float32)  9.8 us
  transfers between devices with their start and end apart: 1, of which 1 were waited for; matrix products, arithmetic and copies ran while one was open for 0% of the time, Pallas kernels for 0%

profile of v2, /device:TPU:7, one launch (start us, length us, event | category | flops | bytes accessed | tf_op | source)
XLA Modules:
  0.0 450.2 jit_solution(7494427737260187108)
XLA Ops:
  6.5 0.0 copy-start
  6.5 0.0 reduce-scatter.2.cloned.1.call-start
  6.6 1.2 copy.38
  7.7 0.1 copy.39
  7.9 0.7 gather_fusion
  8.7 1.1 select_bitcast_fusion
  9.8 1.6 copy.40
  11.4 2.3 copy.37
  13.7 1.4 pad_maximum_fusion
  15.1 35.0 %all_to_all.15 = bf16[16,128,512]{1,2,0:T(8,128)(2,1)} all-to-all(bf16[16,128,512]{1,2,0:T(8,128)(2,1)S(1)} %pad_maximum_fusion), channel_id=1, replica_groups=mesh['grp'=8,'seq'=16] {'seq'}, dimensions={0} | all-to-all | bytes 4194304 | tf_op jit(solution)/shard_map/all_to_all | solution.py:76
  50.0 3.9 copy.41
  53.9 0.0 copy-start.2
  53.9 1.6 copy-done.2
  55.5 22.6 %shard_map.91 = bf16[2048,256]{1,0:T(8,128)(2,1)S(1)} custom-call(bf16[2048,512]{1,0:T(8,128)(2,1)S(1)} %bitcast.35, bf16[2048,512]{1,0:T(8,128)(2,1)S(1)} %bitcast.36, bf16[2048,512]{1,0:T(8,128)(2,1)S(1)} %bitcast.37), custom_call_target="tpu_custom_call" | custom-call | tf_op jit(solution)/shard_map/pallas_call | solution.py:38
  78.1 0.0 copy-done
  78.1 8.2 %convolution_convert_fusion = bf16[2048,4096]{1,0:T(8,128)(2,1)} fusion(bf16[2048,256]{1,0:T(8,128)(2,1)S(1)} %shard_map.91, bf16[256,4096]{1,0:T(8,128)(2,1)S(1)} %copy-done), kind=kOutput, calls=%fused_computation.1 | convolution fusion | flops 4303355904 | bytes 19922944 | tf_op jit(solution)/shard_map/dot_general | solution.py:82
  86.3 0.0 copy-start.6
  86.3 0.0 copy-start.5
  86.3 0.0 copy-start.3
  86.3 0.0 reduce-scatter.2.cloned.1.call-update
  86.3 0.7 copy-done.6
  87.0 0.1 copy.42
  87.1 0.1 eq.38
  87.2 0.3 fusion.12
  87.5 0.1 convert_element_type.52
  87.6 0.1 copy.43
  87.7 0.0 copy-done.5
  87.7 0.4 fusion.9
  88.1 107.8 %reduce-scatter.2.cloned.1.call-done = bf16[128,4096]{1,0:T(8,128)(2,1)} async-done(((bf16[2048,4096]{1,0:T(8,128)(2,1)}), bf16[128,4096]{1,0:T(8,128)(2,1)}) %reduce-scatter.2.cloned.1.call-update) | async-done | bytes 1048592 | tf_op jit(solution)/shard_map/reduce_scatter | solution.py:81
  195.9 0.0 copy-done.3
  195.9 1.6 multiply_reduce_fusion.1
  197.5 3.7 convert_bitcast_fusion.1
  201.2 0.0 slice-start
  201.2 105.7 %all_to_all.16 = bf16[128,8,4096]{2,1,0:T(8,128)(2,1)S(1)} all-to-all(bf16[128,8,4096]{2,1,0:T(8,128)(2,1)S(1)} %convert_bitcast_fusion.1), channel_id=1, replica_groups=mesh['grp'=8,'seq'=16] {'grp','seq'}, dimensions={0} | all-to-all | bytes 16777216 | tf_op jit(solution)/shard_map/all_to_all | solution.py:115
  306.9 0.0 slice-start.1
  306.9 17.2 %fusion = f32[1024,1536]{1,0:T(8,128)} fusion(bf16[1,4096,1536]{2,1,0:T(8,128)(2,1)} %param.14, bf16[128,8,4096]{2,1,0:T(8,128)(2,1)S(1)} %all_to_all.16), kind=kOutput, calls=%fused_computation.2 | convolution fusion | flops 12884901888 | bytes 27262976 | tf_op jit(solution)/shard_map/dot_general | solution.py:117
  324.1 0.0 slice-done
  324.1 0.0 slice-done.1
  324.2 9.8 %convert_bitcast_fusion = bf16[128,8,4096]{2,1,0:T(8,128)(2,1)S(1)} fusion(bf16[1,768,4096]{2,1,0:T(8,128)(2,1)S(1)} %bitcast.43, f32[1024,1536]{1,0:T(8,128)} %fusion), kind=kOutput, calls=%fused_computation.8 | convolution fusion | flops 6451363840 | bytes 20971520 | tf_op jit(solution)/shard_map/dot_general | solution.py:119
  334.0 0.0 copy-start.7
  334.0 102.9 %all_to_all.17 = bf16[128,8,4096]{2,1,0:T(8,128)(2,1)S(1)} all-to-all(bf16[128,8,4096]{2,1,0:T(8,128)(2,1)S(1)} %convert_bitcast_fusion), channel_id=1, replica_groups=mesh['grp'=8,'seq'=16] {'grp','seq'}, dimensions={0} | all-to-all | bytes 16777216 | tf_op jit(solution)/shard_map/all_to_all | solution.py:120
  436.9 0.0 copy-done.7
  436.9 0.0 copy-start.4
  436.9 0.0 copy-start.1
  436.9 5.1 %multiply_reduce_fusion = f32[128,4096]{1,0:T(8,128)S(1)} fusion(bf16[128,8,4096]{2,1,0:T(8,128)(2,1)S(1)} %all_to_all.17, f32[4,128]{1,0:T(4,128)S(1)} %bitcast.44, s32[4,128]{1,0:T(4,128)S(1)} %bitcast.41), kind=kOutput, calls=%fused_computation.7 | convolution fusion | flops 4299161600 | bytes 10489856 | tf_op jit(solution)/shard_map/dot_general | solution.py:125
  442.0 0.0 copy-done.4
  442.0 1.4 add_convert_fusion
  443.4 0.0 copy-done.1
  (8 shorter events, 0.1 us)
Async XLA Ops:
  6.5 71.6 %copy-start = (bf16[256,4096]{1,0:T(8,128)(2,1)S(1)}, bf16[256,4096]{1,0:T(8,128)(2,1)}, u32[]{:S(2)}) copy-start(bf16[256,4096]{1,0:T(8,128)(2,1)} %param.13) | copy-start | bytes 6291460
  6.5 189.4 %reduce-scatter.2.cloned.1.call-start = ((), (), s32[]{:S(2)}) async-start(), calls=%async_computation.4 | async-start | bytes 17825792 | tf_op jit(solution)/shard_map/reduce_scatter | solution.py:81
  53.9 1.6 copy-start.2
  86.3 0.7 copy-start.6
  86.3 1.4 copy-start.5
  86.3 109.6 %copy-start.3 = (bf16[128,4096]{1,0:T(8,128)(2,1)S(1)}, bf16[128,4096]{1,0:T(8,128)(2,1)}, u32[]{:S(2)}) copy-start(bf16[128,4096]{1,0:T(8,128)(2,1)} %param.11) | copy-start | bytes 3145732
  201.2 122.9 %slice-start = ((s8[6291456]{0:T(1024)(128)(4,1)}), s8[4194304]{0:T(1024)(128)(4,1)S(1)}, s32[]{:S(2)}) async-start(s8[6291456]{0:T(1024)(128)(4,1)} %bitcast.42), calls=%async_computation.5 | async-start | bytes 8388608
  306.9 17.2 %slice-start.1 = ((s8[6291456]{0:T(1024)(128)(4,1)}), s8[2097152]{0:T(1024)(128)(4,1)S(1)}, s32[]{:S(2)}) async-start(s8[6291456]{0:T(1024)(128)(4,1)} %bitcast.42), calls=%async_computation.6 | async-start | bytes 4194304
  334.0 102.9 %copy-start.7 = (f32[128,4]{0,1:T(4,128)S(1)}, f32[128,4]{0,1:T(4,128)}, u32[]{:S(2)}) copy-start(f32[128,4]{0,1:T(4,128)} %param.17) | copy-start | bytes 6148
  436.9 5.1 %copy-start.4 = (bf16[128,4096]{1,0:T(8,128)(2,1)S(1)}, bf16[128,4096]{1,0:T(8,128)(2,1)}, u32[]{:S(2)}) copy-start(bf16[128,4096]{1,0:T(8,128)(2,1)} %reduce-scatter.2.cloned.1.call-done) | copy-start | bytes 3145732
  436.9 6.5 %copy-start.1 = (bf16[256,4096]{1,0:T(8,128)(2,1)S(1)}, bf16[256,4096]{1,0:T(8,128)(2,1)}, u32[]{:S(2)}) copy-start(bf16[256,4096]{1,0:T(8,128)(2,1)} %param.13) | copy-start | bytes 6291460
Sparse Core Ops, SparseCore 0:
  86.4 109.3 reduce-scatter.1

commit v3 on v2

v3 whole, which is shorter than its diff:
```python
import functools
import math

import jax
import jax.numpy as jnp
from jax import lax
from jax.experimental import pallas as pl
from jax.experimental.pallas import tpu as pltpu
from jax.sharding import Mesh, PartitionSpec as P

HD = 128
Q_BLOCK = 256


def _attend_kernel(meta_ref, q_ref, k_ref, v_ref, o_ref, *, block, scale, tok_dev, n_sb):
    qi = pl.program_id(1)
    sb = meta_ref[0]
    q = q_ref[...]
    k = k_ref[...]
    length = k.shape[0]
    scores = lax.dot_general(
        q, k, (((1,), (1,)), ((), ())), preferred_element_type=jnp.float32
    ) * scale
    local = qi * block + lax.broadcasted_iota(jnp.int32, (block, length), 0)
    q_pos = ((local // tok_dev) * n_sb + sb) * tok_dev + local % tok_dev
    k_pos = lax.broadcasted_iota(jnp.int32, (block, length), 1)
    scores = jnp.where(k_pos <= q_pos, scores, jnp.float32(-1e30))
    top = jnp.max(scores, axis=1, keepdims=True)
    weights = jnp.exp(scores - top)
    total = jnp.sum(weights, axis=1, keepdims=True)
    probs = (weights / total).astype(jnp.bfloat16)
    o_ref[...] = jnp.dot(probs, v_ref[...], preferred_element_type=jnp.float32).astype(
        o_ref.dtype
    )


def attention(meta, q_rows, kv_all, heads, head_size, tok_dev, n_sb):
    rows = q_rows.shape[0]
    seq_len = kv_all.shape[1]
    block = min(Q_BLOCK, rows)
    kernel = functools.partial(
        _attend_kernel, block=block, scale=1.0 / head_size**0.5, tok_dev=tok_dev, n_sb=n_sb
    )
    return pl.pallas_call(
        kernel,
        out_shape=jax.ShapeDtypeStruct((rows, heads * head_size), jnp.bfloat16),
        grid_spec=pltpu.PrefetchScalarGridSpec(
            num_scalar_prefetch=1,
            grid=(heads, rows // block),
            in_specs=[
                pl.BlockSpec((block, head_size), lambda h, i, m: (i, h)),
                pl.BlockSpec((None, seq_len, head_size), lambda h, i, m: (0, 0, m[1])),
                pl.BlockSpec((None, seq_len, head_size), lambda h, i, m: (1, 0, m[1])),
            ],
            out_specs=pl.BlockSpec((block, head_size), lambda h, i, m: (i, h)),
        ),
        compiler_params=pltpu.CompilerParams(
            dimension_semantics=("arbitrary", "arbitrary"),
            vmem_limit_bytes=48 * 1024 * 1024,
        ),
    )(meta, q_rows, kv_all, kv_all)


def shards(
    queries, kv_pairs, residual, norm_gain, o_weight, w_in, w_down, expert_ids, route_weights
):
    tok_dev = queries.shape[0]
    width = residual.shape[1]
    n_sa = lax.axis_size("sa")
    n_sb = lax.axis_size("sb")
    n_seq = n_sa * n_sb
    n_grp = lax.axis_size("grp")
    devices = n_seq * n_grp
    head_size = HD
    heads_all = queries.shape[1] // head_size
    key_heads = kv_pairs.shape[2] // head_size
    sharing = heads_all // key_heads
    heads_here = heads_all // n_sa
    block_rows = o_weight.shape[0]
    assert sharing % heads_here == 0
    sa = lax.axis_index("sa")
    sb = lax.axis_index("sb")

    w_rows = lax.all_gather(o_weight, "sb", axis=0, tiled=True)
    kv_all = lax.all_gather(kv_pairs, ("sa", "sb"), axis=1, tiled=True)
    q_send = queries.reshape(tok_dev, n_sa, heads_here * head_size).transpose(1, 0, 2)
    q_rows = lax.all_to_all(q_send, "sa", split_axis=0, concat_axis=0, tiled=True)
    q_rows = q_rows.reshape(n_sa * tok_dev, heads_here * head_size)
    meta = jnp.stack([sb, (sa * heads_here) // sharing]).astype(jnp.int32)
    attended = attention(meta, q_rows, kv_all, heads_here, head_size, tok_dev, n_sb)

    partial_sum = None
    for j in range(w_rows.shape[0] // block_rows):
        cols = slice(j * block_rows, (j + 1) * block_rows)
        partial_j = jnp.dot(
            attended[:, cols], w_rows[cols], preferred_element_type=jnp.float32
        ).astype(jnp.bfloat16).astype(jnp.float32)
        partial_sum = partial_j if partial_sum is None else partial_sum + partial_j
    attn_out = lax.psum_scatter(
        partial_sum.astype(jnp.bfloat16), "sa", scatter_dimension=0, tiled=True
    ).astype(jnp.float32)
    mixed = residual.astype(jnp.float32) + attn_out
    mean_square = jnp.mean(mixed * mixed, axis=1, keepdims=True)
    normed = (mixed * lax.rsqrt(mean_square + 1e-06) * norm_gain.astype(jnp.float32)).astype(
        jnp.bfloat16
    )

    top_count = expert_ids.shape[1]
    capacity = 2 * tok_dev * top_count // devices
    slots = devices * capacity
    flat_ids = expert_ids.reshape(-1)
    flat_weights = route_weights.reshape(-1)
    n_flat = flat_ids.shape[0]
    onehot = (flat_ids[:, None] == jnp.arange(devices, dtype=jnp.int32)[None, :]).astype(
        jnp.bfloat16
    )
    row = lax.broadcasted_iota(jnp.int32, (n_flat, n_flat), 0)
    col = lax.broadcasted_iota(jnp.int32, (n_flat, n_flat), 1)
    before = (col < row).astype(jnp.bfloat16)
    earlier = jnp.dot(before, onehot, preferred_element_type=jnp.float32)
    rank = jnp.sum(earlier * onehot.astype(jnp.float32), axis=1).astype(jnp.int32)
    slot_index = flat_ids * capacity + rank
    picks = slot_index[:, None] == jnp.arange(slots, dtype=jnp.int32)[None, :]
    token_slots = jnp.any(picks.reshape(tok_dev, top_count, slots), axis=1).astype(jnp.bfloat16)
    outgoing_rows = lax.dot_general(
        token_slots, normed, (((0,), (0,)), ((), ())), preferred_element_type=jnp.float32
    ).astype(jnp.bfloat16)
    outgoing_rows = outgoing_rows.reshape(devices, capacity, width)
    ffe_width = w_down.shape[1]
    arrived = lax.all_to_all(outgoing_rows, ("grp", "sa", "sb"), split_axis=0, concat_axis=0, tiled=True)
    flat_rows = arrived.reshape(-1, width)
    projected = jnp.dot(flat_rows, w_in[0], preferred_element_type=jnp.float32)
    hidden = (jax.nn.silu(projected[:, :ffe_width]) * projected[:, ffe_width:]).astype(jnp.bfloat16)
    produced = jnp.dot(hidden, w_down[0], preferred_element_type=jnp.float32).astype(jnp.bfloat16)
    returned = lax.all_to_all(
        produced.reshape(arrived.shape), ("grp", "sa", "sb"), split_axis=0, concat_axis=0, tiled=True
    )
    returned = returned.reshape(slots, width)
    picks_by_choice = picks.reshape(tok_dev, top_count, slots).transpose(1, 0, 2)
    picked = jnp.dot(
        picks_by_choice.reshape(n_flat, slots).astype(jnp.bfloat16),
        returned,
        preferred_element_type=jnp.float32,
    ).reshape(top_count, tok_dev, width)
    weights_by_choice = route_weights.T.reshape(top_count, tok_dev, 1)
    combined = jnp.sum(picked * weights_by_choice, axis=0)
    return (mixed + combined).astype(jnp.bfloat16)


def solution(mesh):
    n_grp, n_seq = mesh.shape["grp"], mesh.shape["seq"]
    n_sb = math.isqrt(n_seq)
    grid = Mesh(mesh.devices.reshape(n_grp, n_seq // n_sb, n_sb), ("grp", "sa", "sb"))
    tokens = ("grp", "sa", "sb")
    return jax.shard_map(
        shards,
        mesh=grid,
        in_specs=(
            P(tokens, None),
            P(None, tokens, None),
            P(tokens, None),
            P(),
            P(("sa", "sb"), None),
            P(tokens, None, None),
            P(tokens, None, None),
            P(tokens, None),
            P(tokens, None),
        ),
        out_specs=P(tokens, None),
        check_vma=False,
    )
```

time: 451 us -> 458 us (1.016)
  waiting for transfers between devices: 108 us -> 152 us
  blocking collectives: 244 us -> 209 us
  local copies, waits for them, and re-layouts: 12.5 us -> 4.94 us
  starting transfers between devices: 0.01 us -> 5.07 us
    all_gather x0 -> x2, waiting for transfers between devices: none -> 88.8 us  [the longest x1 60.6 us: shards(): w_rows = lax.all_gather(o_weight, 'sb', axis=0, tiled=True)]
    reduce_scatter x1, waiting for transfers between devices: 108 us -> 46.5 us  [shards(): lax.psum_scatter(partial_sum.astype(jnp.bfloat16), 'sa', scatter_dimensio...]
    all_to_all x3 -> x2, blocking collectives: 244 us -> 209 us  [the longest x1 106 us: shards(): lax.all_to_all(outgoing_rows, ('grp', 'sa', 'sb'), split_axis=0, concat_a...]
    all_to_all x0 -> x1, waiting for transfers between devices: none -> 14.9 us  [shards(): lax.all_to_all(q_send, 'sa', split_axis=0, concat_axis=0, tiled=True)]
    all_to_all x0 -> x1, starting transfers between devices: none -> 5.03 us  [shards(): lax.all_to_all(q_send, 'sa', split_axis=0, concat_axis=0, tiled=True)]
    dot_general x1 -> x4, matrix products: 8.18 us -> 10.8 us  [shards(): jnp.dot(attended[:, cols], w_rows[cols], preferred_element_type=jnp.float32)]
  transfers between devices with their start and end apart: 1 -> 4, of which waited for: 1 -> 4; matrix products, arithmetic and copies ran while one was open for 0% -> 1% of each run, Pallas kernels for 0% -> 5%
where the time goes in v3:
time: 458 us; the launch traced here: 457 us
  blocking collectives  209 us (46%)
  waiting for transfers between devices  152 us (33%)
  matrix products  47 us (10%)
  Pallas kernels  23.1 us (5%)
  between operations  13.2 us (3%)
  starting transfers between devices  5.07 us (1%)
  local copies, waits for them, and re-layouts  4.94 us (1%)
    all_to_all x1, blocking collectives, shards(): lax.all_to_all(outgoing_rows, ('grp', 'sa', 'sb'), split_axis=0, concat_a...  106 us
    all_to_all x1, blocking collectives, shards(): lax.all_to_all(produced.reshape(arrived.shape), ('grp', 'sa', 'sb'), spli...  103 us
    all_gather x1, waiting for transfers between devices, shards(): w_rows = lax.all_gather(o_weight, 'sb', axis=0, tiled=True)  60.6 us
    reduce_scatter x1, waiting for transfers between devices, shards(): lax.psum_scatter(partial_sum.astype(jnp.bfloat16), 'sa', scatter_dimensio...  46.5 us
    all_gather x1, waiting for transfers between devices, shards(): kv_all = lax.all_gather(kv_pairs, ('sa', 'sb'), axis=1, tiled=True)  28.2 us
    pallas_call x1, Pallas kernels, attention(): pl.pallas_call(kernel, out_shape=jax.ShapeDtypeStruct((rows, heads * head...  23.1 us
    dot_general x1, matrix products, shards(): projected = jnp.dot(flat_rows, w_in[0], preferred_element_type=jnp.float32)  17.3 us
    all_to_all x1, waiting for transfers between devices, shards(): lax.all_to_all(q_send, 'sa', split_axis=0, concat_axis=0, tiled=True)  14.9 us
  transfers between devices with their start and end apart: 4, of which 4 were waited for; matrix products, arithmetic and copies ran while one was open for 1% of the time, Pallas kernels for 5%

profile of v3, /device:TPU:7, one launch (start us, length us, event | category | flops | bytes accessed | tf_op | source)
XLA Modules:
  0.0 457.3 jit_solution(15170454272537143234)
XLA Ops:
  6.5 0.0 all-gather.3.cloned.1.call-start
  6.5 0.7 all-gather.3.cloned.1.call-update
  7.3 0.0 all-gather.5.cloned.1.call-start
  7.3 0.7 all-gather.5.cloned.1.call-update
  8.0 2.3 copy.28
  10.3 5.0 %all-to-all-start = ((bf16[4,128,1024]{2,1,0:T(8,128)(2,1)}), bf16[4,128,1024]{2,1,0:T(8,128)(2,1)S(1)}, u32[]{:S(2)}, u32[]{:S(2)}) async-start(bf16[4,128,1024]{2,1,0:T(8,128)(2,1)} %bitcast.32), calls=%async_computation | async-start | bytes 2097152 | tf_op jit(solution)/shard_map/all_to_all | solution.py:87
  15.3 0.0 reduce-scatter.2.cloned.1.call-start
  15.3 0.1 pad_add_fusion.meta_ref
  15.4 14.9 %all-to-all-done = bf16[4,128,1024]{2,1,0:T(8,128)(2,1)S(1)} async-done(((bf16[4,128,1024]{2,1,0:T(8,128)(2,1)}), bf16[4,128,1024]{2,1,0:T(8,128)(2,1)S(1)}, u32[]{:S(2)}, u32[]{:S(2)}) %all-to-all-start) | async-done | bytes 1048608 | tf_op jit(solution)/shard_map/all_to_all | solution.py:87
  30.3 28.2 %all-gather.3.cloned.1.call-done.k_ref.v_ref = bf16[2,2048,256]{2,1,0:T(8,128)(2,1)} async-done(((bf16[2,128,256]{2,1,0:T(8,128)(2,1)}), bf16[2,2048,256]{2,1,0:T(8,128)(2,1)}) %all-gather.3.cloned.1.call-update) | async-done | bytes 2097168 | tf_op jit(solution)/shard_map/all_gather | solution.py:85
  58.5 0.0 copy-start
  58.5 1.6 copy-done
  60.1 23.1 %shard_map.91 = bf16[512,1024]{1,0:T(8,128)(2,1)S(1)} custom-call(s32[2]{0:T(128)S(1)} %pad_add_fusion.meta_ref, bf16[512,1024]{1,0:T(8,128)(2,1)S(1)} %bitcast.33, bf16[2,2048,256]{2,1,0:T(8,128)(2,1)S(1)} %copy-done, bf16[2,2048,256]{2,1,0:T(8,128)(2,1)S(1)} %copy-done), custom_call_target="tpu_custom_call" | custom-call | tf_op jit(solution)/shard_map/pallas_call | solution.py:44
  83.2 60.6 %all-gather.5.cloned.1.call-done = bf16[1024,4096]{1,0:T(8,128)(2,1)} async-done(((bf16[256,4096]{1,0:T(8,128)(2,1)}), bf16[1024,4096]{1,0:T(8,128)(2,1)}) %all-gather.5.cloned.1.call-update) | async-done | bytes 8388624 | tf_op jit(solution)/shard_map/all_gather | solution.py:84
  143.9 0.0 copy-start.3
  143.9 3.0 convolution_convert_fusion
  146.9 2.9 convolution_convert_fusion.1
  149.8 0.0 copy-done.3
  149.8 1.3 convolution_convert_fusion.2
  151.0 3.7 add_convert_fusion
  154.7 0.0 copy-start.5
  154.7 0.0 copy-start.1
  154.7 0.0 reduce-scatter.2.cloned.1.call-update
  154.8 0.7 copy-done.5
  155.4 0.1 copy.24
  155.5 0.1 eq.38
  155.6 0.3 fusion.16
  156.0 0.1 convert_element_type.84
  156.1 0.1 copy.25
  156.1 0.0 copy-done.4
  156.2 0.4 fusion.13
  156.6 46.5 %reduce-scatter.2.cloned.1.call-done = bf16[128,4096]{1,0:T(8,128)(2,1)} async-done(((bf16[512,4096]{1,0:T(8,128)(2,1)}), bf16[128,4096]{1,0:T(8,128)(2,1)}) %reduce-scatter.2.cloned.1.call-update) | async-done | bytes 1048592 | tf_op jit(solution)/shard_map/reduce_scatter | solution.py:99
  203.0 0.0 copy-done.1
  203.0 1.6 multiply_reduce_fusion.1
  204.7 3.7 convert_bitcast_fusion.1
  208.4 0.0 slice-start
  208.4 105.9 %all_to_all.15 = bf16[128,8,4096]{2,1,0:T(8,128)(2,1)S(1)} all-to-all(bf16[128,8,4096]{2,1,0:T(8,128)(2,1)S(1)} %convert_bitcast_fusion.1), channel_id=1, replica_groups=mesh['grp'=8,'sa'=4,'sb'=4] {'grp','sa','sb'}, dimensions={0} | all-to-all | bytes 16777216 | tf_op jit(solution)/shard_map/all_to_all | solution.py:130
  314.2 0.0 slice-start.1
  314.2 17.3 %fusion = f32[1024,1536]{1,0:T(8,128)} fusion(bf16[1,4096,1536]{2,1,0:T(8,128)(2,1)} %param.14, bf16[128,8,4096]{2,1,0:T(8,128)(2,1)S(1)} %all_to_all.15), kind=kOutput, calls=%fused_computation | convolution fusion | flops 12884901888 | bytes 27262976 | tf_op jit(solution)/shard_map/dot_general | solution.py:132
  331.5 0.0 slice-done
  331.5 0.0 slice-done.1
  331.5 9.8 %convert_bitcast_fusion = bf16[128,8,4096]{2,1,0:T(8,128)(2,1)S(1)} fusion(bf16[1,768,4096]{2,1,0:T(8,128)(2,1)S(1)} %bitcast.37, f32[1024,1536]{1,0:T(8,128)} %fusion), kind=kOutput, calls=%fused_computation.6 | convolution fusion | flops 6451363840 | bytes 20971520 | tf_op jit(solution)/shard_map/dot_general | solution.py:134
  341.3 0.0 copy-start.6
  341.4 102.9 %all_to_all.16 = bf16[128,8,4096]{2,1,0:T(8,128)(2,1)S(1)} all-to-all(bf16[128,8,4096]{2,1,0:T(8,128)(2,1)S(1)} %convert_bitcast_fusion), channel_id=1, replica_groups=mesh['grp'=8,'sa'=4,'sb'=4] {'grp','sa','sb'}, dimensions={0} | all-to-all | bytes 16777216 | tf_op jit(solution)/shard_map/all_to_all | solution.py:135
  444.3 0.0 copy-done.6
  444.3 5.1 %multiply_reduce_fusion = f32[128,4096]{1,0:T(8,128)S(1)} fusion(bf16[128,8,4096]{2,1,0:T(8,128)(2,1)S(1)} %all_to_all.16, f32[4,128]{1,0:T(4,128)S(1)} %bitcast.38, s32[4,128]{1,0:T(4,128)S(1)} %bitcast.35), kind=kOutput, calls=%fused_computation.5 | convolution fusion | flops 4299161600 | bytes 10489856 | tf_op jit(solution)/shard_map/dot_general | solution.py:140
  449.4 0.0 copy-done.2
  449.4 1.4 add_convert_fusion.1
  (7 shorter events, 0.0 us)
Async XLA Ops:
  6.5 52.0 %all-gather.3.cloned.1.call-start = ((), (), s32[]{:S(2)}) async-start(), calls=%async_computation.4 | async-start | bytes 2228224 | tf_op jit(solution)/shard_map/all_gather | solution.py:85
  7.3 136.6 %all-gather.5.cloned.1.call-start = ((), (), s32[]{:S(2)}) async-start(), calls=%async_computation.5 | async-start | bytes 10485760 | tf_op jit(solution)/shard_map/all_gather | solution.py:84
  10.3 20.0 %all-to-all-start = ((bf16[4,128,1024]{2,1,0:T(8,128)(2,1)}), bf16[4,128,1024]{2,1,0:T(8,128)(2,1)S(1)}, u32[]{:S(2)}, u32[]{:S(2)}) async-start(bf16[4,128,1024]{2,1,0:T(8,128)(2,1)} %bitcast.32), calls=%async_computation | async-start | bytes 2097152 | tf_op jit(solution)/shard_map/all_to_all | solution.py:87
  15.3 187.7 %reduce-scatter.2.cloned.1.call-start = ((), (), s32[]{:S(2)}) async-start(), calls=%async_computation.6 | async-start | bytes 5242880 | tf_op jit(solution)/shard_map/reduce_scatter | solution.py:99
  58.5 1.6 copy-start
  143.9 5.9 %copy-start.3 = (bf16[1024,4096]{1,0:T(8,128)(2,1)S(1)}, bf16[1024,4096]{1,0:T(8,128)(2,1)}, u32[]{:S(2)}) copy-start(bf16[1024,4096]{1,0:T(8,128)(2,1)} %all-gather.5.cloned.1.call-done) | copy-start | bytes 25165828
  154.7 0.7 copy-start.5
  154.7 1.4 copy-start.4
  154.7 48.3 %copy-start.1 = (bf16[128,4096]{1,0:T(8,128)(2,1)S(1)}, bf16[128,4096]{1,0:T(8,128)(2,1)}, u32[]{:S(2)}) copy-start(bf16[128,4096]{1,0:T(8,128)(2,1)} %param.11) | copy-start | bytes 3145732
  208.4 123.2 %slice-start = ((s8[6291456]{0:T(1024)(128)(4,1)}), s8[4194304]{0:T(1024)(128)(4,1)S(1)}, s32[]{:S(2)}) async-start(s8[6291456]{0:T(1024)(128)(4,1)} %bitcast.36), calls=%async_computation.7 | async-start | bytes 8388608
  314.2 17.3 %slice-start.1 = ((s8[6291456]{0:T(1024)(128)(4,1)}), s8[2097152]{0:T(1024)(128)(4,1)S(1)}, s32[]{:S(2)}) async-start(s8[6291456]{0:T(1024)(128)(4,1)} %bitcast.36), calls=%async_computation.8 | async-start | bytes 4194304
  341.3 102.9 %copy-start.6 = (f32[128,4]{0,1:T(4,128)S(1)}, f32[128,4]{0,1:T(4,128)}, u32[]{:S(2)}) copy-start(f32[128,4]{0,1:T(4,128)} %param.17) | copy-start | bytes 6148
  444.3 5.1 %copy-start.2 = (bf16[128,4096]{1,0:T(8,128)(2,1)S(1)}, bf16[128,4096]{1,0:T(8,128)(2,1)}, u32[]{:S(2)}) copy-start(bf16[128,4096]{1,0:T(8,128)(2,1)} %reduce-scatter.2.cloned.1.call-done) | copy-start | bytes 3145732
Sparse Core Ops, SparseCore 0:
  9.5 48.9 all-gather.2
  60.2 83.6 all-gather.4
  154.9 48.0 reduce-scatter.1

commit v4 on v3

--- a/solution.py
+++ b/solution.py
@@ -81,7 +81,15 @@
     sa = lax.axis_index("sa")
     sb = lax.axis_index("sb")
 
-    w_rows = lax.all_gather(o_weight, "sb", axis=0, tiled=True)
+    pair = lax.axis_index("grp") % 2
+    half = o_weight.shape[1] // 2
+    w_mine = lax.all_gather(
+        lax.dynamic_slice_in_dim(o_weight, pair * half, half, axis=1), "sb", axis=0, tiled=True
+    )
+    w_other = lax.ppermute(w_mine, "grp", [(g, g ^ 1) for g in range(n_grp)])
+    w_rows = jnp.zeros((w_mine.shape[0], 2 * half), o_weight.dtype)
+    w_rows = lax.dynamic_update_slice_in_dim(w_rows, w_mine, pair * half, axis=1)
+    w_rows = lax.dynamic_update_slice_in_dim(w_rows, w_other, (1 - pair) * half, axis=1)
     kv_all = lax.all_gather(kv_pairs, ("sa", "sb"), axis=1, tiled=True)
     q_send = queries.reshape(tok_dev, n_sa, heads_here * head_size).transpose(1, 0, 2)
     q_rows = lax.all_to_all(q_send, "sa", split_axis=0, concat_axis=0, tiled=True)

time: 458 us -> 449 us (0.980)
  waiting for transfers between devices: 152 us -> 138 us
  local copies, waits for them, and re-layouts: 4.94 us -> 13.2 us
    all_gather x1, waiting for transfers between devices: 60.6 us -> 49.8 us  [shards(): lax.all_gather(lax.dynamic_slice_in_dim(o_weight, pair * half, half, axis...]
  transfers between devices with their start and end apart: 4 -> 5, of which waited for: 4 -> 4; matrix products, arithmetic and copies ran while one was open for 1% -> 1% of each run, Pallas kernels for 5% -> 5%
where the time goes in v4:
time: 449 us
  blocking collectives  209 us (47%)
  waiting for transfers between devices  138 us (31%)
  matrix products  43.7 us (10%)
  Pallas kernels  23.1 us (5%)
  between operations  13.3 us (3%)
  local copies, waits for them, and re-layouts  13.2 us (3%)
  starting transfers between devices  5.02 us (1%)
    all_to_all x1, blocking collectives, shards(): lax.all_to_all(outgoing_rows, ('grp', 'sa', 'sb'), split_axis=0, concat_a...  106 us
    all_to_all x1, blocking collectives, shards(): lax.all_to_all(produced.reshape(arrived.shape), ('grp', 'sa', 'sb'), spli...  103 us
    all_gather x1, waiting for transfers between devices, shards(): lax.all_gather(lax.dynamic_slice_in_dim(o_weight, pair * half, half, axis...  49.8 us
    reduce_scatter x1, waiting for transfers between devices, shards(): lax.psum_scatter(partial_sum.astype(jnp.bfloat16), 'sa', scatter_dimensio...  46.1 us
    all_gather x1, waiting for transfers between devices, shards(): kv_all = lax.all_gather(kv_pairs, ('sa', 'sb'), axis=1, tiled=True)  25.8 us
    pallas_call x1, Pallas kernels, attention(): pl.pallas_call(kernel, out_shape=jax.ShapeDtypeStruct((rows, heads * head...  23.1 us
    dot_general x1, matrix products, shards(): projected = jnp.dot(flat_rows, w_in[0], preferred_element_type=jnp.float32)  17.3 us
    all_to_all x1, waiting for transfers between devices, shards(): lax.all_to_all(q_send, 'sa', split_axis=0, concat_axis=0, tiled=True)  16 us
  transfers between devices with their start and end apart: 5, of which 4 were waited for; matrix products, arithmetic and copies ran while one was open for 1% of the time, Pallas kernels for 5%

profile of v4, /device:TPU:7, one launch (start us, length us, event | category | flops | bytes accessed | tf_op | source)
XLA Modules:
  0.0 449.0 jit_solution(4907881395736339488)
XLA Ops:
  6.5 0.0 copy-start
  6.5 0.0 all-gather.5.cloned.1.call-start
  6.5 1.6 copy-done
  8.1 1.1 constant_dynamic-slice_fusion
  9.2 0.0 all-gather.5.cloned.1.call-update
  9.2 0.0 all-gather.3.cloned.1.call-start
  9.3 0.7 all-gather.3.cloned.1.call-update
  10.0 49.8 %all-gather.5.cloned.1.call-done = bf16[1024,2048]{1,0:T(8,128)(2,1)} async-done(((bf16[256,2048]{1,0:T(8,128)(2,1)}), bf16[1024,2048]{1,0:T(8,128)(2,1)}) %all-gather.5.cloned.1.call-update) | async-done | bytes 4194320 | tf_op jit(solution)/shard_map/all_gather | solution.py:86
  59.8 0.8 collective-permute-start
  60.6 2.3 copy.28
  62.9 4.1 all-to-all-start
  67.0 0.0 reduce-scatter.2.cloned.1.call-start
  67.0 0.1 pad_add_fusion.meta_ref
  67.1 16.0 %all-to-all-done = bf16[4,128,1024]{2,1,0:T(8,128)(2,1)S(1)} async-done(((bf16[4,128,1024]{2,1,0:T(8,128)(2,1)}), bf16[4,128,1024]{2,1,0:T(8,128)(2,1)S(1)}, u32[]{:S(2)}, u32[]{:S(2)}) %all-to-all-start) | async-done | bytes 1048608 | tf_op jit(solution)/shard_map/all_to_all | solution.py:95
  83.1 25.8 %all-gather.3.cloned.1.call-done.k_ref.v_ref = bf16[2,2048,256]{2,1,0:T(8,128)(2,1)} async-done(((bf16[2,128,256]{2,1,0:T(8,128)(2,1)}), bf16[2,2048,256]{2,1,0:T(8,128)(2,1)}) %all-gather.3.cloned.1.call-update) | async-done | bytes 2097168 | tf_op jit(solution)/shard_map/all_gather | solution.py:93
  108.9 1.6 copy-done.2
  110.5 23.1 %shard_map.91 = bf16[512,1024]{1,0:T(8,128)(2,1)S(1)} custom-call(s32[2]{0:T(128)S(1)} %pad_add_fusion.meta_ref, bf16[512,1024]{1,0:T(8,128)(2,1)S(1)} %bitcast.33, bf16[2,2048,256]{2,1,0:T(8,128)(2,1)S(1)} %copy-done.2, bf16[2,2048,256]{2,1,0:T(8,128)(2,1)S(1)} %copy-done.2), custom_call_target="tpu_custom_call" | custom-call | tf_op jit(solution)/shard_map/pallas_call | solution.py:44
  133.6 0.0 copy-start.5
  133.6 1.0 broadcast_in_dim.2
  134.7 1.1 copy-done.5
  135.8 0.6 constant_dynamic-update-slice_fusion.1
  136.5 0.0 collective-permute-done
  136.5 2.8 constant_dynamic-update-slice_fusion
  139.3 1.3 convolution_convert_fusion.2
  140.5 1.3 convolution_convert_fusion.3
  141.8 1.3 convolution_convert_fusion.1
  143.1 3.8 add_convert_fusion
  146.9 0.0 reduce-scatter.2.cloned.1.call-update
  146.9 0.7 copy-done.7
  147.5 0.1 copy.24
  147.7 0.1 eq.40
  147.8 0.3 fusion.16
  148.1 0.1 convert_element_type.84
  148.2 0.1 copy.25
  148.3 0.0 copy-done.6
  148.3 0.4 fusion.13
  148.7 46.1 %reduce-scatter.2.cloned.1.call-done = bf16[128,4096]{1,0:T(8,128)(2,1)} async-done(((bf16[512,4096]{1,0:T(8,128)(2,1)}), bf16[128,4096]{1,0:T(8,128)(2,1)}) %reduce-scatter.2.cloned.1.call-update) | async-done | bytes 1048592 | tf_op jit(solution)/shard_map/reduce_scatter | solution.py:107
  194.8 1.6 multiply_reduce_fusion.1
  196.5 3.7 convert_bitcast_fusion.1
  200.1 0.0 slice-start
  200.1 105.9 %all_to_all.15 = bf16[128,8,4096]{2,1,0:T(8,128)(2,1)S(1)} all-to-all(bf16[128,8,4096]{2,1,0:T(8,128)(2,1)S(1)} %convert_bitcast_fusion.1), channel_id=1, replica_groups=mesh['grp'=8,'sa'=4,'sb'=4] {'grp','sa','sb'}, dimensions={0} | all-to-all | bytes 16777216 | tf_op jit(solution)/shard_map/all_to_all | solution.py:138
  306.0 17.3 %fusion = f32[1024,1536]{1,0:T(8,128)} fusion(bf16[1,4096,1536]{2,1,0:T(8,128)(2,1)} %param.14, bf16[128,8,4096]{2,1,0:T(8,128)(2,1)S(1)} %all_to_all.15), kind=kOutput, calls=%fused_computation | convolution fusion | flops 12884901888 | bytes 27262976 | tf_op jit(solution)/shard_map/dot_general | solution.py:140
  323.3 0.0 slice-done.1
  323.3 9.8 %convert_bitcast_fusion = bf16[128,8,4096]{2,1,0:T(8,128)(2,1)S(1)} fusion(bf16[1,768,4096]{2,1,0:T(8,128)(2,1)S(1)} %bitcast.37, f32[1024,1536]{1,0:T(8,128)} %fusion), kind=kOutput, calls=%fused_computation.6 | convolution fusion | flops 6451363840 | bytes 20971520 | tf_op jit(solution)/shard_map/dot_general | solution.py:142
  333.1 0.0 copy-start.8
  333.1 102.9 %all_to_all.16 = bf16[128,8,4096]{2,1,0:T(8,128)(2,1)S(1)} all-to-all(bf16[128,8,4096]{2,1,0:T(8,128)(2,1)S(1)} %convert_bitcast_fusion), channel_id=1, replica_groups=mesh['grp'=8,'sa'=4,'sb'=4] {'grp','sa','sb'}, dimensions={0} | all-to-all | bytes 16777216 | tf_op jit(solution)/shard_map/all_to_all | solution.py:143
  436.1 5.1 %multiply_reduce_fusion = f32[128,4096]{1,0:T(8,128)S(1)} fusion(bf16[128,8,4096]{2,1,0:T(8,128)(2,1)S(1)} %all_to_all.16, f32[4,128]{1,0:T(4,128)S(1)} %bitcast.38, s32[4,128]{1,0:T(4,128)S(1)} %bitcast.35), kind=kOutput, calls=%fused_computation.5 | convolution fusion | flops 4299161600 | bytes 10489856 | tf_op jit(solution)/shard_map/dot_general | solution.py:148
  441.2 1.3 add_convert_fusion.1
  (17 shorter events, 0.1 us)
Async XLA Ops:
  6.5 1.6 copy-start
  6.5 53.2 %all-gather.5.cloned.1.call-start = ((), (), s32[]{:S(2)}) async-start(), calls=%async_computation.5 | async-start | bytes 5242880 | tf_op jit(solution)/shard_map/all_gather | solution.py:86
  9.2 99.6 %all-gather.3.cloned.1.call-start = ((), (), s32[]{:S(2)}) async-start(), calls=%async_computation.4 | async-start | bytes 2228224 | tf_op jit(solution)/shard_map/all_gather | solution.py:93
  59.8 76.7 %collective-permute-start = (bf16[1024,2048]{1,0:T(8,128)(2,1)}, bf16[1024,2048]{1,0:T(8,128)(2,1)}, u32[]{:S(2)}, u32[]{:S(2)}) collective-permute-start(bf16[1024,2048]{1,0:T(8,128)(2,1)} %all-gather.5.cloned.1.call-done), channel_id=1, source_target_pairs={{0,16},{16,0},{32,48},{48,32},{64,80},{80,64},{96,112},{112,96},{1... | collective-permute-start | bytes 12582920 | tf_op jit(solution)/shard_map/ppermute | solution.py:89
  62.9 20.2 %all-to-all-start = ((bf16[4,128,1024]{2,1,0:T(8,128)(2,1)}), bf16[4,128,1024]{2,1,0:T(8,128)(2,1)S(1)}, u32[]{:S(2)}, u32[]{:S(2)}) async-start(bf16[4,128,1024]{2,1,0:T(8,128)(2,1)} %bitcast.32), calls=%async_computation | async-start | bytes 2097152 | tf_op jit(solution)/shard_map/all_to_all | solution.py:95
  67.0 127.8 %reduce-scatter.2.cloned.1.call-start = ((), (), s32[]{:S(2)}) async-start(), calls=%async_computation.6 | async-start | bytes 5242880 | tf_op jit(solution)/shard_map/reduce_scatter | solution.py:107
  108.9 1.6 copy-start.2
  133.6 2.2 copy-start.5
  146.9 0.7 copy-start.7
  146.9 1.4 copy-start.6
  146.9 47.9 %copy-start.3 = (bf16[128,4096]{1,0:T(8,128)(2,1)S(1)}, bf16[128,4096]{1,0:T(8,128)(2,1)}, u32[]{:S(2)}) copy-start(bf16[128,4096]{1,0:T(8,128)(2,1)} %param.11) | copy-start | bytes 3145732
  200.1 123.2 %slice-start = ((s8[6291456]{0:T(1024)(128)(4,1)}), s8[4194304]{0:T(1024)(128)(4,1)S(1)}, s32[]{:S(2)}) async-start(s8[6291456]{0:T(1024)(128)(4,1)} %bitcast.36), calls=%async_computation.7 | async-start | bytes 8388608
  306.0 17.3 %slice-start.1 = ((s8[6291456]{0:T(1024)(128)(4,1)}), s8[2097152]{0:T(1024)(128)(4,1)S(1)}, s32[]{:S(2)}) async-start(s8[6291456]{0:T(1024)(128)(4,1)} %bitcast.36), calls=%async_computation.8 | async-start | bytes 4194304
  333.1 103.0 %copy-start.8 = (f32[128,4]{0,1:T(4,128)S(1)}, f32[128,4]{0,1:T(4,128)}, u32[]{:S(2)}) copy-start(f32[128,4]{0,1:T(4,128)} %param.17) | copy-start | bytes 6148
  436.1 5.1 %copy-start.4 = (bf16[128,4096]{1,0:T(8,128)(2,1)S(1)}, bf16[128,4096]{1,0:T(8,128)(2,1)}, u32[]{:S(2)}) copy-start(bf16[128,4096]{1,0:T(8,128)(2,1)} %reduce-scatter.2.cloned.1.call-done) | copy-start | bytes 3145732
  436.1 6.4 %copy-start.1 = (bf16[256,4096]{1,0:T(8,128)(2,1)S(1)}, bf16[256,4096]{1,0:T(8,128)(2,1)}, u32[]{:S(2)}) copy-start(bf16[256,4096]{1,0:T(8,128)(2,1)} %param.13) | copy-start | bytes 6291460
Sparse Core Ops, SparseCore 0:
  9.4 50.3 all-gather.4
  61.9 46.9 all-gather.2
  147.0 47.7 reduce-scatter.1

commit v5 on v4

--- a/solution.py
+++ b/solution.py
@@ -83,9 +83,20 @@
 
     pair = lax.axis_index("grp") % 2
     half = o_weight.shape[1] // 2
-    w_mine = lax.all_gather(
-        lax.dynamic_slice_in_dim(o_weight, pair * half, half, axis=1), "sb", axis=0, tiled=True
-    )
+    own = lax.dynamic_slice_in_dim(o_weight, pair * half, half, axis=1)
+    block_rows = o_weight.shape[0]
+    pieces = {0: own}
+    for step_dir, count in ((1, n_sb // 2), (-1, (n_sb - 1) // 2)):
+        ring = [(i, (i + step_dir) % n_sb) for i in range(n_sb)]
+        held = own
+        for k in range(1, count + 1):
+            held = lax.ppermute(held, "sb", ring)
+            pieces[-step_dir * k] = held
+    w_mine = jnp.zeros((n_sb * block_rows, half), o_weight.dtype)
+    for offset, piece in pieces.items():
+        w_mine = lax.dynamic_update_slice_in_dim(
+            w_mine, piece, ((sb + offset) % n_sb) * block_rows, axis=0
+        )
     w_other = lax.ppermute(w_mine, "grp", [(g, g ^ 1) for g in range(n_grp)])
     w_rows = jnp.zeros((w_mine.shape[0], 2 * half), o_weight.dtype)
     w_rows = lax.dynamic_update_slice_in_dim(w_rows, w_mine, pair * half, axis=1)

time: 449 us -> 460 us (1.024)
  waiting for transfers between devices: 138 us -> 123 us
  local copies, waits for them, and re-layouts: 13.2 us -> 25 us
  matrix products: 43.7 us -> 50.4 us
  starting transfers between devices: 5.02 us -> 11.3 us
    all_gather x1 -> x0, waiting for transfers between devices: 49.8 us -> none  [shards(): lax.all_gather(lax.dynamic_slice_in_dim(o_weight, pair * half, half, axis...]
    ppermute x0 -> x3, waiting for transfers between devices: none -> 44.9 us  [shards(): held = lax.ppermute(held, 'sb', ring)]
    all_to_all x1, waiting for transfers between devices: 16 us -> 7 us  [shards(): lax.all_to_all(q_send, 'sa', split_axis=0, concat_axis=0, tiled=True)]
    dot_general x4, matrix products: 7.58 us -> 14.2 us  [shards(): jnp.dot(attended[:, cols], w_rows[cols], preferred_element_type=jnp.float32)]
    dynamic_update_slice x0 -> x4, local copies, waits for them, and re-layouts: none -> 4.79 us  [shards(): lax.dynamic_update_slice_in_dim(w_mine, piece, (sb + offset) % n_sb * blo...]
  transfers between devices with their start and end apart: 5 -> 7, of which waited for: 4 -> 5; matrix products, arithmetic and copies ran while one was open for 1% -> 3% of each run, Pallas kernels for 5% -> 5%
where the time goes in v5:
time: 460 us; the launch traced here: 459 us
  blocking collectives  209 us (45%)
  waiting for transfers between devices  123 us (27%)
  matrix products  50.4 us (11%)
  local copies, waits for them, and re-layouts  25 us (5%)
  Pallas kernels  23.3 us (5%)
  between operations  13.5 us (3%)
  starting transfers between devices  11.3 us (2%)
    all_to_all x1, blocking collectives, shards(): lax.all_to_all(outgoing_rows, ('grp', 'sa', 'sb'), split_axis=0, concat_a...  106 us
    all_to_all x1, blocking collectives, shards(): lax.all_to_all(produced.reshape(arrived.shape), ('grp', 'sa', 'sb'), spli...  103 us
    reduce_scatter x1, waiting for transfers between devices, shards(): lax.psum_scatter(partial_sum.astype(jnp.bfloat16), 'sa', scatter_dimensio...  46.2 us
    ppermute x3, waiting for transfers between devices, shards(): held = lax.ppermute(held, 'sb', ring)  44.9 us
    all_gather x1, waiting for transfers between devices, shards(): kv_all = lax.all_gather(kv_pairs, ('sa', 'sb'), axis=1, tiled=True)  25 us
    pallas_call x1, Pallas kernels, attention(): pl.pallas_call(kernel, out_shape=jax.ShapeDtypeStruct((rows, heads * head...  23.3 us
    dot_general x1, matrix products, shards(): projected = jnp.dot(flat_rows, w_in[0], preferred_element_type=jnp.float32)  17.3 us
    dot_general x4, matrix products, shards(): jnp.dot(attended[:, cols], w_rows[cols], preferred_element_type=jnp.float32)  14.2 us
  transfers between devices with their start and end apart: 7, of which 5 were waited for; matrix products, arithmetic and copies ran while one was open for 3% of the time, Pallas kernels for 5%

profile of v5, /device:TPU:7, one launch (start us, length us, event | category | flops | bytes accessed | tf_op | source)
XLA Modules:
  0.0 459.0 jit_solution(11661550741992182578)
XLA Ops:
  6.5 2.5 broadcast_in_dim.5
  9.0 1.7 constant_dynamic-update-slice_fusion.5
  10.6 1.2 collective-permute-start
  11.9 24.2 %collective-permute-done = bf16[256,2048]{1,0:T(8,128)(2,1)S(1)} collective-permute-done((bf16[256,2048]{1,0:T(8,128)(2,1)}, bf16[256,2048]{1,0:T(8,128)(2,1)S(1)}, u32[]{:S(2)}, u32[]{:S(2)}) %collective-permute-start) | collective-permute-done | bytes 1048608 | tf_op jit(solution)/shard_map/ppermute | solution.py:93
  36.1 0.0 collective-permute-start.1
  36.1 2.7 collective-permute-start.2
  38.8 1.0 constant_dynamic-update-slice_fusion.4
  39.8 20.7 %collective-permute-done.1 = bf16[256,2048]{1,0:T(8,128)(2,1)S(1)} collective-permute-done((bf16[256,2048]{1,0:T(8,128)(2,1)S(1)}, bf16[256,2048]{1,0:T(8,128)(2,1)S(1)}, u32[]{:S(2)}, u32[]{:S(2)}) %collective-permute-start.1) | collective-permute-done | bytes 1048608 | tf_op jit(solution)/shard_map/ppermute | solution.py:93
  60.5 1.0 constant_dynamic-update-slice_fusion.3
  61.6 0.0 collective-permute-done.2
  61.6 1.0 constant_dynamic-update-slice_fusion.2
  62.6 2.4 collective-permute-start.3
  65.0 0.0 all-gather.2.cloned.1.call-update
  65.0 1.1 copy.28
  66.1 5.0 %all-to-all-start = ((bf16[4,128,1024]{2,1,0:T(8,128)(2,1)}), bf16[4,128,1024]{2,1,0:T(8,128)(2,1)S(1)}, u32[]{:S(2)}, u32[]{:S(2)}) async-start(bf16[4,128,1024]{2,1,0:T(8,128)(2,1)} %bitcast.32), calls=%async_computation | async-start | bytes 2097152 | tf_op jit(solution)/shard_map/all_to_all | solution.py:106
  71.1 0.1 pad_add_fusion.meta_ref
  71.2 4.3 broadcast_in_dim.4
  75.5 5.0 %constant_dynamic-update-slice_fusion.1 = bf16[1024,4096]{1,0:T(8,128)(2,1)} fusion(bf16[1024,4096]{1,0:T(8,128)(2,1)} %broadcast_in_dim.4, bf16[1024,2048]{1,0:T(8,128)(2,1)} %constant_dynamic-update-slice_fusion.2, s32[]{:T(128)S(6)} %select_n.48), kind=kLoop, calls=%fused_computation.44 | loop fusion | bytes 8388612 | tf_op jit(solution)/shard_map/dynamic_update_slice | solution.py:102
  80.4 7.0 %all-to-all-done = bf16[4,128,1024]{2,1,0:T(8,128)(2,1)S(1)} async-done(((bf16[4,128,1024]{2,1,0:T(8,128)(2,1)}), bf16[4,128,1024]{2,1,0:T(8,128)(2,1)S(1)}, u32[]{:S(2)}, u32[]{:S(2)}) %all-to-all-start) | async-done | bytes 1048608 | tf_op jit(solution)/shard_map/all_to_all | solution.py:106
  87.4 25.0 %all-gather.2.cloned.1.call-done.k_ref.v_ref = bf16[2,2048,256]{2,1,0:T(8,128)(2,1)} async-done(((bf16[2,128,256]{2,1,0:T(8,128)(2,1)}), bf16[2,2048,256]{2,1,0:T(8,128)(2,1)}) %all-gather.2.cloned.1.call-update) | async-done | bytes 2097168 | tf_op jit(solution)/shard_map/all_gather | solution.py:104
  112.4 1.6 copy-done
  114.0 23.3 %shard_map.91 = bf16[512,1024]{1,0:T(8,128)(2,1)S(1)} custom-call(s32[2]{0:T(128)S(1)} %pad_add_fusion.meta_ref, bf16[512,1024]{1,0:T(8,128)(2,1)S(1)} %bitcast.33, bf16[2,2048,256]{2,1,0:T(8,128)(2,1)S(1)} %copy-done, bf16[2,2048,256]{2,1,0:T(8,128)(2,1)S(1)} %copy-done), custom_call_target="tpu_custom_call" | custom-call | tf_op jit(solution)/shard_map/pallas_call | solution.py:44
  137.4 0.0 collective-permute-done.3
  137.4 4.8 %constant_dynamic-update-slice_fusion = bf16[1024,4096]{1,0:T(8,128)(2,1)} fusion(bf16[1024,4096]{1,0:T(8,128)(2,1)} %constant_dynamic-update-slice_fusion.1, bf16[1024,2048]{1,0:T(8,128)(2,1)} %collective-permute-done.3, s32[]{:T(128)S(6)} %select_n.57), kind=kLoop, calls=%fused_computation.43 | loop fusion | bytes 8388612 | tf_op jit(solution)/shard_map/dynamic_update_slice | solution.py:103
  142.2 2.8 convolution_convert_fusion.2
  145.1 2.8 convolution_convert_fusion.3
  147.9 2.8 convolution_convert_fusion.1
  150.8 5.6 %add_convert_fusion = bf16[512,4096]{1,0:T(8,128)(2,1)} fusion(bf16[512,4096]{1,0:T(8,128)(2,1)S(1)} %convolution_convert_fusion.1, bf16[512,4096]{1,0:T(8,128)(2,1)S(1)} %convolution_convert_fusion.2, bf16[512,4096]{1,0:T(8,128)(2,1)S(1)} %convolution_convert_fusion.3, bf16[1024,4096]{1,0:T(8,128)(2,1)} %constant_dynamic-update-slice_fusion, ...), kind=kOutput, calls=%fused_computation.8 | convolution fusion | flops 1092616192 | bytes 19136512 | tf_op jit(solution)/shard_map/dot_general | solution.py:114
  156.4 0.0 reduce-scatter.2.cloned.1.call-update
  156.5 0.7 copy-done.6
  157.1 0.1 copy.24
  157.2 0.1 eq.44
  157.3 0.3 fusion.16
  157.7 0.1 convert_element_type.84
  157.8 0.1 copy.25
  157.9 0.4 fusion.13
  158.3 46.2 %reduce-scatter.2.cloned.1.call-done = bf16[128,4096]{1,0:T(8,128)(2,1)} async-done(((bf16[512,4096]{1,0:T(8,128)(2,1)}), bf16[128,4096]{1,0:T(8,128)(2,1)}) %reduce-scatter.2.cloned.1.call-update) | async-done | bytes 1048592 | tf_op jit(solution)/shard_map/reduce_scatter | solution.py:118
  204.4 1.6 multiply_reduce_fusion.1
  206.1 3.7 convert_bitcast_fusion.1
  209.7 0.0 slice-start
  209.8 105.8 %all_to_all.15 = bf16[128,8,4096]{2,1,0:T(8,128)(2,1)S(1)} all-to-all(bf16[128,8,4096]{2,1,0:T(8,128)(2,1)S(1)} %convert_bitcast_fusion.1), channel_id=1, replica_groups=mesh['grp'=8,'sa'=4,'sb'=4] {'grp','sa','sb'}, dimensions={0} | all-to-all | bytes 16777216 | tf_op jit(solution)/shard_map/all_to_all | solution.py:149
  315.6 17.3 %fusion = f32[1024,1536]{1,0:T(8,128)} fusion(bf16[1,4096,1536]{2,1,0:T(8,128)(2,1)} %param.14, bf16[128,8,4096]{2,1,0:T(8,128)(2,1)S(1)} %all_to_all.15), kind=kOutput, calls=%fused_computation | convolution fusion | flops 12884901888 | bytes 27262976 | tf_op jit(solution)/shard_map/dot_general | solution.py:151
  332.9 0.0 slice-done
  332.9 9.8 %convert_bitcast_fusion = bf16[128,8,4096]{2,1,0:T(8,128)(2,1)S(1)} fusion(bf16[1,768,4096]{2,1,0:T(8,128)(2,1)S(1)} %bitcast.37, f32[1024,1536]{1,0:T(8,128)} %fusion), kind=kOutput, calls=%fused_computation.6 | convolution fusion | flops 6451363840 | bytes 20971520 | tf_op jit(solution)/shard_map/dot_general | solution.py:153
  342.7 0.0 copy-start.7
  342.7 102.9 %all_to_all.16 = bf16[128,8,4096]{2,1,0:T(8,128)(2,1)S(1)} all-to-all(bf16[128,8,4096]{2,1,0:T(8,128)(2,1)S(1)} %convert_bitcast_fusion), channel_id=1, replica_groups=mesh['grp'=8,'sa'=4,'sb'=4] {'grp','sa','sb'}, dimensions={0} | all-to-all | bytes 16777216 | tf_op jit(solution)/shard_map/all_to_all | solution.py:154
  445.7 5.1 %multiply_reduce_fusion = f32[128,4096]{1,0:T(8,128)S(1)} fusion(bf16[128,8,4096]{2,1,0:T(8,128)(2,1)S(1)} %all_to_all.16, f32[4,128]{1,0:T(4,128)S(1)} %bitcast.38, s32[4,128]{1,0:T(4,128)S(1)} %bitcast.35), kind=kOutput, calls=%fused_computation.5 | convolution fusion | flops 4299161600 | bytes 10489856 | tf_op jit(solution)/shard_map/dot_general | solution.py:159
  450.8 1.4 add_convert_fusion.1
  (22 shorter events, 0.1 us)
Async XLA Ops:
  6.5 2.5 copy-start.4
  6.5 105.9 %all-gather.2.cloned.1.call-start = ((), (), s32[]{:S(2)}) async-start(), calls=%async_computation.4 | async-start | bytes 2228224 | tf_op jit(solution)/shard_map/all_gather | solution.py:104
  10.6 25.5 %collective-permute-start = (bf16[256,2048]{1,0:T(8,128)(2,1)}, bf16[256,2048]{1,0:T(8,128)(2,1)S(1)}, u32[]{:S(2)}, u32[]{:S(2)}) collective-permute-start(bf16[256,2048]{1,0:T(8,128)(2,1)} %get-tuple-element.6), channel_id=1, source_target_pairs={{0,1},{1,2},{2,3},{3,0},{4,5},{5,6},{6,7},{7,4},{8,9},{9,10},{10,1... | collective-permute-start | bytes 3145736 | tf_op jit(solution)/shard_map/ppermute | solution.py:93
  36.1 24.4 %collective-permute-start.1 = (bf16[256,2048]{1,0:T(8,128)(2,1)S(1)}, bf16[256,2048]{1,0:T(8,128)(2,1)S(1)}, u32[]{:S(2)}, u32[]{:S(2)}) collective-permute-start(bf16[256,2048]{1,0:T(8,128)(2,1)S(1)} %collective-permute-done), channel_id=1, source_target_pairs={{0,1},{1,2},{2,3},{3,0},{4,5},{5,6},{6,7},{7,4},{8,9},{9,10},{10,1... | collective-permute-start | bytes 3145736 | tf_op jit(solution)/shard_map/ppermute | solution.py:93
  36.1 25.4 %collective-permute-start.2 = (bf16[256,2048]{1,0:T(8,128)(2,1)}, bf16[256,2048]{1,0:T(8,128)(2,1)S(1)}, u32[]{:S(2)}, u32[]{:S(2)}) collective-permute-start(bf16[256,2048]{1,0:T(8,128)(2,1)} %get-tuple-element.6), channel_id=1, source_target_pairs={{0,3},{1,0},{2,1},{3,2},{4,7},{5,4},{6,5},{7,6},{8,11},{9,8},{10,9... | collective-permute-start | bytes 3145736 | tf_op jit(solution)/shard_map/ppermute | solution.py:93
  60.5 4.5 copy-start.3
  62.6 74.8 %collective-permute-start.3 = (bf16[1024,2048]{1,0:T(8,128)(2,1)}, bf16[1024,2048]{1,0:T(8,128)(2,1)}, u32[]{:S(2)}, u32[]{:S(2)}) collective-permute-start(bf16[1024,2048]{1,0:T(8,128)(2,1)} %constant_dynamic-update-slice_fusion.2), channel_id=1, source_target_pairs={{0,16},{16,0},{32,48},{48,32},{64,80},{80,64},{96,112},{112,96},{1... | collective-permute-start | bytes 12582920 | tf_op jit(solution)/shard_map/ppermute | solution.py:100
  66.1 21.3 %all-to-all-start = ((bf16[4,128,1024]{2,1,0:T(8,128)(2,1)}), bf16[4,128,1024]{2,1,0:T(8,128)(2,1)S(1)}, u32[]{:S(2)}, u32[]{:S(2)}) async-start(bf16[4,128,1024]{2,1,0:T(8,128)(2,1)} %bitcast.32), calls=%async_computation | async-start | bytes 2097152 | tf_op jit(solution)/shard_map/all_to_all | solution.py:106
  71.1 133.3 %reduce-scatter.2.cloned.1.call-start = ((), (), s32[]{:S(2)}) async-start(), calls=%async_computation.5 | async-start | bytes 5242880 | tf_op jit(solution)/shard_map/reduce_scatter | solution.py:118
  112.4 1.6 copy-start
  156.4 0.7 copy-start.6
  156.4 1.4 copy-start.5
  156.4 48.0 %copy-start.1 = (bf16[128,4096]{1,0:T(8,128)(2,1)S(1)}, bf16[128,4096]{1,0:T(8,128)(2,1)}, u32[]{:S(2)}) copy-start(bf16[128,4096]{1,0:T(8,128)(2,1)} %param.11) | copy-start | bytes 3145732
  209.7 123.2 %slice-start = ((s8[6291456]{0:T(1024)(128)(4,1)}), s8[4194304]{0:T(1024)(128)(4,1)S(1)}, s32[]{:S(2)}) async-start(s8[6291456]{0:T(1024)(128)(4,1)} %bitcast.36), calls=%async_computation.6 | async-start | bytes 8388608
  315.6 17.3 %slice-start.1 = ((s8[6291456]{0:T(1024)(128)(4,1)}), s8[2097152]{0:T(1024)(128)(4,1)S(1)}, s32[]{:S(2)}) async-start(s8[6291456]{0:T(1024)(128)(4,1)} %bitcast.36), calls=%async_computation.7 | async-start | bytes 4194304
  342.7 102.9 %copy-start.7 = (f32[128,4]{0,1:T(4,128)S(1)}, f32[128,4]{0,1:T(4,128)}, u32[]{:S(2)}) copy-start(f32[128,4]{0,1:T(4,128)} %param.17) | copy-start | bytes 6148
  445.6 5.1 %copy-start.2 = (bf16[128,4096]{1,0:T(8,128)(2,1)S(1)}, bf16[128,4096]{1,0:T(8,128)(2,1)}, u32[]{:S(2)}) copy-start(bf16[128,4096]{1,0:T(8,128)(2,1)} %reduce-scatter.2.cloned.1.call-done) | copy-start | bytes 3145732
Sparse Core Ops, SparseCore 0:
  65.1 47.2 all-gather.1
  156.6 47.7 reduce-scatter.1

commit v6 on v4

--- a/solution.py
+++ b/solution.py
@@ -83,9 +83,11 @@
 
     pair = lax.axis_index("grp") % 2
     half = o_weight.shape[1] // 2
-    w_mine = lax.all_gather(
-        lax.dynamic_slice_in_dim(o_weight, pair * half, half, axis=1), "sb", axis=0, tiled=True
-    )
+    own = lax.dynamic_slice_in_dim(o_weight, pair * half, half, axis=1)
+    w_mine = lax.all_to_all(
+        jnp.broadcast_to(own[None], (n_sb,) + own.shape), "sb", split_axis=0, concat_axis=0,
+        tiled=True,
+    ).reshape(n_sb * own.shape[0], half)
     w_other = lax.ppermute(w_mine, "grp", [(g, g ^ 1) for g in range(n_grp)])
     w_rows = jnp.zeros((w_mine.shape[0], 2 * half), o_weight.dtype)
     w_rows = lax.dynamic_update_slice_in_dim(w_rows, w_mine, pair * half, axis=1)

time: 449 us -> 456 us (1.016)
  waiting for transfers between devices: 138 us -> 77.3 us
  blocking collectives: 209 us -> 261 us
  matrix products: 43.7 us -> 50.4 us
  local copies, waits for them, and re-layouts: 13.2 us -> 19.8 us
    all_to_all x0 -> x1, blocking collectives: none -> 52.2 us  [shards(): lax.all_to_all(jnp.broadcast_to(own[None], (n_sb,) + own.shape), 'sb', sp...]
    all_gather x1 -> x0, waiting for transfers between devices: 49.8 us -> none  [shards(): lax.all_gather(lax.dynamic_slice_in_dim(o_weight, pair * half, half, axis...]
    all_to_all x1, waiting for transfers between devices: 16 us -> 7.47 us  [shards(): lax.all_to_all(q_send, 'sa', split_axis=0, concat_axis=0, tiled=True)]
    dot_general x4, matrix products: 7.58 us -> 14.2 us  [shards(): jnp.dot(attended[:, cols], w_rows[cols], preferred_element_type=jnp.float32)]
  transfers between devices with their start and end apart: 5 -> 4, of which waited for: 4 -> 3; matrix products, arithmetic and copies ran while one was open for 1% -> 2% of each run, Pallas kernels for 5% -> 5%
where the time goes in v6:
time: 456 us; the launch traced here: 455 us
  blocking collectives  261 us (57%)
  waiting for transfers between devices  77.3 us (17%)
  matrix products  50.4 us (11%)
  Pallas kernels  23.1 us (5%)
  local copies, waits for them, and re-layouts  19.8 us (4%)
  between operations  13.6 us (3%)
  starting transfers between devices  6.84 us (2%)
    all_to_all x1, blocking collectives, shards(): lax.all_to_all(outgoing_rows, ('grp', 'sa', 'sb'), split_axis=0, concat_a...  106 us
    all_to_all x1, blocking collectives, shards(): lax.all_to_all(produced.reshape(arrived.shape), ('grp', 'sa', 'sb'), spli...  103 us
    all_to_all x1, blocking collectives, shards(): lax.all_to_all(jnp.broadcast_to(own[None], (n_sb,) + own.shape), 'sb', sp...  52.2 us
    reduce_scatter x1, waiting for transfers between devices, shards(): lax.psum_scatter(partial_sum.astype(jnp.bfloat16), 'sa', scatter_dimensio...  46.1 us
    all_gather x1, waiting for transfers between devices, shards(): kv_all = lax.all_gather(kv_pairs, ('sa', 'sb'), axis=1, tiled=True)  23.7 us
    pallas_call x1, Pallas kernels, attention(): pl.pallas_call(kernel, out_shape=jax.ShapeDtypeStruct((rows, heads * head...  23.1 us
    dot_general x1, matrix products, shards(): projected = jnp.dot(flat_rows, w_in[0], preferred_element_type=jnp.float32)  17.3 us
    dot_general x4, matrix products, shards(): jnp.dot(attended[:, cols], w_rows[cols], preferred_element_type=jnp.float32)  14.2 us
  transfers between devices with their start and end apart: 4, of which 3 were waited for; matrix products, arithmetic and copies ran while one was open for 2% of the time, Pallas kernels for 5%

profile of v6, /device:TPU:7, one launch (start us, length us, event | category | flops | bytes accessed | tf_op | source)
XLA Modules:
  0.0 455.4 jit_solution(16816488136973167716)
XLA Ops:
  6.5 0.0 copy-start
  6.5 0.0 all-gather.2.cloned.1.call-start
  6.5 1.6 copy-done
  8.1 0.1 constant_dynamic-slice_fusion
  8.2 0.5 broadcast_in_dim.5
  8.8 0.0 copy-start.5
  8.8 52.2 %all_to_all.20 = bf16[4,256,2048]{2,1,0:T(8,128)(2,1)} all-to-all(bf16[4,256,2048]{2,1,0:T(8,128)(2,1)S(1)} %broadcast_in_dim.5), channel_id=1, replica_groups=mesh['grp'=8,'sa'=4,'sb'=4] {'sb'}, dimensions={0} | all-to-all | bytes 8388608 | tf_op jit(solution)/shard_map/all_to_all | solution.py:87
  60.9 1.8 collective-permute-start
  62.8 0.0 all-gather.2.cloned.1.call-update
  62.8 0.0 copy-done.5
  62.8 1.1 copy.28
  63.9 5.0 %all-to-all-start = ((bf16[4,128,1024]{2,1,0:T(8,128)(2,1)}), bf16[4,128,1024]{2,1,0:T(8,128)(2,1)S(1)}, u32[]{:S(2)}, u32[]{:S(2)}) async-start(bf16[4,128,1024]{2,1,0:T(8,128)(2,1)} %bitcast.33), calls=%async_computation | async-start | bytes 2097152 | tf_op jit(solution)/shard_map/all_to_all | solution.py:97
  68.9 0.0 reduce-scatter.2.cloned.1.call-start
  68.9 0.1 pad_add_fusion.meta_ref
  69.0 4.3 broadcast_in_dim.4
  73.2 4.8 %constant_dynamic-update-slice_fusion.1 = bf16[1024,4096]{1,0:T(8,128)(2,1)} fusion(bf16[1024,4096]{1,0:T(8,128)(2,1)} %broadcast_in_dim.4, bf16[1024,2048]{1,0:T(8,128)(2,1)} %bitcast.4, s32[]{:T(128)S(6)} %select_n.20), kind=kLoop, calls=%fused_computation.44 | loop fusion | bytes 8388612 | tf_op jit(solution)/shard_map/dynamic_update_slice | solution.py:93
  78.0 7.5 %all-to-all-done = bf16[4,128,1024]{2,1,0:T(8,128)(2,1)S(1)} async-done(((bf16[4,128,1024]{2,1,0:T(8,128)(2,1)}), bf16[4,128,1024]{2,1,0:T(8,128)(2,1)S(1)}, u32[]{:S(2)}, u32[]{:S(2)}) %all-to-all-start) | async-done | bytes 1048608 | tf_op jit(solution)/shard_map/all_to_all | solution.py:97
  85.5 23.7 %all-gather.2.cloned.1.call-done.k_ref.v_ref = bf16[2,2048,256]{2,1,0:T(8,128)(2,1)} async-done(((bf16[2,128,256]{2,1,0:T(8,128)(2,1)}), bf16[2,2048,256]{2,1,0:T(8,128)(2,1)}) %all-gather.2.cloned.1.call-update) | async-done | bytes 2097168 | tf_op jit(solution)/shard_map/all_gather | solution.py:95
  109.2 1.6 copy-done.2
  110.8 23.1 %shard_map.91 = bf16[512,1024]{1,0:T(8,128)(2,1)S(1)} custom-call(s32[2]{0:T(128)S(1)} %pad_add_fusion.meta_ref, bf16[512,1024]{1,0:T(8,128)(2,1)S(1)} %bitcast.34, bf16[2,2048,256]{2,1,0:T(8,128)(2,1)S(1)} %copy-done.2, bf16[2,2048,256]{2,1,0:T(8,128)(2,1)S(1)} %copy-done.2), custom_call_target="tpu_custom_call" | custom-call | tf_op jit(solution)/shard_map/pallas_call | solution.py:44
  133.9 0.0 collective-permute-done
  133.9 4.8 %constant_dynamic-update-slice_fusion = bf16[1024,4096]{1,0:T(8,128)(2,1)} fusion(bf16[1024,4096]{1,0:T(8,128)(2,1)} %constant_dynamic-update-slice_fusion.1, bf16[1024,2048]{1,0:T(8,128)(2,1)} %collective-permute-done, s32[]{:T(128)S(6)} %select_n.21), kind=kLoop, calls=%fused_computation.43 | loop fusion | bytes 8388612 | tf_op jit(solution)/shard_map/dynamic_update_slice | solution.py:94
  138.7 2.8 convolution_convert_fusion.2
  141.5 2.8 convolution_convert_fusion.3
  144.4 2.8 convolution_convert_fusion.1
  147.3 5.6 %add_convert_fusion = bf16[512,4096]{1,0:T(8,128)(2,1)} fusion(bf16[512,4096]{1,0:T(8,128)(2,1)S(1)} %convolution_convert_fusion.1, bf16[512,4096]{1,0:T(8,128)(2,1)S(1)} %convolution_convert_fusion.2, bf16[512,4096]{1,0:T(8,128)(2,1)S(1)} %convolution_convert_fusion.3, bf16[1024,4096]{1,0:T(8,128)(2,1)} %constant_dynamic-update-slice_fusion, ...), kind=kOutput, calls=%fused_computation.8 | convolution fusion | flops 1092616192 | bytes 19136512 | tf_op jit(solution)/shard_map/dot_general | solution.py:105
  152.9 0.0 reduce-scatter.2.cloned.1.call-update
  152.9 0.7 copy-done.7
  153.6 0.1 copy.24
  153.7 0.1 eq.40
  153.8 0.3 fusion.16
  154.1 0.1 convert_element_type.84
  154.2 0.1 copy.25
  154.3 0.0 copy-done.6
  154.3 0.4 fusion.13
  154.7 46.1 %reduce-scatter.2.cloned.1.call-done = bf16[128,4096]{1,0:T(8,128)(2,1)} async-done(((bf16[512,4096]{1,0:T(8,128)(2,1)}), bf16[128,4096]{1,0:T(8,128)(2,1)}) %reduce-scatter.2.cloned.1.call-update) | async-done | bytes 1048592 | tf_op jit(solution)/shard_map/reduce_scatter | solution.py:109
  200.9 0.0 copy-done.3
  200.9 1.6 multiply_reduce_fusion.1
  202.5 3.7 convert_bitcast_fusion.1
  206.2 0.0 slice-start
  206.2 105.8 %all_to_all.21 = bf16[128,8,4096]{2,1,0:T(8,128)(2,1)S(1)} all-to-all(bf16[128,8,4096]{2,1,0:T(8,128)(2,1)S(1)} %convert_bitcast_fusion.1), channel_id=1, replica_groups=mesh['grp'=8,'sa'=4,'sb'=4] {'grp','sa','sb'}, dimensions={0} | all-to-all | bytes 16777216 | tf_op jit(solution)/shard_map/all_to_all | solution.py:140
  312.0 17.3 %fusion = f32[1024,1536]{1,0:T(8,128)} fusion(bf16[1,4096,1536]{2,1,0:T(8,128)(2,1)} %param.14, bf16[128,8,4096]{2,1,0:T(8,128)(2,1)S(1)} %all_to_all.21), kind=kOutput, calls=%fused_computation | convolution fusion | flops 12884901888 | bytes 27262976 | tf_op jit(solution)/shard_map/dot_general | solution.py:142
  329.4 9.8 %convert_bitcast_fusion = bf16[128,8,4096]{2,1,0:T(8,128)(2,1)S(1)} fusion(bf16[1,768,4096]{2,1,0:T(8,128)(2,1)S(1)} %bitcast.38, f32[1024,1536]{1,0:T(8,128)} %fusion), kind=kOutput, calls=%fused_computation.6 | convolution fusion | flops 6451363840 | bytes 20971520 | tf_op jit(solution)/shard_map/dot_general | solution.py:144
  339.2 0.0 copy-start.8
  339.2 102.9 %all_to_all.22 = bf16[128,8,4096]{2,1,0:T(8,128)(2,1)S(1)} all-to-all(bf16[128,8,4096]{2,1,0:T(8,128)(2,1)S(1)} %convert_bitcast_fusion), channel_id=1, replica_groups=mesh['grp'=8,'sa'=4,'sb'=4] {'grp','sa','sb'}, dimensions={0} | all-to-all | bytes 16777216 | tf_op jit(solution)/shard_map/all_to_all | solution.py:145
  442.1 5.1 %multiply_reduce_fusion = f32[128,4096]{1,0:T(8,128)S(1)} fusion(bf16[128,8,4096]{2,1,0:T(8,128)(2,1)S(1)} %all_to_all.22, f32[4,128]{1,0:T(4,128)S(1)} %bitcast.39, s32[4,128]{1,0:T(4,128)S(1)} %bitcast.36), kind=kOutput, calls=%fused_computation.5 | convolution fusion | flops 4299161600 | bytes 10489856 | tf_op jit(solution)/shard_map/dot_general | solution.py:150
  447.2 0.0 copy-done.4
  447.2 1.3 add_convert_fusion.1
  (16 shorter events, 0.1 us)
Async XLA Ops:
  6.5 1.6 copy-start
  6.5 102.6 %all-gather.2.cloned.1.call-start = ((), (), s32[]{:S(2)}) async-start(), calls=%async_computation.5 | async-start | bytes 2228224 | tf_op jit(solution)/shard_map/all_gather | solution.py:95
  8.8 54.0 %copy-start.5 = (bf16[128,4096]{1,0:T(8,128)(2,1)S(1)}, bf16[128,4096]{1,0:T(8,128)(2,1)}, u32[]{:S(2)}) copy-start(bf16[128,4096]{1,0:T(8,128)(2,1)} %param.9) | copy-start | bytes 3145732
  60.9 73.0 %collective-permute-start = (bf16[1024,2048]{1,0:T(8,128)(2,1)}, bf16[1024,2048]{1,0:T(8,128)(2,1)}, u32[]{:S(2)}, u32[]{:S(2)}) collective-permute-start(bf16[1024,2048]{1,0:T(8,128)(2,1)} %bitcast.4), channel_id=1, source_target_pairs={{0,16},{16,0},{32,48},{48,32},{64,80},{80,64},{96,112},{112,96},{1... | collective-permute-start | bytes 12582920 | tf_op jit(solution)/shard_map/ppermute | solution.py:91
  63.9 21.6 %all-to-all-start = ((bf16[4,128,1024]{2,1,0:T(8,128)(2,1)}), bf16[4,128,1024]{2,1,0:T(8,128)(2,1)S(1)}, u32[]{:S(2)}, u32[]{:S(2)}) async-start(bf16[4,128,1024]{2,1,0:T(8,128)(2,1)} %bitcast.33), calls=%async_computation | async-start | bytes 2097152 | tf_op jit(solution)/shard_map/all_to_all | solution.py:97
  68.9 132.0 %reduce-scatter.2.cloned.1.call-start = ((), (), s32[]{:S(2)}) async-start(), calls=%async_computation.6 | async-start | bytes 5242880 | tf_op jit(solution)/shard_map/reduce_scatter | solution.py:109
  109.2 1.6 copy-start.2
  152.9 0.7 copy-start.7
  152.9 1.4 copy-start.6
  152.9 47.9 %copy-start.3 = (bf16[128,4096]{1,0:T(8,128)(2,1)S(1)}, bf16[128,4096]{1,0:T(8,128)(2,1)}, u32[]{:S(2)}) copy-start(bf16[128,4096]{1,0:T(8,128)(2,1)} %param.11) | copy-start | bytes 3145732
  206.2 123.2 %slice-start = ((s8[6291456]{0:T(1024)(128)(4,1)}), s8[4194304]{0:T(1024)(128)(4,1)S(1)}, s32[]{:S(2)}) async-start(s8[6291456]{0:T(1024)(128)(4,1)} %bitcast.37), calls=%async_computation.7 | async-start | bytes 8388608
  312.0 17.3 %slice-start.1 = ((s8[6291456]{0:T(1024)(128)(4,1)}), s8[2097152]{0:T(1024)(128)(4,1)S(1)}, s32[]{:S(2)}) async-start(s8[6291456]{0:T(1024)(128)(4,1)} %bitcast.37), calls=%async_computation.8 | async-start | bytes 4194304
  339.2 102.9 %copy-start.8 = (f32[128,4]{0,1:T(4,128)S(1)}, f32[128,4]{0,1:T(4,128)}, u32[]{:S(2)}) copy-start(f32[128,4]{0,1:T(4,128)} %param.17) | copy-start | bytes 6148
  442.1 5.1 %copy-start.4 = (bf16[128,4096]{1,0:T(8,128)(2,1)S(1)}, bf16[128,4096]{1,0:T(8,128)(2,1)}, u32[]{:S(2)}) copy-start(bf16[128,4096]{1,0:T(8,128)(2,1)} %reduce-scatter.2.cloned.1.call-done) | copy-start | bytes 3145732
  442.1 6.4 %copy-start.1 = (bf16[256,4096]{1,0:T(8,128)(2,1)S(1)}, bf16[256,4096]{1,0:T(8,128)(2,1)}, u32[]{:S(2)}) copy-start(bf16[256,4096]{1,0:T(8,128)(2,1)} %param.13) | copy-start | bytes 6291460
Sparse Core Ops, SparseCore 0:
  62.9 46.2 all-gather.1
  153.1 47.7 reduce-scatter.1

commit v7 on v4

--- a/solution.py
+++ b/solution.py
@@ -36,7 +36,7 @@
 
 def attention(meta, q_rows, kv_all, heads, head_size, tok_dev, n_sb):
     rows = q_rows.shape[0]
-    seq_len = kv_all.shape[1]
+    seq_len = kv_all.shape[0]
     block = min(Q_BLOCK, rows)
     kernel = functools.partial(
         _attend_kernel, block=block, scale=1.0 / head_size**0.5, tok_dev=tok_dev, n_sb=n_sb
@@ -49,8 +49,8 @@
             grid=(heads, rows // block),
             in_specs=[
                 pl.BlockSpec((block, head_size), lambda h, i, m: (i, h)),
-                pl.BlockSpec((None, seq_len, head_size), lambda h, i, m: (0, 0, m[1])),
-                pl.BlockSpec((None, seq_len, head_size), lambda h, i, m: (1, 0, m[1])),
+                pl.BlockSpec((seq_len, head_size), lambda h, i, m: (0, 0)),
+                pl.BlockSpec((seq_len, head_size), lambda h, i, m: (0, 1)),
             ],
             out_specs=pl.BlockSpec((block, head_size), lambda h, i, m: (i, h)),
         ),
@@ -86,16 +86,29 @@
     w_mine = lax.all_gather(
         lax.dynamic_slice_in_dim(o_weight, pair * half, half, axis=1), "sb", axis=0, tiled=True
     )
+    q_send = queries.reshape(tok_dev, n_sa, heads_here * head_size).transpose(1, 0, 2)
+    kv_heads = kv_pairs.reshape(2, tok_dev, key_heads, head_size)
+    head_of_dest = (jnp.arange(n_sa) * heads_here) // sharing
+    kv_send = jnp.take(kv_heads, head_of_dest, axis=2)
+    kv_send = kv_send.transpose(2, 1, 0, 3).reshape(n_sa, tok_dev, 2 * head_size)
+    packed = lax.all_to_all(
+        jnp.concatenate([q_send, kv_send], axis=2), "sa", split_axis=0, concat_axis=0, tiled=True
+    )
+    q_rows = packed[:, :, : heads_here * head_size].reshape(n_sa * tok_dev, heads_here * head_size)
+    kv_col = packed[:, :, heads_here * head_size :]
+    kv_grid = lax.all_to_all(
+        jnp.broadcast_to(kv_col[None], (n_sb,) + kv_col.shape), "sb", split_axis=0,
+        concat_axis=0, tiled=True,
+    )
+    kv_all = kv_grid.transpose(1, 0, 2, 3).reshape(n_seq * tok_dev, 2 * head_size)
+    meta = jnp.stack([sb, jnp.zeros_like(sb)]).astype(jnp.int32)
+    attended = attention(meta, q_rows, kv_all, heads_here, head_size, tok_dev, n_sb)
+
+    w_mine, attended = lax.optimization_barrier((w_mine, attended))
     w_other = lax.ppermute(w_mine, "grp", [(g, g ^ 1) for g in range(n_grp)])
     w_rows = jnp.zeros((w_mine.shape[0], 2 * half), o_weight.dtype)
     w_rows = lax.dynamic_update_slice_in_dim(w_rows, w_mine, pair * half, axis=1)
     w_rows = lax.dynamic_update_slice_in_dim(w_rows, w_other, (1 - pair) * half, axis=1)
-    kv_all = lax.all_gather(kv_pairs, ("sa", "sb"), axis=1, tiled=True)
-    q_send = queries.reshape(tok_dev, n_sa, heads_here * head_size).transpose(1, 0, 2)
-    q_rows = lax.all_to_all(q_send, "sa", split_axis=0, concat_axis=0, tiled=True)
-    q_rows = q_rows.reshape(n_sa * tok_dev, heads_here * head_size)
-    meta = jnp.stack([sb, (sa * heads_here) // sharing]).astype(jnp.int32)
-    attended = attention(meta, q_rows, kv_all, heads_here, head_size, tok_dev, n_sb)
 
     partial_sum = None
     for j in range(w_rows.shape[0] // block_rows):

time: 449 us -> 410 us (0.913)
  waiting for transfers between devices: 138 us -> 71.6 us
  blocking collectives: 209 us -> 231 us
    all_gather x1, waiting for transfers between devices: 49.8 us -> 0.02 us  [shards(): lax.all_gather(lax.dynamic_slice_in_dim(o_weight, pair * half, half, axis...]
    all_gather x1 -> x0, waiting for transfers between devices: 25.8 us -> none  [shards(): kv_all = lax.all_gather(kv_pairs, ('sa', 'sb'), axis=1, tiled=True)]
    all_to_all x0 -> x1, blocking collectives: none -> 21.9 us  [shards(): lax.all_to_all(jnp.concatenate([q_send, kv_send], axis=2), 'sa', split_ax...]
    all_to_all x1, waiting for transfers between devices: 16 us -> 24.8 us  [shards(): lax.all_to_all(jnp.broadcast_to(kv_col[None], (n_sb,) + kv_col.shape), 's...]
  transfers between devices with their start and end apart: 5 -> 4, of which waited for: 4 -> 3; matrix products, arithmetic and copies ran while one was open for 1% -> 2% of each run, Pallas kernels for 5% -> 6%
where the time goes in v7:
time: 410 us; the launch traced here: 409 us
  blocking collectives  231 us (56%)
  waiting for transfers between devices  71.6 us (17%)
  matrix products  43.6 us (11%)
  Pallas kernels  23.1 us (6%)
  local copies, waits for them, and re-layouts  15.3 us (4%)
  between operations  13.7 us (3%)
  starting transfers between devices  7.37 us (2%)
    all_to_all x1, blocking collectives, shards(): lax.all_to_all(outgoing_rows, ('grp', 'sa', 'sb'), split_axis=0, concat_a...  106 us
    all_to_all x1, blocking collectives, shards(): lax.all_to_all(produced.reshape(arrived.shape), ('grp', 'sa', 'sb'), spli...  103 us
    reduce_scatter x1, waiting for transfers between devices, shards(): lax.psum_scatter(partial_sum.astype(jnp.bfloat16), 'sa', scatter_dimensio...  42.5 us
    all_to_all x1, waiting for transfers between devices, shards(): lax.all_to_all(jnp.broadcast_to(kv_col[None], (n_sb,) + kv_col.shape), 's...  24.8 us
    pallas_call x1, Pallas kernels, attention(): pl.pallas_call(kernel, out_shape=jax.ShapeDtypeStruct((rows, heads * head...  23.1 us
    all_to_all x1, blocking collectives, shards(): lax.all_to_all(jnp.concatenate([q_send, kv_send], axis=2), 'sa', split_ax...  21.9 us
    dot_general x1, matrix products, shards(): projected = jnp.dot(flat_rows, w_in[0], preferred_element_type=jnp.float32)  17.2 us
    dot_general x1, matrix products, shards(): jnp.dot(hidden, w_down[0], preferred_element_type=jnp.float32)  9.8 us
  transfers between devices with their start and end apart: 4, of which 3 were waited for; matrix products, arithmetic and copies ran while one was open for 2% of the time, Pallas kernels for 6%

profile of v7, /device:TPU:7, one launch (start us, length us, event | category | flops | bytes accessed | tf_op | source)
XLA Modules:
  0.0 409.1 jit_solution(6516363227578272714)
XLA Ops:
  6.5 1.6 copy-done
  8.1 1.1 constant_dynamic-slice_fusion
  9.2 0.0 all-gather.2.cloned.1.call-update
  9.2 1.0 copy.49
  10.3 0.1 copy.50
  10.4 0.6 gather_fusion
  11.1 0.1 select_bitcast_fusion
  11.2 0.2 copy.51
  11.3 0.1 copy.52
  11.5 0.1 copy.58
  11.6 0.1 pad_maximum_fusion
  11.7 21.9 %all_to_all.20 = bf16[4,128,1280]{2,1,0:T(8,128)(2,1)S(1)} all-to-all(bf16[4,128,1280]{2,1,0:T(8,128)(2,1)S(1)} %pad_maximum_fusion), channel_id=1, replica_groups=mesh['grp'=8,'sa'=4,'sb'=4] {'sa'}, dimensions={0} | all-to-all | bytes 2621440 | tf_op jit(solution)/shard_map/all_to_all | solution.py:94
  33.6 1.2 broadcast_in_dim.26
  34.8 4.2 %all-to-all-start.1 = ((bf16[4,4,128,256]{3,2,1,0:T(8,128)(2,1)}), bf16[4,4,128,256]{3,2,1,0:T(8,128)(2,1)}, u32[]{:S(2)}, u32[]{:S(2)}) async-start(bf16[4,4,128,256]{3,2,1,0:T(8,128)(2,1)} %broadcast_in_dim.26), calls=%async_computation.1 | async-start | bytes 2097152 | tf_op jit(solution)/shard_map/all_to_all | solution.py:99
  39.0 0.0 reduce-scatter.2.cloned.1.call-start
  39.1 0.1 pad_add_fusion.meta_ref
  39.2 1.3 slice.50
  40.5 24.8 %all-to-all-done.1 = bf16[4,4,128,256]{3,2,1,0:T(8,128)(2,1)} async-done(((bf16[4,4,128,256]{3,2,1,0:T(8,128)(2,1)}), bf16[4,4,128,256]{3,2,1,0:T(8,128)(2,1)}, u32[]{:S(2)}, u32[]{:S(2)}) %all-to-all-start.1) | async-done | bytes 1048608 | tf_op jit(solution)/shard_map/all_to_all | solution.py:99
  65.3 1.3 copy.53
  66.6 23.1 %shard_map.91 = bf16[512,1024]{1,0:T(8,128)(2,1)S(1)} custom-call(s32[2]{0:T(128)S(1)} %pad_add_fusion.meta_ref, bf16[512,1024]{1,0:T(8,128)(2,1)S(1)} %bitcast.42, bf16[2048,256]{1,0:T(8,128)(2,1)S(1)} %bitcast.40, bf16[2048,256]{1,0:T(8,128)(2,1)S(1)} %bitcast.41), custom_call_target="tpu_custom_call" | custom-call | tf_op jit(solution)/shard_map/pallas_call | solution.py:44
  89.8 0.0 all-gather.2.cloned.1.call-done
  89.8 3.1 collective-permute-start
  92.9 1.0 broadcast_in_dim.27
  93.9 1.1 copy-done.5
  95.1 0.6 constant_dynamic-update-slice_fusion.1
  95.7 4.3 %collective-permute-done = bf16[1024,2048]{1,0:T(8,128)(2,1)} collective-permute-done((bf16[1024,2048]{1,0:T(8,128)(2,1)}, bf16[1024,2048]{1,0:T(8,128)(2,1)}, u32[]{:S(2)}, u32[]{:S(2)}) %collective-permute-start) | collective-permute-done | bytes 4194336 | tf_op jit(solution)/shard_map/ppermute | solution.py:108
  100.0 2.8 constant_dynamic-update-slice_fusion
  102.8 1.3 convolution_convert_fusion.3
  104.1 1.3 convolution_convert_fusion.2
  105.3 1.3 convolution_convert_fusion.1
  106.6 3.8 add_convert_fusion
  110.4 0.0 reduce-scatter.2.cloned.1.call-update
  110.4 0.7 copy-done.8
  111.1 0.1 copy.54
  111.2 0.1 eq.40
  111.3 0.3 fusion.16
  111.6 0.1 convert_element_type.84
  111.7 0.1 copy.55
  111.8 0.4 fusion.13
  112.2 42.5 %reduce-scatter.2.cloned.1.call-done = bf16[128,4096]{1,0:T(8,128)(2,1)} async-done(((bf16[512,4096]{1,0:T(8,128)(2,1)}), bf16[128,4096]{1,0:T(8,128)(2,1)}) %reduce-scatter.2.cloned.1.call-update) | async-done | bytes 1048592 | tf_op jit(solution)/shard_map/reduce_scatter | solution.py:120
  154.7 1.6 multiply_reduce_fusion.1
  156.3 3.7 convert_bitcast_fusion.1
  160.0 105.9 %all_to_all.21 = bf16[128,8,4096]{2,1,0:T(8,128)(2,1)S(1)} all-to-all(bf16[128,8,4096]{2,1,0:T(8,128)(2,1)S(1)} %convert_bitcast_fusion.1), channel_id=1, replica_groups=mesh['grp'=8,'sa'=4,'sb'=4] {'grp','sa','sb'}, dimensions={0} | all-to-all | bytes 16777216 | tf_op jit(solution)/shard_map/all_to_all | solution.py:151
  265.9 17.2 %fusion = f32[1024,1536]{1,0:T(8,128)} fusion(bf16[1,4096,1536]{2,1,0:T(8,128)(2,1)} %param.14, bf16[128,8,4096]{2,1,0:T(8,128)(2,1)S(1)} %all_to_all.21), kind=kOutput, calls=%fused_computation.1 | convolution fusion | flops 12884901888 | bytes 27262976 | tf_op jit(solution)/shard_map/dot_general | solution.py:153
  283.0 9.8 %convert_bitcast_fusion = bf16[128,8,4096]{2,1,0:T(8,128)(2,1)S(1)} fusion(bf16[1,768,4096]{2,1,0:T(8,128)(2,1)S(1)} %bitcast.49, f32[1024,1536]{1,0:T(8,128)} %fusion), kind=kOutput, calls=%fused_computation.7 | convolution fusion | flops 6451363840 | bytes 20971520 | tf_op jit(solution)/shard_map/dot_general | solution.py:155
  292.9 102.9 %all_to_all.22 = bf16[128,8,4096]{2,1,0:T(8,128)(2,1)S(1)} all-to-all(bf16[128,8,4096]{2,1,0:T(8,128)(2,1)S(1)} %convert_bitcast_fusion), channel_id=1, replica_groups=mesh['grp'=8,'sa'=4,'sb'=4] {'grp','sa','sb'}, dimensions={0} | all-to-all | bytes 16777216 | tf_op jit(solution)/shard_map/all_to_all | solution.py:156
  395.8 5.1 %multiply_reduce_fusion = f32[128,4096]{1,0:T(8,128)S(1)} fusion(bf16[128,8,4096]{2,1,0:T(8,128)(2,1)S(1)} %all_to_all.22, f32[4,128]{1,0:T(4,128)S(1)} %bitcast.50, s32[4,128]{1,0:T(4,128)S(1)} %bitcast.47), kind=kOutput, calls=%fused_computation.6 | convolution fusion | flops 4299161600 | bytes 10489856 | tf_op jit(solution)/shard_map/dot_general | solution.py:161
  400.9 1.4 add_convert_fusion.1
  (31 shorter events, 0.1 us)
Async XLA Ops:
  6.5 1.6 copy-start
  6.5 5.0 %copy-start.6 = (bf16[128,4096]{1,0:T(8,128)(2,1)S(1)}, bf16[128,4096]{1,0:T(8,128)(2,1)}, u32[]{:S(2)}) copy-start(bf16[128,4096]{1,0:T(8,128)(2,1)} %param.9) | copy-start | bytes 3145732
  6.5 83.3 %all-gather.2.cloned.1.call-start = ((), (), s32[]{:S(2)}) async-start(), calls=%async_computation.5 | async-start | bytes 5242880 | tf_op jit(solution)/shard_map/all_gather | solution.py:86
  33.6 5.5 %copy-start.4 = (bf16[4,128,1280]{2,1,0:T(8,128)(2,1)}, bf16[4,128,1280]{2,1,0:T(8,128)(2,1)S(1)}, u32[]{:S(2)}) copy-start(bf16[4,128,1280]{2,1,0:T(8,128)(2,1)S(1)} %all_to_all.20) | copy-start | bytes 3932164
  34.8 30.5 %all-to-all-start.1 = ((bf16[4,4,128,256]{3,2,1,0:T(8,128)(2,1)}), bf16[4,4,128,256]{3,2,1,0:T(8,128)(2,1)}, u32[]{:S(2)}, u32[]{:S(2)}) async-start(bf16[4,4,128,256]{3,2,1,0:T(8,128)(2,1)} %broadcast_in_dim.26), calls=%async_computation.1 | async-start | bytes 2097152 | tf_op jit(solution)/shard_map/all_to_all | solution.py:99
  39.0 115.6 %reduce-scatter.2.cloned.1.call-start = ((), (), s32[]{:S(2)}) async-start(), calls=%async_computation.6 | async-start | bytes 5242880 | tf_op jit(solution)/shard_map/reduce_scatter | solution.py:120
  89.8 10.2 %collective-permute-start = (bf16[1024,2048]{1,0:T(8,128)(2,1)}, bf16[1024,2048]{1,0:T(8,128)(2,1)}, u32[]{:S(2)}, u32[]{:S(2)}) collective-permute-start(bf16[1024,2048]{1,0:T(8,128)(2,1)} %all-gather.2.cloned.1.call-done), channel_id=1, source_target_pairs={{0,16},{16,0},{32,48},{48,32},{64,80},{80,64},{96,112},{112,96},{1... | collective-permute-start | bytes 12582920 | tf_op jit(solution)/shard_map/ppermute | solution.py:108
  92.9 2.2 copy-start.5
  110.4 0.7 copy-start.8
  110.4 1.4 copy-start.7
  110.4 44.3 %copy-start.2 = (bf16[128,4096]{1,0:T(8,128)(2,1)S(1)}, bf16[128,4096]{1,0:T(8,128)(2,1)}, u32[]{:S(2)}) copy-start(bf16[128,4096]{1,0:T(8,128)(2,1)} %param.11) | copy-start | bytes 3145732
  160.0 123.1 %slice-start = ((s8[6291456]{0:T(1024)(128)(4,1)}), s8[4194304]{0:T(1024)(128)(4,1)S(1)}, s32[]{:S(2)}) async-start(s8[6291456]{0:T(1024)(128)(4,1)} %bitcast.48), calls=%async_computation.7 | async-start | bytes 8388608
  265.9 17.2 %slice-start.1 = ((s8[6291456]{0:T(1024)(128)(4,1)}), s8[2097152]{0:T(1024)(128)(4,1)S(1)}, s32[]{:S(2)}) async-start(s8[6291456]{0:T(1024)(128)(4,1)} %bitcast.48), calls=%async_computation.8 | async-start | bytes 4194304
  292.9 102.9 %copy-start.9 = (f32[128,4]{0,1:T(4,128)S(1)}, f32[128,4]{0,1:T(4,128)}, u32[]{:S(2)}) copy-start(f32[128,4]{0,1:T(4,128)} %param.17) | copy-start | bytes 6148
  395.8 5.1 %copy-start.3 = (bf16[128,4096]{1,0:T(8,128)(2,1)S(1)}, bf16[128,4096]{1,0:T(8,128)(2,1)}, u32[]{:S(2)}) copy-start(bf16[128,4096]{1,0:T(8,128)(2,1)} %reduce-scatter.2.cloned.1.call-done) | copy-start | bytes 3145732
  395.8 6.5 %copy-start.1 = (bf16[256,4096]{1,0:T(8,128)(2,1)S(1)}, bf16[256,4096]{1,0:T(8,128)(2,1)}, u32[]{:S(2)}) copy-start(bf16[256,4096]{1,0:T(8,128)(2,1)} %param.13) | copy-start | bytes 6291460
Sparse Core Ops, SparseCore 0:
  9.4 61.5 all-gather.1
  110.5 44.0 reduce-scatter.1

commit v8 on v7

--- a/solution.py
+++ b/solution.py
@@ -140,23 +140,37 @@
     before = (col < row).astype(jnp.bfloat16)
     earlier = jnp.dot(before, onehot, preferred_element_type=jnp.float32)
     rank = jnp.sum(earlier * onehot.astype(jnp.float32), axis=1).astype(jnp.int32)
-    slot_index = flat_ids * capacity + rank
+    halves = 2
+    cap_half = capacity // halves
+    slots_half = devices * cap_half
+    slot_index = (rank // cap_half) * slots_half + flat_ids * cap_half + rank % cap_half
     picks = slot_index[:, None] == jnp.arange(slots, dtype=jnp.int32)[None, :]
     token_slots = jnp.any(picks.reshape(tok_dev, top_count, slots), axis=1).astype(jnp.bfloat16)
-    outgoing_rows = lax.dot_general(
-        token_slots, normed, (((0,), (0,)), ((), ())), preferred_element_type=jnp.float32
-    ).astype(jnp.bfloat16)
-    outgoing_rows = outgoing_rows.reshape(devices, capacity, width)
     ffe_width = w_down.shape[1]
-    arrived = lax.all_to_all(outgoing_rows, ("grp", "sa", "sb"), split_axis=0, concat_axis=0, tiled=True)
-    flat_rows = arrived.reshape(-1, width)
-    projected = jnp.dot(flat_rows, w_in[0], preferred_element_type=jnp.float32)
-    hidden = (jax.nn.silu(projected[:, :ffe_width]) * projected[:, ffe_width:]).astype(jnp.bfloat16)
-    produced = jnp.dot(hidden, w_down[0], preferred_element_type=jnp.float32).astype(jnp.bfloat16)
-    returned = lax.all_to_all(
-        produced.reshape(arrived.shape), ("grp", "sa", "sb"), split_axis=0, concat_axis=0, tiled=True
-    )
-    returned = returned.reshape(slots, width)
+    returned = []
+    for h in range(halves):
+        outgoing_rows = lax.dot_general(
+            token_slots[:, h * slots_half : (h + 1) * slots_half], normed,
+            (((0,), (0,)), ((), ())), preferred_element_type=jnp.float32,
+        ).astype(jnp.bfloat16).reshape(devices, cap_half, width)
+        arrived = lax.all_to_all(
+            outgoing_rows, ("grp", "sa", "sb"), split_axis=0, concat_axis=0, tiled=True
+        )
+        flat_rows = arrived.reshape(-1, width)
+        projected = jnp.dot(flat_rows, w_in[0], preferred_element_type=jnp.float32)
+        hidden = (jax.nn.silu(projected[:, :ffe_width]) * projected[:, ffe_width:]).astype(
+            jnp.bfloat16
+        )
+        produced = jnp.dot(hidden, w_down[0], preferred_element_type=jnp.float32).astype(
+            jnp.bfloat16
+        )
+        returned.append(
+            lax.all_to_all(
+                produced.reshape(arrived.shape), ("grp", "sa", "sb"), split_axis=0,
+                concat_axis=0, tiled=True,
+            ).reshape(slots_half, width)
+        )
+    returned = jnp.concatenate(returned, axis=0)
     picks_by_choice = picks.reshape(tok_dev, top_count, slots).transpose(1, 0, 2)
     picked = jnp.dot(
         picks_by_choice.reshape(n_flat, slots).astype(jnp.bfloat16),

time: 410 us -> 425 us (1.037)
  blocking collectives: 231 us -> 21.9 us
  waiting for transfers between devices: 71.6 us -> 195 us
  local copies, waits for them, and re-layouts: 15.3 us -> 71.8 us
  starting transfers between devices: 7.37 us -> 33.6 us
  matrix products: 43.6 us -> 59.6 us
    all_to_all x2 -> x0, blocking collectives: 209 us -> none  [the longest x1 106 us: shards(): lax.all_to_all(outgoing_rows, ('grp', 'sa', 'sb'), split_axis=0, concat_a...]
    all_to_all x0 -> x4, waiting for transfers between devices: none -> 123 us  [the longest x2 63.4 us: shards(): lax.all_to_all(produced.reshape(arrived.shape), ('grp', 'sa', 'sb'), spli...]
    reshape x0 -> x8, local copies, waits for them, and re-layouts: none -> 56.5 us  [the longest x2 14.4 us: shards(): outgoing_rows = lax.dot_general(token_slots[:, h * slots_half:(h + 1) * s...]
    all_to_all x0 -> x4, starting transfers between devices: none -> 26.2 us  [the longest x2 14.6 us: shards(): lax.all_to_all(outgoing_rows, ('grp', 'sa', 'sb'), split_axis=0, concat_a...]
    dot_general x1 -> x2, matrix products: 9.8 us -> 15.7 us  [shards(): jnp.dot(hidden, w_down[0], preferred_element_type=jnp.float32)]
    dot_general x1 -> x2, matrix products: 17.2 us -> 21 us  [shards(): projected = jnp.dot(flat_rows, w_in[0], preferred_element_type=jnp.float32)]
  transfers between devices with their start and end apart: 4 -> 8, of which waited for: 3 -> 7; matrix products, arithmetic and copies ran while one was open for 2% -> 22% of each run, Pallas kernels for 6% -> 5%
where the time goes in v8:
time: 425 us; the launch traced here: 422 us
  waiting for transfers between devices  195 us (46%)
  local copies, waits for them, and re-layouts  71.8 us (17%)
  matrix products  59.6 us (14%)
  starting transfers between devices  33.6 us (8%)
  Pallas kernels  23.1 us (5%)
  blocking collectives  21.9 us (5%)
  between operations  13.7 us (3%)
    all_to_all x2, waiting for transfers between devices, shards(): lax.all_to_all(produced.reshape(arrived.shape), ('grp', 'sa', 'sb'), spli...  63.4 us
    all_to_all x2, waiting for transfers between devices, shards(): lax.all_to_all(outgoing_rows, ('grp', 'sa', 'sb'), split_axis=0, concat_a...  59.8 us
    reduce_scatter x1, waiting for transfers between devices, shards(): lax.psum_scatter(partial_sum.astype(jnp.bfloat16), 'sa', scatter_dimensio...  42.4 us
    all_to_all x1, waiting for transfers between devices, shards(): lax.all_to_all(jnp.broadcast_to(kv_col[None], (n_sb,) + kv_col.shape), 's...  24.8 us
    pallas_call x1, Pallas kernels, attention(): pl.pallas_call(kernel, out_shape=jax.ShapeDtypeStruct((rows, heads * head...  23.1 us
    all_to_all x1, blocking collectives, shards(): lax.all_to_all(jnp.concatenate([q_send, kv_send], axis=2), 'sa', split_ax...  21.9 us
    dot_general x2, matrix products, shards(): projected = jnp.dot(flat_rows, w_in[0], preferred_element_type=jnp.float32)  21 us
    dot_general x2, matrix products, shards(): jnp.dot(hidden, w_down[0], preferred_element_type=jnp.float32)  15.7 us
  transfers between devices with their start and end apart: 8, of which 7 were waited for; matrix products, arithmetic and copies ran while one was open for 22% of the time, Pallas kernels for 5%

profile of v8, /device:TPU:7, one launch (start us, length us, event | category | flops | bytes accessed | tf_op | source)
XLA Modules:
  0.0 422.4 jit_solution(14744336034959737648)
XLA Ops:
  6.5 1.6 copy-done
  8.1 1.1 constant_dynamic-slice_fusion
  9.2 1.0 copy.63
  10.4 0.6 gather_fusion
  11.7 21.9 %all_to_all.30 = bf16[4,128,1280]{2,1,0:T(8,128)(2,1)S(1)} all-to-all(bf16[4,128,1280]{2,1,0:T(8,128)(2,1)S(1)} %pad_maximum_fusion), channel_id=1, replica_groups=mesh['grp'=8,'sa'=4,'sb'=4] {'sa'}, dimensions={0} | all-to-all | bytes 2621440 | tf_op jit(solution)/shard_map/all_to_all | solution.py:94
  33.6 1.2 broadcast_in_dim.26
  34.8 4.3 %all-to-all-start.1 = ((bf16[4,4,128,256]{3,2,1,0:T(8,128)(2,1)}), bf16[4,4,128,256]{3,2,1,0:T(8,128)(2,1)}, u32[]{:S(2)}, u32[]{:S(2)}) async-start(bf16[4,4,128,256]{3,2,1,0:T(8,128)(2,1)} %broadcast_in_dim.26), calls=%async_computation.1 | async-start | bytes 2097152 | tf_op jit(solution)/shard_map/all_to_all | solution.py:99
  39.2 1.3 slice.66
  40.5 24.8 %all-to-all-done.1 = bf16[4,4,128,256]{3,2,1,0:T(8,128)(2,1)} async-done(((bf16[4,4,128,256]{3,2,1,0:T(8,128)(2,1)}), bf16[4,4,128,256]{3,2,1,0:T(8,128)(2,1)}, u32[]{:S(2)}, u32[]{:S(2)}) %all-to-all-start.1) | async-done | bytes 1048608 | tf_op jit(solution)/shard_map/all_to_all | solution.py:99
  65.3 1.3 copy.67
  66.6 23.1 %shard_map.91 = bf16[512,1024]{1,0:T(8,128)(2,1)S(1)} custom-call(s32[2]{0:T(128)S(1)} %pad_add_fusion.meta_ref, bf16[512,1024]{1,0:T(8,128)(2,1)S(1)} %bitcast.42, bf16[2048,256]{1,0:T(8,128)(2,1)S(1)} %bitcast.40, bf16[2048,256]{1,0:T(8,128)(2,1)S(1)} %bitcast.41), custom_call_target="tpu_custom_call" | custom-call | tf_op jit(solution)/shard_map/pallas_call | solution.py:44
  89.8 3.0 collective-permute-start
  92.9 1.0 broadcast_in_dim.27
  93.9 1.1 copy-done.6
  95.0 0.6 constant_dynamic-update-slice_fusion.1
  95.7 4.3 %collective-permute-done = bf16[1024,2048]{1,0:T(8,128)(2,1)} collective-permute-done((bf16[1024,2048]{1,0:T(8,128)(2,1)}, bf16[1024,2048]{1,0:T(8,128)(2,1)}, u32[]{:S(2)}, u32[]{:S(2)}) %collective-permute-start) | collective-permute-done | bytes 4194336 | tf_op jit(solution)/shard_map/ppermute | solution.py:108
  100.0 2.8 constant_dynamic-update-slice_fusion
  102.8 1.3 convolution_convert_fusion.5
  104.0 1.3 convolution_convert_fusion.4
  105.3 1.3 convolution_convert_fusion.3
  106.6 3.7 add_convert_fusion
  110.3 0.7 copy-done.9
  112.1 42.4 %reduce-scatter.2.cloned.1.call-done = bf16[128,4096]{1,0:T(8,128)(2,1)} async-done(((bf16[512,4096]{1,0:T(8,128)(2,1)}), bf16[128,4096]{1,0:T(8,128)(2,1)}) %reduce-scatter.2.cloned.1.call-update) | async-done | bytes 1048592 | tf_op jit(solution)/shard_map/reduce_scatter | solution.py:120
  154.6 1.6 multiply_reduce_fusion.1
  156.2 4.5 %convolution_convert_fusion.1 = bf16[512,4096]{1,0:T(8,128)(2,1)} fusion(pred[128,1024]{1,0:T(8,128)(4,1)S(1)} %fusion.21, bf16[128,4096]{1,0:T(8,128)(2,1)} %reduce-scatter.2.cloned.1.call-done, bf16[128,4096]{1,0:T(8,128)(2,1)S(1)} %copy-done.2, f32[4096]{0:T(1024)S(1)} %convert_element_type.94, f32[128]{0:T(128)S(1)} %add_rsqrt_fusion), kind=kOutput, calls=%fused_computation.16 | convolution fusion | flops 542113792 | bytes 6373888 | tf_op jit(solution)/shard_map/dot_general | solution.py:152
  160.8 7.2 %reshape.176 = bf16[128,4,4096]{2,1,0:T(4,128)(2,1)} reshape(bf16[512,4096]{1,0:T(8,128)(2,1)} %convolution_convert_fusion.1) | data formatting | bytes 8388608 | tf_op jit(solution)/shard_map/reshape | solution.py:155
  168.0 8.5 %all-to-all-start.2 = ((bf16[128,4,4096]{2,1,0:T(4,128)(2,1)}), bf16[128,4,4096]{2,1,0:T(4,128)(2,1)}, u32[]{:S(2)}, u32[]{:S(2)}) async-start(bf16[128,4,4096]{2,1,0:T(4,128)(2,1)} %reshape.176), calls=%async_computation.3 | async-start | bytes 8388608 | tf_op jit(solution)/shard_map/all_to_all | solution.py:156
  176.6 3.3 convolution_convert_fusion
  179.8 7.2 %reshape.180 = bf16[128,4,4096]{2,1,0:T(4,128)(2,1)} reshape(bf16[512,4096]{1,0:T(8,128)(2,1)} %convolution_convert_fusion) | data formatting | bytes 8388608 | tf_op jit(solution)/shard_map/reshape | solution.py:155
  187.0 40.9 %all-to-all-done.2 = bf16[128,4,4096]{2,1,0:T(4,128)(2,1)} async-done(((bf16[128,4,4096]{2,1,0:T(4,128)(2,1)}), bf16[128,4,4096]{2,1,0:T(4,128)(2,1)}, u32[]{:S(2)}, u32[]{:S(2)}) %all-to-all-start.2) | async-done | bytes 4194336 | tf_op jit(solution)/shard_map/all_to_all | solution.py:156
  227.9 6.0 %all-to-all-start.4 = ((bf16[128,4,4096]{2,1,0:T(4,128)(2,1)}), bf16[128,4,4096]{2,1,0:T(4,128)(2,1)}, u32[]{:S(2)}, u32[]{:S(2)}) async-start(bf16[128,4,4096]{2,1,0:T(4,128)(2,1)} %reshape.180), calls=%async_computation.5 | async-start | bytes 8388608 | tf_op jit(solution)/shard_map/all_to_all | solution.py:156
  233.9 6.9 %reshape.177 = bf16[512,4096]{1,0:T(8,128)(2,1)} reshape(bf16[128,4,4096]{2,1,0:T(4,128)(2,1)} %all-to-all-done.2) | data formatting | bytes 8388608 | tf_op jit(solution)/shard_map/reshape | solution.py:159
  240.9 10.5 %fusion.2 = f32[512,1536]{1,0:T(8,128)S(1)} fusion(bf16[512,4096]{1,0:T(8,128)(2,1)} %reshape.177, bf16[1,4096,1536]{2,1,0:T(8,128)(2,1)} %param.14), kind=kOutput, calls=%fused_computation.3 | convolution fusion | flops 6442450944 | bytes 19922944 | tf_op jit(solution)/shard_map/dot_general | solution.py:160
  251.4 7.8 %fusion.11 = bf16[512,4096]{1,0:T(8,128)(2,1)} fusion(bf16[1,768,4096]{2,1,0:T(8,128)(2,1)} %param.15, f32[512,1536]{1,0:T(8,128)S(1)} %fusion.2), kind=kOutput, calls=%fused_computation.17 | convolution fusion | flops 3225681920 | bytes 13631488 | tf_op jit(solution)/shard_map/dot_general | solution.py:164
  259.2 7.2 %reshape.178 = bf16[128,4,4096]{2,1,0:T(4,128)(2,1)} reshape(bf16[512,4096]{1,0:T(8,128)(2,1)} %fusion.11) | data formatting | bytes 8388608 | tf_op jit(solution)/shard_map/reshape | solution.py:169
  266.4 19.0 %all-to-all-done.4 = bf16[128,4,4096]{2,1,0:T(4,128)(2,1)} async-done(((bf16[128,4,4096]{2,1,0:T(4,128)(2,1)}), bf16[128,4,4096]{2,1,0:T(4,128)(2,1)}, u32[]{:S(2)}, u32[]{:S(2)}) %all-to-all-start.4) | async-done | bytes 4194336 | tf_op jit(solution)/shard_map/all_to_all | solution.py:156
  285.4 5.8 %all-to-all-start.3 = ((bf16[128,4,4096]{2,1,0:T(4,128)(2,1)}), bf16[128,4,4096]{2,1,0:T(4,128)(2,1)}, u32[]{:S(2)}, u32[]{:S(2)}) async-start(bf16[128,4,4096]{2,1,0:T(4,128)(2,1)} %reshape.178), calls=%async_computation.4 | async-start | bytes 8388608 | tf_op jit(solution)/shard_map/all_to_all | solution.py:168
  291.2 6.9 %reshape.181 = bf16[512,4096]{1,0:T(8,128)(2,1)} reshape(bf16[128,4,4096]{2,1,0:T(4,128)(2,1)} %all-to-all-done.4) | data formatting | bytes 8388608 | tf_op jit(solution)/shard_map/reshape | solution.py:159
  298.1 10.5 %fusion = f32[512,1536]{1,0:T(8,128)S(1)} fusion(bf16[512,4096]{1,0:T(8,128)(2,1)} %reshape.181, bf16[1,4096,1536]{2,1,0:T(8,128)(2,1)} %param.14), kind=kOutput, calls=%fused_computation.1 | convolution fusion | flops 6442450944 | bytes 19922944 | tf_op jit(solution)/shard_map/dot_general | solution.py:160
  308.6 7.8 %fusion.14 = bf16[512,4096]{1,0:T(8,128)(2,1)} fusion(bf16[1,768,4096]{2,1,0:T(8,128)(2,1)} %param.15, f32[512,1536]{1,0:T(8,128)S(1)} %fusion), kind=kOutput, calls=%fused_computation.18 | convolution fusion | flops 3225681920 | bytes 13631488 | tf_op jit(solution)/shard_map/dot_general | solution.py:164
  316.4 7.2 %reshape.182 = bf16[128,4,4096]{2,1,0:T(4,128)(2,1)} reshape(bf16[512,4096]{1,0:T(8,128)(2,1)} %fusion.14) | data formatting | bytes 8388608 | tf_op jit(solution)/shard_map/reshape | solution.py:169
  323.7 18.9 %all-to-all-done.3 = bf16[128,4,4096]{2,1,0:T(4,128)(2,1)} async-done(((bf16[128,4,4096]{2,1,0:T(4,128)(2,1)}), bf16[128,4,4096]{2,1,0:T(4,128)(2,1)}, u32[]{:S(2)}, u32[]{:S(2)}) %all-to-all-start.3) | async-done | bytes 4194336 | tf_op jit(solution)/shard_map/all_to_all | solution.py:168
  342.6 5.8 %all-to-all-start.5 = ((bf16[128,4,4096]{2,1,0:T(4,128)(2,1)}), bf16[128,4,4096]{2,1,0:T(4,128)(2,1)}, u32[]{:S(2)}, u32[]{:S(2)}) async-start(bf16[128,4,4096]{2,1,0:T(4,128)(2,1)} %reshape.182), calls=%async_computation.6 | async-start | bytes 8388608 | tf_op jit(solution)/shard_map/all_to_all | solution.py:168
  348.4 6.9 %reshape.179 = bf16[512,4096]{1,0:T(8,128)(2,1)} reshape(bf16[128,4,4096]{2,1,0:T(4,128)(2,1)} %all-to-all-done.3) | data formatting | bytes 8388608 | tf_op jit(solution)/shard_map/reshape | solution.py:171
  355.4 44.5 %all-to-all-done.5 = bf16[128,4,4096]{2,1,0:T(4,128)(2,1)} async-done(((bf16[128,4,4096]{2,1,0:T(4,128)(2,1)}), bf16[128,4,4096]{2,1,0:T(4,128)(2,1)}, u32[]{:S(2)}, u32[]{:S(2)}) %all-to-all-start.5) | async-done | bytes 4194336 | tf_op jit(solution)/shard_map/all_to_all | solution.py:168
  399.9 6.9 %reshape.183 = bf16[512,4096]{1,0:T(8,128)(2,1)} reshape(bf16[128,4,4096]{2,1,0:T(4,128)(2,1)} %all-to-all-done.5) | data formatting | bytes 8388608 | tf_op jit(solution)/shard_map/reshape | solution.py:171
  406.8 7.4 %multiply_reduce_fusion = f32[128,4096]{1,0:T(8,128)S(1)} fusion(bf16[512,4096]{1,0:T(8,128)(2,1)} %reshape.183, bf16[512,4096]{1,0:T(8,128)(2,1)} %reshape.179, f32[4,128]{1,0:T(4,128)S(1)} %bitcast.48, s32[4,128]{1,0:T(4,128)S(1)} %bitcast.47), kind=kOutput, calls=%fused_computation.9 | convolution fusion | flops 4315938816 | bytes 10489856 | tf_op jit(solution)/shard_map/dot_general | solution.py:175
  414.2 1.4 add_convert_fusion.1
  (45 shorter events, 2.1 us)
Async XLA Ops:
  6.5 1.6 copy-start
  6.5 5.0 %copy-start.7 = (bf16[128,4096]{1,0:T(8,128)(2,1)S(1)}, bf16[128,4096]{1,0:T(8,128)(2,1)}, u32[]{:S(2)}) copy-start(bf16[128,4096]{1,0:T(8,128)(2,1)} %param.9) | copy-start | bytes 3145732
  6.5 83.3 %all-gather.2.cloned.1.call-start = ((), (), s32[]{:S(2)}) async-start(), calls=%async_computation.7 | async-start | bytes 5242880 | tf_op jit(solution)/shard_map/all_gather | solution.py:86
  33.6 5.5 %copy-start.5 = (bf16[4,128,1280]{2,1,0:T(8,128)(2,1)}, bf16[4,128,1280]{2,1,0:T(8,128)(2,1)S(1)}, u32[]{:S(2)}) copy-start(bf16[4,128,1280]{2,1,0:T(8,128)(2,1)S(1)} %all_to_all.30) | copy-start | bytes 3932164
  34.8 30.5 %all-to-all-start.1 = ((bf16[4,4,128,256]{3,2,1,0:T(8,128)(2,1)}), bf16[4,4,128,256]{3,2,1,0:T(8,128)(2,1)}, u32[]{:S(2)}, u32[]{:S(2)}) async-start(bf16[4,4,128,256]{3,2,1,0:T(8,128)(2,1)} %broadcast_in_dim.26), calls=%async_computation.1 | async-start | bytes 2097152 | tf_op jit(solution)/shard_map/all_to_all | solution.py:99
  39.0 115.6 %reduce-scatter.2.cloned.1.call-start = ((), (), s32[]{:S(2)}) async-start(), calls=%async_computation.8 | async-start | bytes 5242880 | tf_op jit(solution)/shard_map/reduce_scatter | solution.py:120
  89.8 10.2 %collective-permute-start = (bf16[1024,2048]{1,0:T(8,128)(2,1)}, bf16[1024,2048]{1,0:T(8,128)(2,1)}, u32[]{:S(2)}, u32[]{:S(2)}) collective-permute-start(bf16[1024,2048]{1,0:T(8,128)(2,1)} %all-gather.2.cloned.1.call-done), channel_id=1, source_target_pairs={{0,16},{16,0},{32,48},{48,32},{64,80},{80,64},{96,112},{112,96},{1... | collective-permute-start | bytes 12582920 | tf_op jit(solution)/shard_map/ppermute | solution.py:108
  92.9 2.2 copy-start.6
  110.3 0.7 copy-start.9
  110.3 1.4 copy-start.8
  110.3 44.3 %copy-start.2 = (bf16[128,4096]{1,0:T(8,128)(2,1)S(1)}, bf16[128,4096]{1,0:T(8,128)(2,1)}, u32[]{:S(2)}) copy-start(bf16[128,4096]{1,0:T(8,128)(2,1)} %param.11) | copy-start | bytes 3145732
  168.0 8.5 %copy-start.3 = (bf16[128,4096]{1,0:T(8,128)(2,1)S(1)}, bf16[128,4096]{1,0:T(8,128)(2,1)}, u32[]{:S(2)}) copy-start(bf16[128,4096]{1,0:T(8,128)(2,1)} %reduce-scatter.2.cloned.1.call-done) | copy-start | bytes 3145732
  168.0 59.9 %all-to-all-start.2 = ((bf16[128,4,4096]{2,1,0:T(4,128)(2,1)}), bf16[128,4,4096]{2,1,0:T(4,128)(2,1)}, u32[]{:S(2)}, u32[]{:S(2)}) async-start(bf16[128,4,4096]{2,1,0:T(4,128)(2,1)} %reshape.176), calls=%async_computation.3 | async-start | bytes 8388608 | tf_op jit(solution)/shard_map/all_to_all | solution.py:156
  227.9 57.5 %all-to-all-start.4 = ((bf16[128,4,4096]{2,1,0:T(4,128)(2,1)}), bf16[128,4,4096]{2,1,0:T(4,128)(2,1)}, u32[]{:S(2)}, u32[]{:S(2)}) async-start(bf16[128,4,4096]{2,1,0:T(4,128)(2,1)} %reshape.180), calls=%async_computation.5 | async-start | bytes 8388608 | tf_op jit(solution)/shard_map/all_to_all | solution.py:156
  285.4 57.3 %all-to-all-start.3 = ((bf16[128,4,4096]{2,1,0:T(4,128)(2,1)}), bf16[128,4,4096]{2,1,0:T(4,128)(2,1)}, u32[]{:S(2)}, u32[]{:S(2)}) async-start(bf16[128,4,4096]{2,1,0:T(4,128)(2,1)} %reshape.178), calls=%async_computation.4 | async-start | bytes 8388608 | tf_op jit(solution)/shard_map/all_to_all | solution.py:168
  342.6 57.3 %all-to-all-start.5 = ((bf16[128,4,4096]{2,1,0:T(4,128)(2,1)}), bf16[128,4,4096]{2,1,0:T(4,128)(2,1)}, u32[]{:S(2)}, u32[]{:S(2)}) async-start(bf16[128,4,4096]{2,1,0:T(4,128)(2,1)} %reshape.182), calls=%async_computation.6 | async-start | bytes 8388608 | tf_op jit(solution)/shard_map/all_to_all | solution.py:168
  355.4 51.4 %copy-start.10 = (f32[128,4]{0,1:T(4,128)S(1)}, f32[128,4]{0,1:T(4,128)}, u32[]{:S(2)}) copy-start(f32[128,4]{0,1:T(4,128)} %param.17) | copy-start | bytes 6148
  406.8 7.4 %copy-start.4 = (bf16[128,4096]{1,0:T(8,128)(2,1)S(1)}, bf16[128,4096]{1,0:T(8,128)(2,1)}, u32[]{:S(2)}) copy-start(bf16[128,4096]{1,0:T(8,128)(2,1)} %reduce-scatter.2.cloned.1.call-done) | copy-start | bytes 3145732
  406.8 8.7 %copy-start.1 = (bf16[256,4096]{1,0:T(8,128)(2,1)S(1)}, bf16[256,4096]{1,0:T(8,128)(2,1)}, u32[]{:S(2)}) copy-start(bf16[256,4096]{1,0:T(8,128)(2,1)} %param.13) | copy-start | bytes 6291460
Sparse Core Ops, SparseCore 0:
  9.4 61.5 all-gather.1
  110.5 44.0 reduce-scatter.1

commit v9 on v7

--- a/solution.py
+++ b/solution.py
@@ -143,28 +143,41 @@
     slot_index = flat_ids * capacity + rank
     picks = slot_index[:, None] == jnp.arange(slots, dtype=jnp.int32)[None, :]
     token_slots = jnp.any(picks.reshape(tok_dev, top_count, slots), axis=1).astype(jnp.bfloat16)
-    outgoing_rows = lax.dot_general(
-        token_slots, normed, (((0,), (0,)), ((), ())), preferred_element_type=jnp.float32
-    ).astype(jnp.bfloat16)
-    outgoing_rows = outgoing_rows.reshape(devices, capacity, width)
     ffe_width = w_down.shape[1]
-    arrived = lax.all_to_all(outgoing_rows, ("grp", "sa", "sb"), split_axis=0, concat_axis=0, tiled=True)
-    flat_rows = arrived.reshape(-1, width)
-    projected = jnp.dot(flat_rows, w_in[0], preferred_element_type=jnp.float32)
+    halves = 2
+    part = width // halves
+    projected = None
+    for h in range(halves):
+        outgoing_rows = lax.dot_general(
+            token_slots, normed[:, h * part : (h + 1) * part], (((0,), (0,)), ((), ())),
+            preferred_element_type=jnp.float32,
+        ).astype(jnp.bfloat16).reshape(devices, capacity, part)
+        arrived = lax.all_to_all(
+            outgoing_rows, ("grp", "sa", "sb"), split_axis=0, concat_axis=0, tiled=True
+        )
+        term = jnp.dot(
+            arrived.reshape(-1, part), w_in[0, h * part : (h + 1) * part],
+            preferred_element_type=jnp.float32,
+        )
+        projected = term if projected is None else projected + term
     hidden = (jax.nn.silu(projected[:, :ffe_width]) * projected[:, ffe_width:]).astype(jnp.bfloat16)
-    produced = jnp.dot(hidden, w_down[0], preferred_element_type=jnp.float32).astype(jnp.bfloat16)
-    returned = lax.all_to_all(
-        produced.reshape(arrived.shape), ("grp", "sa", "sb"), split_axis=0, concat_axis=0, tiled=True
-    )
-    returned = returned.reshape(slots, width)
     picks_by_choice = picks.reshape(tok_dev, top_count, slots).transpose(1, 0, 2)
-    picked = jnp.dot(
-        picks_by_choice.reshape(n_flat, slots).astype(jnp.bfloat16),
-        returned,
-        preferred_element_type=jnp.float32,
-    ).reshape(top_count, tok_dev, width)
+    picks_by_choice = picks_by_choice.reshape(n_flat, slots).astype(jnp.bfloat16)
     weights_by_choice = route_weights.T.reshape(top_count, tok_dev, 1)
-    combined = jnp.sum(picked * weights_by_choice, axis=0)
+    combined = []
+    for h in range(halves):
+        produced = jnp.dot(
+            hidden, w_down[0, :, h * part : (h + 1) * part], preferred_element_type=jnp.float32
+        ).astype(jnp.bfloat16)
+        returned = lax.all_to_all(
+            produced.reshape(devices, capacity, part), ("grp", "sa", "sb"), split_axis=0,
+            concat_axis=0, tiled=True,
+        ).reshape(slots, part)
+        picked = jnp.dot(
+            picks_by_choice, returned, preferred_element_type=jnp.float32
+        ).reshape(top_count, tok_dev, part)
+        combined.append(jnp.sum(picked * weights_by_choice, axis=0))
+    combined = jnp.concatenate(combined, axis=1)
     return (mixed + combined).astype(jnp.bfloat16)
 
 

time: 410 us -> 426 us (1.039)
  blocking collectives: 231 us -> 21.9 us
  waiting for transfers between devices: 71.6 us -> 250 us
  starting transfers between devices: 7.37 us -> 33.4 us
  matrix products: 43.6 us -> 61.3 us
    all_to_all x2 -> x0, blocking collectives: 209 us -> none  [the longest x1 106 us: shards(): lax.all_to_all(outgoing_rows, ('grp', 'sa', 'sb'), split_axis=0, concat_a...]
    all_to_all x0 -> x4, waiting for transfers between devices: none -> 178 us  [the longest x2 90.3 us: shards(): lax.all_to_all(produced.reshape(devices, capacity, part), ('grp', 'sa', '...]
    all_to_all x0 -> x4, starting transfers between devices: none -> 26.1 us  [the longest x2 14.4 us: shards(): lax.all_to_all(outgoing_rows, ('grp', 'sa', 'sb'), split_axis=0, concat_a...]
    dot_general x4 -> x8, matrix products: 35.8 us -> 53.4 us  [the longest x2 22.7 us: shards(): jnp.dot(arrived.reshape(-1, part), w_in[0, h * part:(h + 1) * part], pref...]
  transfers between devices with their start and end apart: 4 -> 8, of which waited for: 3 -> 7; matrix products, arithmetic and copies ran while one was open for 2% -> 9% of each run, Pallas kernels for 6% -> 5%
where the time goes in v9:
time: 426 us; the launch traced here: 425 us
  waiting for transfers between devices  250 us (59%)
  matrix products  61.3 us (14%)
  starting transfers between devices  33.4 us (8%)
  Pallas kernels  23.1 us (5%)
  blocking collectives  21.9 us (5%)
  local copies, waits for them, and re-layouts  15.3 us (4%)
  between operations  13.7 us (3%)
  other arithmetic  6.32 us (1%)
    all_to_all x2, waiting for transfers between devices, shards(): lax.all_to_all(produced.reshape(devices, capacity, part), ('grp', 'sa', '...  90.3 us
    all_to_all x2, waiting for transfers between devices, shards(): lax.all_to_all(outgoing_rows, ('grp', 'sa', 'sb'), split_axis=0, concat_a...  87.6 us
    reduce_scatter x1, waiting for transfers between devices, shards(): lax.psum_scatter(partial_sum.astype(jnp.bfloat16), 'sa', scatter_dimensio...  42.4 us
    all_to_all x1, waiting for transfers between devices, shards(): lax.all_to_all(jnp.broadcast_to(kv_col[None], (n_sb,) + kv_col.shape), 's...  24.8 us
    pallas_call x1, Pallas kernels, attention(): pl.pallas_call(kernel, out_shape=jax.ShapeDtypeStruct((rows, heads * head...  23.1 us
    dot_general x2, matrix products, shards(): jnp.dot(arrived.reshape(-1, part), w_in[0, h * part:(h + 1) * part], pref...  22.7 us
    all_to_all x1, blocking collectives, shards(): lax.all_to_all(jnp.concatenate([q_send, kv_send], axis=2), 'sa', split_ax...  21.9 us
    all_to_all x2, starting transfers between devices, shards(): lax.all_to_all(outgoing_rows, ('grp', 'sa', 'sb'), split_axis=0, concat_a...  14.4 us
  transfers between devices with their start and end apart: 8, of which 7 were waited for; matrix products, arithmetic and copies ran while one was open for 9% of the time, Pallas kernels for 5%

profile of v9, /device:TPU:7, one launch (start us, length us, event | category | flops | bytes accessed | tf_op | source)
XLA Modules:
  0.0 424.6 jit_solution(14832065590847541323)
XLA Ops:
  6.5 1.6 copy-done
  8.1 1.1 constant_dynamic-slice_fusion
  9.2 1.0 copy.49
  10.3 0.1 copy.50
  10.4 0.6 gather_fusion
  11.2 0.2 copy.51
  11.3 0.1 copy.52
  11.7 21.9 %all_to_all.30 = bf16[4,128,1280]{2,1,0:T(8,128)(2,1)S(1)} all-to-all(bf16[4,128,1280]{2,1,0:T(8,128)(2,1)S(1)} %pad_maximum_fusion), channel_id=1, replica_groups=mesh['grp'=8,'sa'=4,'sb'=4] {'sa'}, dimensions={0} | all-to-all | bytes 2621440 | tf_op jit(solution)/shard_map/all_to_all | solution.py:94
  33.6 1.2 broadcast_in_dim.26
  34.8 4.3 %all-to-all-start.1 = ((bf16[4,4,128,256]{3,2,1,0:T(8,128)(2,1)}), bf16[4,4,128,256]{3,2,1,0:T(8,128)(2,1)}, u32[]{:S(2)}, u32[]{:S(2)}) async-start(bf16[4,4,128,256]{3,2,1,0:T(8,128)(2,1)} %broadcast_in_dim.26), calls=%async_computation.1 | async-start | bytes 2097152 | tf_op jit(solution)/shard_map/all_to_all | solution.py:99
  39.2 1.3 slice.74
  40.5 24.8 %all-to-all-done.1 = bf16[4,4,128,256]{3,2,1,0:T(8,128)(2,1)} async-done(((bf16[4,4,128,256]{3,2,1,0:T(8,128)(2,1)}), bf16[4,4,128,256]{3,2,1,0:T(8,128)(2,1)}, u32[]{:S(2)}, u32[]{:S(2)}) %all-to-all-start.1) | async-done | bytes 1048608 | tf_op jit(solution)/shard_map/all_to_all | solution.py:99
  65.3 1.3 copy.53
  66.6 23.1 %shard_map.91 = bf16[512,1024]{1,0:T(8,128)(2,1)S(1)} custom-call(s32[2]{0:T(128)S(1)} %pad_add_fusion.meta_ref, bf16[512,1024]{1,0:T(8,128)(2,1)S(1)} %bitcast.67, bf16[2048,256]{1,0:T(8,128)(2,1)S(1)} %bitcast.65, bf16[2048,256]{1,0:T(8,128)(2,1)S(1)} %bitcast.66), custom_call_target="tpu_custom_call" | custom-call | tf_op jit(solution)/shard_map/pallas_call | solution.py:44
  89.8 3.1 collective-permute-start
  92.9 1.0 broadcast_in_dim.27
  93.9 1.1 copy-done.5
  95.0 0.6 constant_dynamic-update-slice_fusion.1
  95.7 4.3 %collective-permute-done = bf16[1024,2048]{1,0:T(8,128)(2,1)} collective-permute-done((bf16[1024,2048]{1,0:T(8,128)(2,1)}, bf16[1024,2048]{1,0:T(8,128)(2,1)}, u32[]{:S(2)}, u32[]{:S(2)}) %collective-permute-start) | collective-permute-done | bytes 4194336 | tf_op jit(solution)/shard_map/ppermute | solution.py:108
  100.0 2.8 constant_dynamic-update-slice_fusion
  102.8 1.3 convolution_convert_fusion.3
  104.0 1.3 convolution_convert_fusion.2
  105.3 1.3 convolution_convert_fusion.1
  106.6 3.8 add_convert_fusion
  110.4 0.7 copy-done.8
  111.3 0.3 fusion.30
  111.8 0.4 fusion.29
  112.2 42.4 %reduce-scatter.2.cloned.1.call-done = bf16[128,4096]{1,0:T(8,128)(2,1)} async-done(((bf16[512,4096]{1,0:T(8,128)(2,1)}), bf16[128,4096]{1,0:T(8,128)(2,1)}) %reduce-scatter.2.cloned.1.call-update) | async-done | bytes 1048592 | tf_op jit(solution)/shard_map/reduce_scatter | solution.py:120
  154.6 1.6 multiply_reduce_fusion.2
  156.3 1.6 multiply_convert_fusion
  157.9 3.2 convert_bitcast_fusion.2
  161.2 8.5 %all-to-all-start.3 = ((bf16[128,8,2048]{2,1,0:T(8,128)(2,1)}), bf16[128,8,2048]{2,1,0:T(8,128)(2,1)}, u32[]{:S(2)}, u32[]{:S(2)}) async-start(bf16[128,8,2048]{2,1,0:T(8,128)(2,1)} %convert_bitcast_fusion.2), calls=%async_computation.4 | async-start | bytes 8388608 | tf_op jit(solution)/shard_map/all_to_all | solution.py:155
  169.7 3.4 convert_bitcast_fusion.3
  173.1 48.0 %all-to-all-done.3 = bf16[128,8,2048]{2,1,0:T(8,128)(2,1)} async-done(((bf16[128,8,2048]{2,1,0:T(8,128)(2,1)}), bf16[128,8,2048]{2,1,0:T(8,128)(2,1)}, u32[]{:S(2)}, u32[]{:S(2)}) %all-to-all-start.3) | async-done | bytes 4194336 | tf_op jit(solution)/shard_map/all_to_all | solution.py:155
  221.1 5.8 %all-to-all-start.2 = ((bf16[128,8,2048]{2,1,0:T(8,128)(2,1)}), bf16[128,8,2048]{2,1,0:T(8,128)(2,1)}, u32[]{:S(2)}, u32[]{:S(2)}) async-start(bf16[128,8,2048]{2,1,0:T(8,128)(2,1)} %convert_bitcast_fusion.3), calls=%async_computation.3 | async-start | bytes 8388608 | tf_op jit(solution)/shard_map/all_to_all | solution.py:155
  226.9 11.8 %fusion = f32[1024,1536]{1,0:T(8,128)} fusion(bf16[1,4096,1536]{2,1,0:T(8,128)(2,1)} %param.14, bf16[128,8,2048]{2,1,0:T(8,128)(2,1)} %all-to-all-done.3), kind=kOutput, calls=%fused_computation.2 | convolution fusion | flops 6442450944 | bytes 16777216 | tf_op jit(solution)/shard_map/dot_general | solution.py:158
  238.7 39.6 %all-to-all-done.2 = bf16[128,8,2048]{2,1,0:T(8,128)(2,1)} async-done(((bf16[128,8,2048]{2,1,0:T(8,128)(2,1)}), bf16[128,8,2048]{2,1,0:T(8,128)(2,1)}, u32[]{:S(2)}, u32[]{:S(2)}) %all-to-all-start.2) | async-done | bytes 4194336 | tf_op jit(solution)/shard_map/all_to_all | solution.py:155
  278.3 10.9 %fusion.6 = f32[1024,1536]{1,0:T(8,128)S(1)} fusion(f32[1024,1536]{1,0:T(8,128)} %fusion, bf16[1,4096,1536]{2,1,0:T(8,128)(2,1)} %param.14, bf16[128,8,2048]{2,1,0:T(8,128)(2,1)} %all-to-all-done.2), kind=kOutput, calls=%fused_computation.12 | convolution fusion | flops 6444023808 | bytes 23068672 | tf_op jit(solution)/shard_map/dot_general | solution.py:158
  289.2 1.0 fusion.19
  290.2 6.9 %convert_bitcast_fusion.1 = bf16[128,8,2048]{2,1,0:T(8,128)(2,1)} fusion(bf16[1024,768]{1,0:T(8,128)(2,1)S(1)} %fusion.19, bf16[1,768,4096]{2,1,0:T(8,128)(2,1)} %param.15), kind=kOutput, calls=%fused_computation.22 | convolution fusion | flops 3223322624 | bytes 8912896 | tf_op jit(solution)/shard_map/dot_general | solution.py:169
  297.1 5.8 %all-to-all-start.4 = ((bf16[128,8,2048]{2,1,0:T(8,128)(2,1)}), bf16[128,8,2048]{2,1,0:T(8,128)(2,1)}, u32[]{:S(2)}, u32[]{:S(2)}) async-start(bf16[128,8,2048]{2,1,0:T(8,128)(2,1)} %convert_bitcast_fusion.1), calls=%async_computation.5 | async-start | bytes 8388608 | tf_op jit(solution)/shard_map/all_to_all | solution.py:172
  302.9 6.9 %convert_bitcast_fusion = bf16[128,8,2048]{2,1,0:T(8,128)(2,1)} fusion(bf16[1024,768]{1,0:T(8,128)(2,1)S(1)} %fusion.19, bf16[1,768,4096]{2,1,0:T(8,128)(2,1)} %param.15), kind=kOutput, calls=%fused_computation.20 | convolution fusion | flops 3223322624 | bytes 8912896 | tf_op jit(solution)/shard_map/dot_general | solution.py:169
  309.8 44.5 %all-to-all-done.4 = bf16[128,8,2048]{2,1,0:T(8,128)(2,1)} async-done(((bf16[128,8,2048]{2,1,0:T(8,128)(2,1)}), bf16[128,8,2048]{2,1,0:T(8,128)(2,1)}, u32[]{:S(2)}, u32[]{:S(2)}) %all-to-all-start.4) | async-done | bytes 4194336 | tf_op jit(solution)/shard_map/all_to_all | solution.py:172
  354.3 5.9 %all-to-all-start.5 = ((bf16[128,8,2048]{2,1,0:T(8,128)(2,1)}), bf16[128,8,2048]{2,1,0:T(8,128)(2,1)}, u32[]{:S(2)}, u32[]{:S(2)}) async-start(bf16[128,8,2048]{2,1,0:T(8,128)(2,1)} %convert_bitcast_fusion), calls=%async_computation.6 | async-start | bytes 8388608 | tf_op jit(solution)/shard_map/all_to_all | solution.py:172
  360.2 5.6 %multiply_reduce_fusion.1 = f32[128,2048]{1,0:T(8,128)} fusion(bf16[128,8,2048]{2,1,0:T(8,128)(2,1)} %all-to-all-done.4, f32[4,128]{1,0:T(4,128)S(1)} %bitcast.74, s32[4,128]{1,0:T(4,128)S(1)} %bitcast.72), kind=kOutput, calls=%fused_computation.21 | convolution fusion | flops 2149842944 | bytes 5246976 | tf_op jit(solution)/shard_map/dot_general | solution.py:176
  365.8 45.8 %all-to-all-done.5 = bf16[128,8,2048]{2,1,0:T(8,128)(2,1)} async-done(((bf16[128,8,2048]{2,1,0:T(8,128)(2,1)}), bf16[128,8,2048]{2,1,0:T(8,128)(2,1)}, u32[]{:S(2)}, u32[]{:S(2)}) %all-to-all-start.5) | async-done | bytes 4194336 | tf_op jit(solution)/shard_map/all_to_all | solution.py:172
  411.6 4.8 %multiply_reduce_fusion = f32[128,2048]{1,0:T(8,128)S(1)} fusion(bf16[128,8,2048]{2,1,0:T(8,128)(2,1)} %all-to-all-done.5, f32[4,128]{1,0:T(4,128)S(1)} %bitcast.75, s32[4,128]{1,0:T(4,128)S(1)} %bitcast.73), kind=kOutput, calls=%fused_computation.19 | convolution fusion | flops 2149842944 | bytes 5246976 | tf_op jit(solution)/shard_map/dot_general | solution.py:176
  416.4 1.4 fusion.28
  (40 shorter events, 0.9 us)
Async XLA Ops:
  6.5 1.6 copy-start
  6.5 5.0 %copy-start.7 = (bf16[128,4096]{1,0:T(8,128)(2,1)S(1)}, bf16[128,4096]{1,0:T(8,128)(2,1)}, u32[]{:S(2)}) copy-start(bf16[128,4096]{1,0:T(8,128)(2,1)} %param.9) | copy-start | bytes 3145732
  6.5 83.3 %all-gather.2.cloned.1.call-start = ((), (), s32[]{:S(2)}) async-start(), calls=%async_computation.7 | async-start | bytes 5242880 | tf_op jit(solution)/shard_map/all_gather | solution.py:86
  33.6 5.5 %copy-start.4 = (bf16[4,128,1280]{2,1,0:T(8,128)(2,1)}, bf16[4,128,1280]{2,1,0:T(8,128)(2,1)S(1)}, u32[]{:S(2)}) copy-start(bf16[4,128,1280]{2,1,0:T(8,128)(2,1)S(1)} %all_to_all.30) | copy-start | bytes 3932164
  34.8 30.5 %all-to-all-start.1 = ((bf16[4,4,128,256]{3,2,1,0:T(8,128)(2,1)}), bf16[4,4,128,256]{3,2,1,0:T(8,128)(2,1)}, u32[]{:S(2)}, u32[]{:S(2)}) async-start(bf16[4,4,128,256]{3,2,1,0:T(8,128)(2,1)} %broadcast_in_dim.26), calls=%async_computation.1 | async-start | bytes 2097152 | tf_op jit(solution)/shard_map/all_to_all | solution.py:99
  39.0 115.6 %reduce-scatter.2.cloned.1.call-start = ((), (), s32[]{:S(2)}) async-start(), calls=%async_computation.8 | async-start | bytes 5242880 | tf_op jit(solution)/shard_map/reduce_scatter | solution.py:120
  89.8 10.2 %collective-permute-start = (bf16[1024,2048]{1,0:T(8,128)(2,1)}, bf16[1024,2048]{1,0:T(8,128)(2,1)}, u32[]{:S(2)}, u32[]{:S(2)}) collective-permute-start(bf16[1024,2048]{1,0:T(8,128)(2,1)} %all-gather.2.cloned.1.call-done), channel_id=1, source_target_pairs={{0,16},{16,0},{32,48},{48,32},{64,80},{80,64},{96,112},{112,96},{1... | collective-permute-start | bytes 12582920 | tf_op jit(solution)/shard_map/ppermute | solution.py:108
  92.9 2.2 copy-start.5
  110.4 0.7 copy-start.8
  110.4 0.7 copy-start.9
  110.4 44.3 %copy-start.2 = (bf16[128,4096]{1,0:T(8,128)(2,1)S(1)}, bf16[128,4096]{1,0:T(8,128)(2,1)}, u32[]{:S(2)}) copy-start(bf16[128,4096]{1,0:T(8,128)(2,1)} %param.11) | copy-start | bytes 3145732
  161.2 59.9 %all-to-all-start.3 = ((bf16[128,8,2048]{2,1,0:T(8,128)(2,1)}), bf16[128,8,2048]{2,1,0:T(8,128)(2,1)}, u32[]{:S(2)}, u32[]{:S(2)}) async-start(bf16[128,8,2048]{2,1,0:T(8,128)(2,1)} %convert_bitcast_fusion.2), calls=%async_computation.4 | async-start | bytes 8388608 | tf_op jit(solution)/shard_map/all_to_all | solution.py:155
  221.1 57.3 %all-to-all-start.2 = ((bf16[128,8,2048]{2,1,0:T(8,128)(2,1)}), bf16[128,8,2048]{2,1,0:T(8,128)(2,1)}, u32[]{:S(2)}, u32[]{:S(2)}) async-start(bf16[128,8,2048]{2,1,0:T(8,128)(2,1)} %convert_bitcast_fusion.3), calls=%async_computation.3 | async-start | bytes 8388608 | tf_op jit(solution)/shard_map/all_to_all | solution.py:155
  297.1 57.3 %all-to-all-start.4 = ((bf16[128,8,2048]{2,1,0:T(8,128)(2,1)}), bf16[128,8,2048]{2,1,0:T(8,128)(2,1)}, u32[]{:S(2)}, u32[]{:S(2)}) async-start(bf16[128,8,2048]{2,1,0:T(8,128)(2,1)} %convert_bitcast_fusion.1), calls=%async_computation.5 | async-start | bytes 8388608 | tf_op jit(solution)/shard_map/all_to_all | solution.py:172
  309.8 50.4 %copy-start.10 = (f32[128,4]{0,1:T(4,128)S(1)}, f32[128,4]{0,1:T(4,128)}, u32[]{:S(2)}) copy-start(f32[128,4]{0,1:T(4,128)} %param.17) | copy-start | bytes 6148
  354.3 57.3 %all-to-all-start.5 = ((bf16[128,8,2048]{2,1,0:T(8,128)(2,1)}), bf16[128,8,2048]{2,1,0:T(8,128)(2,1)}, u32[]{:S(2)}, u32[]{:S(2)}) async-start(bf16[128,8,2048]{2,1,0:T(8,128)(2,1)} %convert_bitcast_fusion), calls=%async_computation.6 | async-start | bytes 8388608 | tf_op jit(solution)/shard_map/all_to_all | solution.py:172
  411.6 4.8 %copy-start.3 = (bf16[128,4096]{1,0:T(8,128)(2,1)S(1)}, bf16[128,4096]{1,0:T(8,128)(2,1)}, u32[]{:S(2)}) copy-start(bf16[128,4096]{1,0:T(8,128)(2,1)} %reduce-scatter.2.cloned.1.call-done) | copy-start | bytes 3145732
  411.6 4.8 %copy-start.6 = (f32[128,2048]{1,0:T(8,128)S(1)}, f32[128,2048]{1,0:T(8,128)}, u32[]{:S(2)}) copy-start(f32[128,2048]{1,0:T(8,128)} %multiply_reduce_fusion.1) | copy-start | bytes 3145732
  411.6 6.2 %copy-start.1 = (bf16[256,4096]{1,0:T(8,128)(2,1)S(1)}, bf16[256,4096]{1,0:T(8,128)(2,1)}, u32[]{:S(2)}) copy-start(bf16[256,4096]{1,0:T(8,128)(2,1)} %param.13) | copy-start | bytes 6291460
Sparse Core Ops, SparseCore 0:
  9.4 61.5 all-gather.1
  110.5 44.0 reduce-scatter.1

commit v10 on v7

--- a/solution.py
+++ b/solution.py
@@ -15,23 +15,32 @@
 def _attend_kernel(meta_ref, q_ref, k_ref, v_ref, o_ref, *, block, scale, tok_dev, n_sb):
     qi = pl.program_id(1)
     sb = meta_ref[0]
-    q = q_ref[...]
-    k = k_ref[...]
-    length = k.shape[0]
-    scores = lax.dot_general(
-        q, k, (((1,), (1,)), ((), ())), preferred_element_type=jnp.float32
-    ) * scale
-    local = qi * block + lax.broadcasted_iota(jnp.int32, (block, length), 0)
-    q_pos = ((local // tok_dev) * n_sb + sb) * tok_dev + local % tok_dev
-    k_pos = lax.broadcasted_iota(jnp.int32, (block, length), 1)
-    scores = jnp.where(k_pos <= q_pos, scores, jnp.float32(-1e30))
-    top = jnp.max(scores, axis=1, keepdims=True)
-    weights = jnp.exp(scores - top)
-    total = jnp.sum(weights, axis=1, keepdims=True)
-    probs = (weights / total).astype(jnp.bfloat16)
-    o_ref[...] = jnp.dot(probs, v_ref[...], preferred_element_type=jnp.float32).astype(
-        o_ref.dtype
-    )
+
+    def attend(length):
+        q = q_ref[...]
+        k = k_ref[:length, :]
+        scores = lax.dot_general(
+            q, k, (((1,), (1,)), ((), ())), preferred_element_type=jnp.float32
+        ) * scale
+        local = qi * block + lax.broadcasted_iota(jnp.int32, (block, length), 0)
+        q_pos = ((local // tok_dev) * n_sb + sb) * tok_dev + local % tok_dev
+        k_pos = lax.broadcasted_iota(jnp.int32, (block, length), 1)
+        scores = jnp.where(k_pos <= q_pos, scores, jnp.float32(-1e30))
+        top = jnp.max(scores, axis=1, keepdims=True)
+        weights = jnp.exp(scores - top)
+        total = jnp.sum(weights, axis=1, keepdims=True)
+        probs = (weights / total).astype(jnp.bfloat16)
+        o_ref[...] = jnp.dot(
+            probs, v_ref[:length, :], preferred_element_type=jnp.float32
+        ).astype(o_ref.dtype)
+
+    seq_len = k_ref.shape[0]
+    for i in range(seq_len):
+        length = min(seq_len, (i + 1) * block * n_sb)
+        if length == seq_len:
+            pl.when(qi >= i)(lambda: attend(seq_len))
+            break
+        pl.when(qi == i)(functools.partial(attend, length))
 
 
 def attention(meta, q_rows, kv_all, heads, head_size, tok_dev, n_sb):

time: 410 us -> 406 us (level)
  transfers between devices with their start and end apart: 4 -> 4, of which waited for: 3 -> 3; matrix products, arithmetic and copies ran while one was open for 2% -> 2% of each run, Pallas kernels for 6% -> 5%
where the time goes in v10:
time: 406 us; the launch traced here: 405 us
  blocking collectives  231 us (57%)
  waiting for transfers between devices  71.5 us (18%)
  matrix products  43.6 us (11%)
  Pallas kernels  19.3 us (5%)
  local copies, waits for them, and re-layouts  15.3 us (4%)
  between operations  13.7 us (3%)
  starting transfers between devices  7.46 us (2%)
    all_to_all x1, blocking collectives, shards(): lax.all_to_all(outgoing_rows, ('grp', 'sa', 'sb'), split_axis=0, concat_a...  106 us
    all_to_all x1, blocking collectives, shards(): lax.all_to_all(produced.reshape(arrived.shape), ('grp', 'sa', 'sb'), spli...  103 us
    reduce_scatter x1, waiting for transfers between devices, shards(): lax.psum_scatter(partial_sum.astype(jnp.bfloat16), 'sa', scatter_dimensio...  42.3 us
    all_to_all x1, waiting for transfers between devices, shards(): lax.all_to_all(jnp.broadcast_to(kv_col[None], (n_sb,) + kv_col.shape), 's...  24.8 us
    all_to_all x1, blocking collectives, shards(): lax.all_to_all(jnp.concatenate([q_send, kv_send], axis=2), 'sa', split_ax...  21.9 us
    pallas_call x1, Pallas kernels, attention(): pl.pallas_call(kernel, out_shape=jax.ShapeDtypeStruct((rows, heads * head...  19.3 us
    dot_general x1, matrix products, shards(): projected = jnp.dot(flat_rows, w_in[0], preferred_element_type=jnp.float32)  17.2 us
    dot_general x1, matrix products, shards(): jnp.dot(hidden, w_down[0], preferred_element_type=jnp.float32)  9.81 us
  transfers between devices with their start and end apart: 4, of which 3 were waited for; matrix products, arithmetic and copies ran while one was open for 2% of the time, Pallas kernels for 5%

profile of v10, /device:TPU:7, one launch (start us, length us, event | category | flops | bytes accessed | tf_op | source)
XLA Modules:
  0.0 405.3 jit_solution(8902658553439075796)
XLA Ops:
  6.5 1.6 copy-done
  8.1 1.1 constant_dynamic-slice_fusion
  9.2 0.0 all-gather.2.cloned.1.call-update
  9.2 1.0 copy.49
  10.3 0.1 copy.50
  10.4 0.6 gather_fusion
  11.1 0.1 select_bitcast_fusion
  11.2 0.2 copy.51
  11.3 0.1 copy.52
  11.5 0.1 copy.58
  11.6 0.1 pad_maximum_fusion
  11.7 21.9 %all_to_all.20 = bf16[4,128,1280]{2,1,0:T(8,128)(2,1)S(1)} all-to-all(bf16[4,128,1280]{2,1,0:T(8,128)(2,1)S(1)} %pad_maximum_fusion), channel_id=1, replica_groups=mesh['grp'=8,'sa'=4,'sb'=4] {'sa'}, dimensions={0} | all-to-all | bytes 2621440 | tf_op jit(solution)/shard_map/all_to_all | solution.py:103
  33.6 1.2 broadcast_in_dim.26
  34.8 4.2 %all-to-all-start.1 = ((bf16[4,4,128,256]{3,2,1,0:T(8,128)(2,1)}), bf16[4,4,128,256]{3,2,1,0:T(8,128)(2,1)}, u32[]{:S(2)}, u32[]{:S(2)}) async-start(bf16[4,4,128,256]{3,2,1,0:T(8,128)(2,1)} %broadcast_in_dim.26), calls=%async_computation.1 | async-start | bytes 2097152 | tf_op jit(solution)/shard_map/all_to_all | solution.py:108
  39.0 0.0 reduce-scatter.2.cloned.1.call-start
  39.1 0.1 pad_add_fusion.meta_ref
  39.2 1.3 slice.50
  40.5 24.8 %all-to-all-done.1 = bf16[4,4,128,256]{3,2,1,0:T(8,128)(2,1)} async-done(((bf16[4,4,128,256]{3,2,1,0:T(8,128)(2,1)}), bf16[4,4,128,256]{3,2,1,0:T(8,128)(2,1)}, u32[]{:S(2)}, u32[]{:S(2)}) %all-to-all-start.1) | async-done | bytes 1048608 | tf_op jit(solution)/shard_map/all_to_all | solution.py:108
  65.3 1.3 copy.53
  66.6 19.3 %shard_map.91 = bf16[512,1024]{1,0:T(8,128)(2,1)S(1)} custom-call(s32[2]{0:T(128)S(1)} %pad_add_fusion.meta_ref, bf16[512,1024]{1,0:T(8,128)(2,1)S(1)} %bitcast.42, bf16[2048,256]{1,0:T(8,128)(2,1)S(1)} %bitcast.40, bf16[2048,256]{1,0:T(8,128)(2,1)S(1)} %bitcast.41), custom_call_target="tpu_custom_call" | custom-call | tf_op jit(solution)/shard_map/pallas_call | solution.py:53
  85.9 0.0 all-gather.2.cloned.1.call-done
  86.0 3.2 collective-permute-start
  89.1 1.0 broadcast_in_dim.27
  90.2 1.1 copy-done.5
  91.3 0.6 constant_dynamic-update-slice_fusion.1
  92.0 4.3 %collective-permute-done = bf16[1024,2048]{1,0:T(8,128)(2,1)} collective-permute-done((bf16[1024,2048]{1,0:T(8,128)(2,1)}, bf16[1024,2048]{1,0:T(8,128)(2,1)}, u32[]{:S(2)}, u32[]{:S(2)}) %collective-permute-start) | collective-permute-done | bytes 4194336 | tf_op jit(solution)/shard_map/ppermute | solution.py:117
  96.3 2.8 constant_dynamic-update-slice_fusion
  99.0 1.3 convolution_convert_fusion.3
  100.3 1.3 convolution_convert_fusion.2
  101.6 1.3 convolution_convert_fusion.1
  102.9 3.8 add_convert_fusion
  106.6 0.0 reduce-scatter.2.cloned.1.call-update
  106.7 0.7 copy-done.8
  107.3 0.1 copy.54
  107.4 0.1 eq.40
  107.5 0.3 fusion.16
  107.9 0.1 convert_element_type.84
  108.0 0.1 copy.55
  108.1 0.4 fusion.13
  108.5 42.3 %reduce-scatter.2.cloned.1.call-done = bf16[128,4096]{1,0:T(8,128)(2,1)} async-done(((bf16[512,4096]{1,0:T(8,128)(2,1)}), bf16[128,4096]{1,0:T(8,128)(2,1)}) %reduce-scatter.2.cloned.1.call-update) | async-done | bytes 1048592 | tf_op jit(solution)/shard_map/reduce_scatter | solution.py:129
  150.8 1.6 multiply_reduce_fusion.1
  152.5 3.7 convert_bitcast_fusion.1
  156.1 105.9 %all_to_all.21 = bf16[128,8,4096]{2,1,0:T(8,128)(2,1)S(1)} all-to-all(bf16[128,8,4096]{2,1,0:T(8,128)(2,1)S(1)} %convert_bitcast_fusion.1), channel_id=1, replica_groups=mesh['grp'=8,'sa'=4,'sb'=4] {'grp','sa','sb'}, dimensions={0} | all-to-all | bytes 16777216 | tf_op jit(solution)/shard_map/all_to_all | solution.py:160
  262.0 17.2 %fusion = f32[1024,1536]{1,0:T(8,128)} fusion(bf16[1,4096,1536]{2,1,0:T(8,128)(2,1)} %param.14, bf16[128,8,4096]{2,1,0:T(8,128)(2,1)S(1)} %all_to_all.21), kind=kOutput, calls=%fused_computation.1 | convolution fusion | flops 12884901888 | bytes 27262976 | tf_op jit(solution)/shard_map/dot_general | solution.py:162
  279.2 9.8 %convert_bitcast_fusion = bf16[128,8,4096]{2,1,0:T(8,128)(2,1)S(1)} fusion(bf16[1,768,4096]{2,1,0:T(8,128)(2,1)S(1)} %bitcast.49, f32[1024,1536]{1,0:T(8,128)} %fusion), kind=kOutput, calls=%fused_computation.7 | convolution fusion | flops 6451363840 | bytes 20971520 | tf_op jit(solution)/shard_map/dot_general | solution.py:164
  289.0 102.9 %all_to_all.22 = bf16[128,8,4096]{2,1,0:T(8,128)(2,1)S(1)} all-to-all(bf16[128,8,4096]{2,1,0:T(8,128)(2,1)S(1)} %convert_bitcast_fusion), channel_id=1, replica_groups=mesh['grp'=8,'sa'=4,'sb'=4] {'grp','sa','sb'}, dimensions={0} | all-to-all | bytes 16777216 | tf_op jit(solution)/shard_map/all_to_all | solution.py:165
  391.9 5.1 %multiply_reduce_fusion = f32[128,4096]{1,0:T(8,128)S(1)} fusion(bf16[128,8,4096]{2,1,0:T(8,128)(2,1)S(1)} %all_to_all.22, f32[4,128]{1,0:T(4,128)S(1)} %bitcast.50, s32[4,128]{1,0:T(4,128)S(1)} %bitcast.47), kind=kOutput, calls=%fused_computation.6 | convolution fusion | flops 4299161600 | bytes 10489856 | tf_op jit(solution)/shard_map/dot_general | solution.py:170
  397.1 1.4 add_convert_fusion.1
  (31 shorter events, 0.1 us)
Async XLA Ops:
  6.5 1.6 copy-start
  6.5 5.0 %copy-start.6 = (bf16[128,4096]{1,0:T(8,128)(2,1)S(1)}, bf16[128,4096]{1,0:T(8,128)(2,1)}, u32[]{:S(2)}) copy-start(bf16[128,4096]{1,0:T(8,128)(2,1)} %param.9) | copy-start | bytes 3145732
  6.5 79.4 %all-gather.2.cloned.1.call-start = ((), (), s32[]{:S(2)}) async-start(), calls=%async_computation.5 | async-start | bytes 5242880 | tf_op jit(solution)/shard_map/all_gather | solution.py:95
  33.6 5.5 %copy-start.4 = (bf16[4,128,1280]{2,1,0:T(8,128)(2,1)}, bf16[4,128,1280]{2,1,0:T(8,128)(2,1)S(1)}, u32[]{:S(2)}) copy-start(bf16[4,128,1280]{2,1,0:T(8,128)(2,1)S(1)} %all_to_all.20) | copy-start | bytes 3932164
  34.8 30.5 %all-to-all-start.1 = ((bf16[4,4,128,256]{3,2,1,0:T(8,128)(2,1)}), bf16[4,4,128,256]{3,2,1,0:T(8,128)(2,1)}, u32[]{:S(2)}, u32[]{:S(2)}) async-start(bf16[4,4,128,256]{3,2,1,0:T(8,128)(2,1)} %broadcast_in_dim.26), calls=%async_computation.1 | async-start | bytes 2097152 | tf_op jit(solution)/shard_map/all_to_all | solution.py:108
  39.0 111.8 %reduce-scatter.2.cloned.1.call-start = ((), (), s32[]{:S(2)}) async-start(), calls=%async_computation.6 | async-start | bytes 5242880 | tf_op jit(solution)/shard_map/reduce_scatter | solution.py:129
  86.0 10.3 %collective-permute-start = (bf16[1024,2048]{1,0:T(8,128)(2,1)}, bf16[1024,2048]{1,0:T(8,128)(2,1)}, u32[]{:S(2)}, u32[]{:S(2)}) collective-permute-start(bf16[1024,2048]{1,0:T(8,128)(2,1)} %all-gather.2.cloned.1.call-done), channel_id=1, source_target_pairs={{0,16},{16,0},{32,48},{48,32},{64,80},{80,64},{96,112},{112,96},{1... | collective-permute-start | bytes 12582920 | tf_op jit(solution)/shard_map/ppermute | solution.py:117
  89.1 2.2 copy-start.5
  106.6 0.7 copy-start.8
  106.6 1.4 copy-start.7
  106.6 44.2 %copy-start.2 = (bf16[128,4096]{1,0:T(8,128)(2,1)S(1)}, bf16[128,4096]{1,0:T(8,128)(2,1)}, u32[]{:S(2)}) copy-start(bf16[128,4096]{1,0:T(8,128)(2,1)} %param.11) | copy-start | bytes 3145732
  156.1 123.0 %slice-start = ((s8[6291456]{0:T(1024)(128)(4,1)}), s8[4194304]{0:T(1024)(128)(4,1)S(1)}, s32[]{:S(2)}) async-start(s8[6291456]{0:T(1024)(128)(4,1)} %bitcast.48), calls=%async_computation.7 | async-start | bytes 8388608
  262.0 17.2 %slice-start.1 = ((s8[6291456]{0:T(1024)(128)(4,1)}), s8[2097152]{0:T(1024)(128)(4,1)S(1)}, s32[]{:S(2)}) async-start(s8[6291456]{0:T(1024)(128)(4,1)} %bitcast.48), calls=%async_computation.8 | async-start | bytes 4194304
  289.0 102.9 %copy-start.9 = (f32[128,4]{0,1:T(4,128)S(1)}, f32[128,4]{0,1:T(4,128)}, u32[]{:S(2)}) copy-start(f32[128,4]{0,1:T(4,128)} %param.17) | copy-start | bytes 6148
  391.9 5.1 %copy-start.3 = (bf16[128,4096]{1,0:T(8,128)(2,1)S(1)}, bf16[128,4096]{1,0:T(8,128)(2,1)}, u32[]{:S(2)}) copy-start(bf16[128,4096]{1,0:T(8,128)(2,1)} %reduce-scatter.2.cloned.1.call-done) | copy-start | bytes 3145732
  391.9 6.5 %copy-start.1 = (bf16[256,4096]{1,0:T(8,128)(2,1)S(1)}, bf16[256,4096]{1,0:T(8,128)(2,1)}, u32[]{:S(2)}) copy-start(bf16[256,4096]{1,0:T(8,128)(2,1)} %param.13) | copy-start | bytes 6291460
Sparse Core Ops, SparseCore 0:
  9.4 61.5 all-gather.1
  106.8 43.9 reduce-scatter.1

commit v11 on v10

--- a/solution.py
+++ b/solution.py
@@ -115,9 +115,7 @@
 
     w_mine, attended = lax.optimization_barrier((w_mine, attended))
     w_other = lax.ppermute(w_mine, "grp", [(g, g ^ 1) for g in range(n_grp)])
-    w_rows = jnp.zeros((w_mine.shape[0], 2 * half), o_weight.dtype)
-    w_rows = lax.dynamic_update_slice_in_dim(w_rows, w_mine, pair * half, axis=1)
-    w_rows = lax.dynamic_update_slice_in_dim(w_rows, w_other, (1 - pair) * half, axis=1)
+    w_rows = jnp.concatenate([w_mine, w_other], axis=1)
 
     partial_sum = None
     for j in range(w_rows.shape[0] // block_rows):
@@ -126,8 +124,11 @@
             attended[:, cols], w_rows[cols], preferred_element_type=jnp.float32
         ).astype(jnp.bfloat16).astype(jnp.float32)
         partial_sum = partial_j if partial_sum is None else partial_sum + partial_j
-    attn_out = lax.psum_scatter(
+    swapped = lax.psum_scatter(
         partial_sum.astype(jnp.bfloat16), "sa", scatter_dimension=0, tiled=True
+    )
+    attn_out = lax.dynamic_slice_in_dim(
+        jnp.concatenate([swapped, swapped], axis=1), pair * half, 2 * half, axis=1
     ).astype(jnp.float32)
     mixed = residual.astype(jnp.float32) + attn_out
     mean_square = jnp.mean(mixed * mixed, axis=1, keepdims=True)

time: 406 us -> 403 us (level)
  transfers between devices with their start and end apart: 4 -> 4, of which waited for: 3 -> 3; matrix products, arithmetic and copies ran while one was open for 2% -> 3% of each run, Pallas kernels for 5% -> 5%
where the time goes in v11:
time: 403 us; the launch traced here: 402 us
  blocking collectives  231 us (57%)
  waiting for transfers between devices  71.6 us (18%)
  matrix products  43 us (11%)
  Pallas kernels  19.3 us (5%)
  between operations  13.7 us (3%)
  local copies, waits for them, and re-layouts  12.8 us (3%)
  starting transfers between devices  7.36 us (2%)
    all_to_all x1, blocking collectives, shards(): lax.all_to_all(outgoing_rows, ('grp', 'sa', 'sb'), split_axis=0, concat_a...  106 us
    all_to_all x1, blocking collectives, shards(): lax.all_to_all(produced.reshape(arrived.shape), ('grp', 'sa', 'sb'), spli...  103 us
    reduce_scatter x1, waiting for transfers between devices, shards(): lax.psum_scatter(partial_sum.astype(jnp.bfloat16), 'sa', scatter_dimensio...  42.5 us
    all_to_all x1, waiting for transfers between devices, shards(): lax.all_to_all(jnp.broadcast_to(kv_col[None], (n_sb,) + kv_col.shape), 's...  24.8 us
    all_to_all x1, blocking collectives, shards(): lax.all_to_all(jnp.concatenate([q_send, kv_send], axis=2), 'sa', split_ax...  21.9 us
    pallas_call x1, Pallas kernels, attention(): pl.pallas_call(kernel, out_shape=jax.ShapeDtypeStruct((rows, heads * head...  19.3 us
    dot_general x1, matrix products, shards(): projected = jnp.dot(flat_rows, w_in[0], preferred_element_type=jnp.float32)  17.1 us
    dot_general x1, matrix products, shards(): jnp.dot(hidden, w_down[0], preferred_element_type=jnp.float32)  10.7 us
  transfers between devices with their start and end apart: 4, of which 3 were waited for; matrix products, arithmetic and copies ran while one was open for 3% of the time, Pallas kernels for 5%

profile of v11, /device:TPU:7, one launch (start us, length us, event | category | flops | bytes accessed | tf_op | source)
XLA Modules:
  0.0 402.3 jit_solution(9649490330544268750)
XLA Ops:
  6.5 1.6 copy-done
  8.1 1.1 constant_dynamic-slice_fusion
  9.2 0.0 all-gather.2.cloned.1.call-update
  9.2 1.0 copy.49
  10.3 0.1 copy.50
  10.4 0.6 gather_fusion
  11.1 0.1 select_bitcast_fusion
  11.2 0.2 copy.51
  11.3 0.1 copy.52
  11.5 0.1 copy.58
  11.6 0.1 pad_maximum_fusion
  11.7 21.9 %all_to_all.20 = bf16[4,128,1280]{2,1,0:T(8,128)(2,1)S(1)} all-to-all(bf16[4,128,1280]{2,1,0:T(8,128)(2,1)S(1)} %pad_maximum_fusion), channel_id=1, replica_groups=mesh['grp'=8,'sa'=4,'sb'=4] {'sa'}, dimensions={0} | all-to-all | bytes 2621440 | tf_op jit(solution)/shard_map/all_to_all | solution.py:103
  33.6 1.2 broadcast_in_dim.14
  34.8 4.3 %all-to-all-start.1 = ((bf16[4,4,128,256]{3,2,1,0:T(8,128)(2,1)}), bf16[4,4,128,256]{3,2,1,0:T(8,128)(2,1)}, u32[]{:S(2)}, u32[]{:S(2)}) async-start(bf16[4,4,128,256]{3,2,1,0:T(8,128)(2,1)} %broadcast_in_dim.14), calls=%async_computation.1 | async-start | bytes 2097152 | tf_op jit(solution)/shard_map/all_to_all | solution.py:108
  39.1 0.0 reduce-scatter.2.cloned.1.call-start
  39.1 0.1 pad_add_fusion.meta_ref
  39.2 1.3 slice.50
  40.5 24.8 %all-to-all-done.1 = bf16[4,4,128,256]{3,2,1,0:T(8,128)(2,1)} async-done(((bf16[4,4,128,256]{3,2,1,0:T(8,128)(2,1)}), bf16[4,4,128,256]{3,2,1,0:T(8,128)(2,1)}, u32[]{:S(2)}, u32[]{:S(2)}) %all-to-all-start.1) | async-done | bytes 1048608 | tf_op jit(solution)/shard_map/all_to_all | solution.py:108
  65.3 1.3 copy.53
  66.7 19.3 %shard_map.91 = bf16[512,1024]{1,0:T(8,128)(2,1)S(1)} custom-call(s32[2]{0:T(128)S(1)} %pad_add_fusion.meta_ref, bf16[512,1024]{1,0:T(8,128)(2,1)S(1)} %bitcast.42, bf16[2048,256]{1,0:T(8,128)(2,1)S(1)} %bitcast.40, bf16[2048,256]{1,0:T(8,128)(2,1)S(1)} %bitcast.41), custom_call_target="tpu_custom_call" | custom-call | tf_op jit(solution)/shard_map/pallas_call | solution.py:53
  86.0 0.0 all-gather.2.cloned.1.call-done
  86.0 3.0 collective-permute-start
  89.0 2.8 constant_dynamic-update-slice_fusion.1
  91.8 4.2 %collective-permute-done = bf16[1024,2048]{1,0:T(8,128)(2,1)S(1)} collective-permute-done((bf16[1024,2048]{1,0:T(8,128)(2,1)}, bf16[1024,2048]{1,0:T(8,128)(2,1)S(1)}, u32[]{:S(2)}, u32[]{:S(2)}) %collective-permute-start) | collective-permute-done | bytes 4194336 | tf_op jit(solution)/shard_map/ppermute | solution.py:117
  96.0 0.3 constant_dynamic-update-slice_fusion
  96.4 1.3 convolution_convert_fusion.3
  97.6 1.3 convolution_convert_fusion.2
  98.9 1.3 convolution_convert_fusion.1
  100.2 3.5 add_convert_fusion
  103.7 0.0 reduce-scatter.2.cloned.1.call-update
  103.7 0.6 copy-done.6
  104.4 0.1 copy.54
  104.5 0.1 eq.40
  104.6 0.3 fusion.16
  104.9 0.1 convert_element_type.84
  105.0 0.1 copy.55
  105.1 0.0 copy-done.5
  105.1 0.4 fusion.13
  105.5 42.5 %reduce-scatter.2.cloned.1.call-done = bf16[128,4096]{1,0:T(8,128)(2,1)} async-done(((bf16[512,4096]{1,0:T(8,128)(2,1)}), bf16[128,4096]{1,0:T(8,128)(2,1)}) %reduce-scatter.2.cloned.1.call-update) | async-done | bytes 1048592 | tf_op jit(solution)/shard_map/reduce_scatter | solution.py:127
  148.0 1.9 multiply_reduce_fusion.1
  149.9 2.4 convert_bitcast_fusion.1
  152.3 105.9 %all_to_all.21 = bf16[128,8,4096]{2,1,0:T(8,128)(2,1)S(1)} all-to-all(bf16[128,8,4096]{2,1,0:T(8,128)(2,1)S(1)} %convert_bitcast_fusion.1), channel_id=1, replica_groups=mesh['grp'=8,'sa'=4,'sb'=4] {'grp','sa','sb'}, dimensions={0} | all-to-all | bytes 16777216 | tf_op jit(solution)/shard_map/all_to_all | solution.py:161
  258.2 17.1 %fusion = f32[1024,1536]{1,0:T(8,128)} fusion(bf16[1,4096,1536]{2,1,0:T(8,128)(2,1)} %param.14, bf16[128,8,4096]{2,1,0:T(8,128)(2,1)S(1)} %all_to_all.21), kind=kOutput, calls=%fused_computation.1 | convolution fusion | flops 12884901888 | bytes 27262976 | tf_op jit(solution)/shard_map/dot_general | solution.py:163
  275.3 10.7 %convert_bitcast_fusion = bf16[128,8,4096]{2,1,0:T(8,128)(2,1)S(1)} fusion(bf16[1,768,4096]{2,1,0:T(8,128)(2,1)} %param.15, f32[1024,1536]{1,0:T(8,128)} %fusion), kind=kOutput, calls=%fused_computation.7 | convolution fusion | flops 6451363840 | bytes 20971520 | tf_op jit(solution)/shard_map/dot_general | solution.py:165
  286.1 0.0 copy-start.7
  286.1 102.9 %all_to_all.22 = bf16[128,8,4096]{2,1,0:T(8,128)(2,1)S(1)} all-to-all(bf16[128,8,4096]{2,1,0:T(8,128)(2,1)S(1)} %convert_bitcast_fusion), channel_id=1, replica_groups=mesh['grp'=8,'sa'=4,'sb'=4] {'grp','sa','sb'}, dimensions={0} | all-to-all | bytes 16777216 | tf_op jit(solution)/shard_map/all_to_all | solution.py:166
  389.0 5.1 %multiply_reduce_fusion = f32[128,4096]{1,0:T(8,128)S(1)} fusion(bf16[128,8,4096]{2,1,0:T(8,128)(2,1)S(1)} %all_to_all.22, f32[4,128]{1,0:T(4,128)S(1)} %bitcast.48, s32[4,128]{1,0:T(4,128)S(1)} %bitcast.47), kind=kOutput, calls=%fused_computation.6 | convolution fusion | flops 4299161600 | bytes 10489856 | tf_op jit(solution)/shard_map/dot_general | solution.py:171
  394.1 1.4 add_convert_fusion.1
  (21 shorter events, 0.1 us)
Async XLA Ops:
  6.5 1.6 copy-start
  6.5 5.0 %copy-start.4 = (bf16[128,4096]{1,0:T(8,128)(2,1)S(1)}, bf16[128,4096]{1,0:T(8,128)(2,1)}, u32[]{:S(2)}) copy-start(bf16[128,4096]{1,0:T(8,128)(2,1)} %param.9) | copy-start | bytes 3145732
  6.5 79.5 %all-gather.2.cloned.1.call-start = ((), (), s32[]{:S(2)}) async-start(), calls=%async_computation.5 | async-start | bytes 5242880 | tf_op jit(solution)/shard_map/all_gather | solution.py:95
  33.6 5.6 %copy-start.3 = (bf16[4,128,1280]{2,1,0:T(8,128)(2,1)}, bf16[4,128,1280]{2,1,0:T(8,128)(2,1)S(1)}, u32[]{:S(2)}) copy-start(bf16[4,128,1280]{2,1,0:T(8,128)(2,1)S(1)} %all_to_all.20) | copy-start | bytes 3932164
  34.8 30.6 %all-to-all-start.1 = ((bf16[4,4,128,256]{3,2,1,0:T(8,128)(2,1)}), bf16[4,4,128,256]{3,2,1,0:T(8,128)(2,1)}, u32[]{:S(2)}, u32[]{:S(2)}) async-start(bf16[4,4,128,256]{3,2,1,0:T(8,128)(2,1)} %broadcast_in_dim.14), calls=%async_computation.1 | async-start | bytes 2097152 | tf_op jit(solution)/shard_map/all_to_all | solution.py:108
  39.1 108.9 %reduce-scatter.2.cloned.1.call-start = ((), (), s32[]{:S(2)}) async-start(), calls=%async_computation.6 | async-start | bytes 5242880 | tf_op jit(solution)/shard_map/reduce_scatter | solution.py:127
  86.0 10.0 %collective-permute-start = (bf16[1024,2048]{1,0:T(8,128)(2,1)}, bf16[1024,2048]{1,0:T(8,128)(2,1)S(1)}, u32[]{:S(2)}, u32[]{:S(2)}) collective-permute-start(bf16[1024,2048]{1,0:T(8,128)(2,1)} %all-gather.2.cloned.1.call-done), channel_id=1, source_target_pairs={{0,16},{16,0},{32,48},{48,32},{64,80},{80,64},{96,112},{112,96},{1... | collective-permute-start | bytes 12582920 | tf_op jit(solution)/shard_map/ppermute | solution.py:117
  103.7 0.7 copy-start.6
  103.7 1.4 copy-start.5
  103.7 44.3 %copy-start.2 = (bf16[128,4096]{1,0:T(8,128)(2,1)S(1)}, bf16[128,4096]{1,0:T(8,128)(2,1)}, u32[]{:S(2)}) copy-start(bf16[128,4096]{1,0:T(8,128)(2,1)} %param.11) | copy-start | bytes 3145732
  286.1 102.9 %copy-start.7 = (f32[128,4]{0,1:T(4,128)S(1)}, f32[128,4]{0,1:T(4,128)}, u32[]{:S(2)}) copy-start(f32[128,4]{0,1:T(4,128)} %param.17) | copy-start | bytes 6148
  389.0 6.5 %copy-start.1 = (bf16[256,4096]{1,0:T(8,128)(2,1)S(1)}, bf16[256,4096]{1,0:T(8,128)(2,1)}, u32[]{:S(2)}) copy-start(bf16[256,4096]{1,0:T(8,128)(2,1)} %param.13) | copy-start | bytes 6291460
Sparse Core Ops, SparseCore 0:
  9.4 61.5 all-gather.1
  103.8 44.0 reduce-scatter.1

commit v12 on v11

--- a/solution.py
+++ b/solution.py
@@ -111,10 +111,9 @@
     )
     kv_all = kv_grid.transpose(1, 0, 2, 3).reshape(n_seq * tok_dev, 2 * head_size)
     meta = jnp.stack([sb, jnp.zeros_like(sb)]).astype(jnp.int32)
+    w_mine, kv_all = lax.optimization_barrier((w_mine, kv_all))
+    w_other = lax.ppermute(w_mine, "grp", [(g, g ^ 1) for g in range(n_grp)])
     attended = attention(meta, q_rows, kv_all, heads_here, head_size, tok_dev, n_sb)
-
-    w_mine, attended = lax.optimization_barrier((w_mine, attended))
-    w_other = lax.ppermute(w_mine, "grp", [(g, g ^ 1) for g in range(n_grp)])
     w_rows = jnp.concatenate([w_mine, w_other], axis=1)
 
     partial_sum = None

time: 403 us -> 404 us (level)
  blocking collectives: 231 us -> 261 us
  waiting for transfers between devices: 71.6 us -> 52.1 us
  starting transfers between devices: 7.36 us -> 0.88 us
    all_to_all x0 -> x1, blocking collectives: none -> 30.2 us  [shards(): lax.all_to_all(jnp.broadcast_to(kv_col[None], (n_sb,) + kv_col.shape), 's...]
    all_to_all x1 -> x0, waiting for transfers between devices: 24.8 us -> none  [shards(): lax.all_to_all(jnp.broadcast_to(kv_col[None], (n_sb,) + kv_col.shape), 's...]
    all_gather x1, waiting for transfers between devices: 0.02 us -> 6.95 us  [shards(): lax.all_gather(lax.dynamic_slice_in_dim(o_weight, pair * half, half, axis...]
    all_to_all x1 -> x0, starting transfers between devices: 4.27 us -> none  [shards(): lax.all_to_all(jnp.broadcast_to(kv_col[None], (n_sb,) + kv_col.shape), 's...]
    ppermute x1, waiting for transfers between devices: 4.23 us -> 0.01 us  [shards(): w_other = lax.ppermute(w_mine, 'grp', [(g, g ^ 1) for g in range(n_grp)])]
  transfers between devices with their start and end apart: 4 -> 3, of which waited for: 3 -> 2; matrix products, arithmetic and copies ran while one was open for 3% -> 1% of each run, Pallas kernels for 5% -> 5%
where the time goes in v12:
time: 404 us; the launch traced here: 403 us
  blocking collectives  261 us (65%)
  waiting for transfers between devices  52.1 us (13%)
  matrix products  43.1 us (11%)
  Pallas kernels  19.3 us (5%)
  between operations  13.7 us (3%)
  local copies, waits for them, and re-layouts  9.56 us (2%)
    all_to_all x1, blocking collectives, shards(): lax.all_to_all(outgoing_rows, ('grp', 'sa', 'sb'), split_axis=0, concat_a...  106 us
    all_to_all x1, blocking collectives, shards(): lax.all_to_all(produced.reshape(arrived.shape), ('grp', 'sa', 'sb'), spli...  103 us
    reduce_scatter x1, waiting for transfers between devices, shards(): lax.psum_scatter(partial_sum.astype(jnp.bfloat16), 'sa', scatter_dimensio...  45.1 us
    all_to_all x1, blocking collectives, shards(): lax.all_to_all(jnp.broadcast_to(kv_col[None], (n_sb,) + kv_col.shape), 's...  30.2 us
    all_to_all x1, blocking collectives, shards(): lax.all_to_all(jnp.concatenate([q_send, kv_send], axis=2), 'sa', split_ax...  21.9 us
    pallas_call x1, Pallas kernels, attention(): pl.pallas_call(kernel, out_shape=jax.ShapeDtypeStruct((rows, heads * head...  19.3 us
    dot_general x1, matrix products, shards(): projected = jnp.dot(flat_rows, w_in[0], preferred_element_type=jnp.float32)  17.2 us
    dot_general x1, matrix products, shards(): jnp.dot(hidden, w_down[0], preferred_element_type=jnp.float32)  10.7 us
  transfers between devices with their start and end apart: 3, of which 2 were waited for; matrix products, arithmetic and copies ran while one was open for 1% of the time, Pallas kernels for 5%

profile of v12, /device:TPU:7, one launch (start us, length us, event | category | flops | bytes accessed | tf_op | source)
XLA Modules:
  0.0 403.5 jit_solution(18098664631095004808)
XLA Ops:
  6.5 1.6 copy-done
  8.1 1.1 constant_dynamic-slice_fusion
  9.2 0.0 all-gather.2.cloned.1.call-update
  9.2 0.0 reduce-scatter.2.cloned.1.call-start
  9.3 1.0 copy.49
  10.3 0.1 copy.50
  10.5 0.6 gather_fusion
  11.1 0.1 select_bitcast_fusion
  11.2 0.2 copy.51
  11.4 0.1 copy.52
  11.6 0.1 copy.58
  11.6 0.1 pad_maximum_fusion
  11.7 21.9 %all_to_all.20 = bf16[4,128,1280]{2,1,0:T(8,128)(2,1)S(1)} all-to-all(bf16[4,128,1280]{2,1,0:T(8,128)(2,1)S(1)} %pad_maximum_fusion), channel_id=1, replica_groups=mesh['grp'=8,'sa'=4,'sb'=4] {'sa'}, dimensions={0} | all-to-all | bytes 2621440 | tf_op jit(solution)/shard_map/all_to_all | solution.py:103
  33.6 0.1 broadcast_in_dim.14
  33.7 30.2 %all_to_all.21 = bf16[4,4,128,256]{3,2,1,0:T(8,128)(2,1)S(1)} all-to-all(bf16[4,4,128,256]{3,2,1,0:T(8,128)(2,1)S(1)} %broadcast_in_dim.14), channel_id=1, replica_groups=mesh['grp'=8,'sa'=4,'sb'=4] {'sb'}, dimensions={0} | all-to-all | bytes 2097152 | tf_op jit(solution)/shard_map/all_to_all | solution.py:108
  63.9 0.1 copy.53
  64.0 7.0 %all-gather.2.cloned.1.call-done = bf16[1024,2048]{1,0:T(8,128)(2,1)} async-done(((bf16[256,2048]{1,0:T(8,128)(2,1)}), bf16[1024,2048]{1,0:T(8,128)(2,1)}) %all-gather.2.cloned.1.call-update) | async-done | bytes 4194320 | tf_op jit(solution)/shard_map/all_gather | solution.py:95
  71.0 0.8 collective-permute-start
  71.8 0.1 pad_add_fusion.meta_ref
  71.9 0.1 slice.50
  72.0 19.3 %shard_map.91 = bf16[512,1024]{1,0:T(8,128)(2,1)S(1)} custom-call(s32[2]{0:T(128)S(1)} %pad_add_fusion.meta_ref, bf16[512,1024]{1,0:T(8,128)(2,1)S(1)} %bitcast.42, bf16[2048,256]{1,0:T(8,128)(2,1)S(1)} %bitcast.40, bf16[2048,256]{1,0:T(8,128)(2,1)S(1)} %bitcast.41), custom_call_target="tpu_custom_call" | custom-call | tf_op jit(solution)/shard_map/pallas_call | solution.py:53
  91.3 0.0 copy-done.3
  91.4 0.6 constant_dynamic-update-slice_fusion.1
  91.9 0.0 collective-permute-done
  91.9 2.8 constant_dynamic-update-slice_fusion
  94.7 1.3 convolution_convert_fusion.1
  96.0 1.3 convolution_convert_fusion.2
  97.3 1.3 convolution_convert_fusion.3
  98.5 3.5 add_convert_fusion
  102.0 0.0 reduce-scatter.2.cloned.1.call-update
  102.1 0.7 copy-done.5
  102.7 0.1 copy.54
  102.8 0.1 eq.40
  102.9 0.3 fusion.16
  103.3 0.1 convert_element_type.84
  103.4 0.1 copy.55
  103.5 0.4 fusion.13
  103.9 45.1 %reduce-scatter.2.cloned.1.call-done = bf16[128,4096]{1,0:T(8,128)(2,1)} async-done(((bf16[512,4096]{1,0:T(8,128)(2,1)}), bf16[128,4096]{1,0:T(8,128)(2,1)}) %reduce-scatter.2.cloned.1.call-update) | async-done | bytes 1048592 | tf_op jit(solution)/shard_map/reduce_scatter | solution.py:126
  149.0 1.9 multiply_reduce_fusion.1
  150.9 2.4 convert_bitcast_fusion.1
  153.4 105.9 %all_to_all.22 = bf16[128,8,4096]{2,1,0:T(8,128)(2,1)S(1)} all-to-all(bf16[128,8,4096]{2,1,0:T(8,128)(2,1)S(1)} %convert_bitcast_fusion.1), channel_id=1, replica_groups=mesh['grp'=8,'sa'=4,'sb'=4] {'grp','sa','sb'}, dimensions={0} | all-to-all | bytes 16777216 | tf_op jit(solution)/shard_map/all_to_all | solution.py:160
  259.3 17.2 %fusion = f32[1024,1536]{1,0:T(8,128)} fusion(bf16[1,4096,1536]{2,1,0:T(8,128)(2,1)} %param.14, bf16[128,8,4096]{2,1,0:T(8,128)(2,1)S(1)} %all_to_all.22), kind=kOutput, calls=%fused_computation.1 | convolution fusion | flops 12884901888 | bytes 27262976 | tf_op jit(solution)/shard_map/dot_general | solution.py:162
  276.5 10.7 %convert_bitcast_fusion = bf16[128,8,4096]{2,1,0:T(8,128)(2,1)S(1)} fusion(bf16[1,768,4096]{2,1,0:T(8,128)(2,1)} %param.15, f32[1024,1536]{1,0:T(8,128)} %fusion), kind=kOutput, calls=%fused_computation.7 | convolution fusion | flops 6451363840 | bytes 20971520 | tf_op jit(solution)/shard_map/dot_general | solution.py:164
  287.2 0.0 copy-start.7
  287.2 102.9 %all_to_all.23 = bf16[128,8,4096]{2,1,0:T(8,128)(2,1)S(1)} all-to-all(bf16[128,8,4096]{2,1,0:T(8,128)(2,1)S(1)} %convert_bitcast_fusion), channel_id=1, replica_groups=mesh['grp'=8,'sa'=4,'sb'=4] {'grp','sa','sb'}, dimensions={0} | all-to-all | bytes 16777216 | tf_op jit(solution)/shard_map/all_to_all | solution.py:165
  390.1 5.1 %multiply_reduce_fusion = f32[128,4096]{1,0:T(8,128)S(1)} fusion(bf16[128,8,4096]{2,1,0:T(8,128)(2,1)S(1)} %all_to_all.23, f32[4,128]{1,0:T(4,128)S(1)} %bitcast.49, s32[4,128]{1,0:T(4,128)S(1)} %bitcast.48), kind=kOutput, calls=%fused_computation.6 | convolution fusion | flops 4299161600 | bytes 10489856 | tf_op jit(solution)/shard_map/dot_general | solution.py:170
  395.3 1.4 add_convert_fusion.1
  396.6 0.0 copy-done.1
  (20 shorter events, 0.1 us)
Async XLA Ops:
  6.5 1.6 copy-start
  6.5 5.0 %copy-start.4 = (bf16[128,4096]{1,0:T(8,128)(2,1)S(1)}, bf16[128,4096]{1,0:T(8,128)(2,1)}, u32[]{:S(2)}) copy-start(bf16[128,4096]{1,0:T(8,128)(2,1)} %param.9) | copy-start | bytes 3145732
  6.5 64.4 %all-gather.2.cloned.1.call-start = ((), (), s32[]{:S(2)}) async-start(), calls=%async_computation.5 | async-start | bytes 5242880 | tf_op jit(solution)/shard_map/all_gather | solution.py:95
  9.2 139.8 %reduce-scatter.2.cloned.1.call-start = ((), (), s32[]{:S(2)}) async-start(), calls=%async_computation.6 | async-start | bytes 5242880 | tf_op jit(solution)/shard_map/reduce_scatter | solution.py:126
  71.0 21.0 %collective-permute-start = (bf16[1024,2048]{1,0:T(8,128)(2,1)}, bf16[1024,2048]{1,0:T(8,128)(2,1)}, u32[]{:S(2)}, u32[]{:S(2)}) collective-permute-start(bf16[1024,2048]{1,0:T(8,128)(2,1)} %all-gather.2.cloned.1.call-done), channel_id=1, source_target_pairs={{0,16},{16,0},{32,48},{48,32},{64,80},{80,64},{96,112},{112,96},{1... | collective-permute-start | bytes 12582920 | tf_op jit(solution)/shard_map/ppermute | solution.py:115
  71.8 19.5 %copy-start.3 = (bf16[1024,2048]{1,0:T(8,128)(2,1)S(1)}, bf16[1024,2048]{1,0:T(8,128)(2,1)}, u32[]{:S(2)}) copy-start(bf16[1024,2048]{1,0:T(8,128)(2,1)} %all-gather.2.cloned.1.call-done) | copy-start | bytes 12582916
  102.0 0.7 copy-start.5
  102.0 0.7 copy-start.6
  102.0 47.0 %copy-start.2 = (bf16[128,4096]{1,0:T(8,128)(2,1)S(1)}, bf16[128,4096]{1,0:T(8,128)(2,1)}, u32[]{:S(2)}) copy-start(bf16[128,4096]{1,0:T(8,128)(2,1)} %param.11) | copy-start | bytes 3145732
  287.2 103.0 %copy-start.7 = (f32[128,4]{0,1:T(4,128)S(1)}, f32[128,4]{0,1:T(4,128)}, u32[]{:S(2)}) copy-start(f32[128,4]{0,1:T(4,128)} %param.17) | copy-start | bytes 6148
  390.1 6.5 %copy-start.1 = (bf16[256,4096]{1,0:T(8,128)(2,1)S(1)}, bf16[256,4096]{1,0:T(8,128)(2,1)}, u32[]{:S(2)}) copy-start(bf16[256,4096]{1,0:T(8,128)(2,1)} %param.13) | copy-start | bytes 6291460
Sparse Core Ops, SparseCore 0:
  9.4 61.5 all-gather.1
  102.2 46.7 reduce-scatter.1

commit v13 on v11

--- a/solution.py
+++ b/solution.py
@@ -9,7 +9,7 @@
 from jax.sharding import Mesh, PartitionSpec as P
 
 HD = 128
-Q_BLOCK = 256
+Q_BLOCK = 128
 
 
 def _attend_kernel(meta_ref, q_ref, k_ref, v_ref, o_ref, *, block, scale, tok_dev, n_sb):

time: 403 us -> 408 us (1.012)
  Pallas kernels: 19.3 us -> 24.5 us
    pallas_call x1, Pallas kernels: 19.3 us -> 24.5 us  [attention(): pl.pallas_call(kernel, out_shape=jax.ShapeDtypeStruct((rows, heads * head...]
  transfers between devices with their start and end apart: 4 -> 4, of which waited for: 3 -> 3; matrix products, arithmetic and copies ran while one was open for 3% -> 2% of each run, Pallas kernels for 5% -> 6%
where the time goes in v13:
time: 408 us
  blocking collectives  231 us (57%)
  waiting for transfers between devices  71.7 us (18%)
  matrix products  43 us (11%)
  Pallas kernels  24.5 us (6%)
  between operations  13.7 us (3%)
  local copies, waits for them, and re-layouts  12.8 us (3%)
  starting transfers between devices  7.22 us (2%)
    all_to_all x1, blocking collectives, shards(): lax.all_to_all(outgoing_rows, ('grp', 'sa', 'sb'), split_axis=0, concat_a...  106 us
    all_to_all x1, blocking collectives, shards(): lax.all_to_all(produced.reshape(arrived.shape), ('grp', 'sa', 'sb'), spli...  103 us
    reduce_scatter x1, waiting for transfers between devices, shards(): lax.psum_scatter(partial_sum.astype(jnp.bfloat16), 'sa', scatter_dimensio...  42.6 us
    all_to_all x1, waiting for transfers between devices, shards(): lax.all_to_all(jnp.broadcast_to(kv_col[None], (n_sb,) + kv_col.shape), 's...  24.8 us
    pallas_call x1, Pallas kernels, attention(): pl.pallas_call(kernel, out_shape=jax.ShapeDtypeStruct((rows, heads * head...  24.5 us
    all_to_all x1, blocking collectives, shards(): lax.all_to_all(jnp.concatenate([q_send, kv_send], axis=2), 'sa', split_ax...  21.9 us
    dot_general x1, matrix products, shards(): projected = jnp.dot(flat_rows, w_in[0], preferred_element_type=jnp.float32)  17.1 us
    dot_general x1, matrix products, shards(): jnp.dot(hidden, w_down[0], preferred_element_type=jnp.float32)  10.7 us
  transfers between devices with their start and end apart: 4, of which 3 were waited for; matrix products, arithmetic and copies ran while one was open for 2% of the time, Pallas kernels for 6%

profile of v13, /device:TPU:7, one launch (start us, length us, event | category | flops | bytes accessed | tf_op | source)
XLA Modules:
  0.0 407.6 jit_solution(9905725619093859330)
XLA Ops:
  6.5 1.6 copy-done
  8.1 1.1 constant_dynamic-slice_fusion
  9.2 0.0 all-gather.2.cloned.1.call-update
  9.2 1.0 copy.49
  10.3 0.1 copy.50
  10.4 0.6 gather_fusion
  11.1 0.1 select_bitcast_fusion
  11.2 0.2 copy.51
  11.3 0.1 copy.52
  11.5 0.1 copy.58
  11.6 0.1 pad_maximum_fusion
  11.7 21.9 %all_to_all.20 = bf16[4,128,1280]{2,1,0:T(8,128)(2,1)S(1)} all-to-all(bf16[4,128,1280]{2,1,0:T(8,128)(2,1)S(1)} %pad_maximum_fusion), channel_id=1, replica_groups=mesh['grp'=8,'sa'=4,'sb'=4] {'sa'}, dimensions={0} | all-to-all | bytes 2621440 | tf_op jit(solution)/shard_map/all_to_all | solution.py:103
  33.6 1.2 broadcast_in_dim.14
  34.8 4.3 %all-to-all-start.1 = ((bf16[4,4,128,256]{3,2,1,0:T(8,128)(2,1)}), bf16[4,4,128,256]{3,2,1,0:T(8,128)(2,1)}, u32[]{:S(2)}, u32[]{:S(2)}) async-start(bf16[4,4,128,256]{3,2,1,0:T(8,128)(2,1)} %broadcast_in_dim.14), calls=%async_computation.1 | async-start | bytes 2097152 | tf_op jit(solution)/shard_map/all_to_all | solution.py:108
  39.1 0.0 reduce-scatter.2.cloned.1.call-start
  39.1 0.1 pad_add_fusion.meta_ref
  39.2 1.3 slice.50
  40.5 24.8 %all-to-all-done.1 = bf16[4,4,128,256]{3,2,1,0:T(8,128)(2,1)} async-done(((bf16[4,4,128,256]{3,2,1,0:T(8,128)(2,1)}), bf16[4,4,128,256]{3,2,1,0:T(8,128)(2,1)}, u32[]{:S(2)}, u32[]{:S(2)}) %all-to-all-start.1) | async-done | bytes 1048608 | tf_op jit(solution)/shard_map/all_to_all | solution.py:108
  65.3 1.3 copy.53
  66.7 24.5 %shard_map.91 = bf16[512,1024]{1,0:T(8,128)(2,1)S(1)} custom-call(s32[2]{0:T(128)S(1)} %pad_add_fusion.meta_ref, bf16[512,1024]{1,0:T(8,128)(2,1)S(1)} %bitcast.42, bf16[2048,256]{1,0:T(8,128)(2,1)S(1)} %bitcast.40, bf16[2048,256]{1,0:T(8,128)(2,1)S(1)} %bitcast.41), custom_call_target="tpu_custom_call" | custom-call | tf_op jit(solution)/shard_map/pallas_call | solution.py:53
  91.2 0.0 all-gather.2.cloned.1.call-done
  91.2 2.9 collective-permute-start
  94.2 2.8 constant_dynamic-update-slice_fusion.1
  96.9 4.2 %collective-permute-done = bf16[1024,2048]{1,0:T(8,128)(2,1)S(1)} collective-permute-done((bf16[1024,2048]{1,0:T(8,128)(2,1)}, bf16[1024,2048]{1,0:T(8,128)(2,1)S(1)}, u32[]{:S(2)}, u32[]{:S(2)}) %collective-permute-start) | collective-permute-done | bytes 4194336 | tf_op jit(solution)/shard_map/ppermute | solution.py:117
  101.2 0.3 constant_dynamic-update-slice_fusion
  101.5 1.3 convolution_convert_fusion.3
  102.7 1.3 convolution_convert_fusion.2
  104.0 1.3 convolution_convert_fusion.1
  105.3 3.5 add_convert_fusion
  108.8 0.0 reduce-scatter.2.cloned.1.call-update
  108.8 0.6 copy-done.6
  109.5 0.1 copy.54
  109.6 0.1 eq.40
  109.7 0.3 fusion.16
  110.0 0.1 convert_element_type.84
  110.1 0.1 copy.55
  110.2 0.0 copy-done.5
  110.2 0.4 fusion.13
  110.6 42.6 %reduce-scatter.2.cloned.1.call-done = bf16[128,4096]{1,0:T(8,128)(2,1)} async-done(((bf16[512,4096]{1,0:T(8,128)(2,1)}), bf16[128,4096]{1,0:T(8,128)(2,1)}) %reduce-scatter.2.cloned.1.call-update) | async-done | bytes 1048592 | tf_op jit(solution)/shard_map/reduce_scatter | solution.py:127
  153.2 1.9 multiply_reduce_fusion.1
  155.2 2.4 convert_bitcast_fusion.1
  157.6 105.9 %all_to_all.21 = bf16[128,8,4096]{2,1,0:T(8,128)(2,1)S(1)} all-to-all(bf16[128,8,4096]{2,1,0:T(8,128)(2,1)S(1)} %convert_bitcast_fusion.1), channel_id=1, replica_groups=mesh['grp'=8,'sa'=4,'sb'=4] {'grp','sa','sb'}, dimensions={0} | all-to-all | bytes 16777216 | tf_op jit(solution)/shard_map/all_to_all | solution.py:161
  263.5 17.1 %fusion = f32[1024,1536]{1,0:T(8,128)} fusion(bf16[1,4096,1536]{2,1,0:T(8,128)(2,1)} %param.14, bf16[128,8,4096]{2,1,0:T(8,128)(2,1)S(1)} %all_to_all.21), kind=kOutput, calls=%fused_computation.1 | convolution fusion | flops 12884901888 | bytes 27262976 | tf_op jit(solution)/shard_map/dot_general | solution.py:163
  280.6 10.7 %convert_bitcast_fusion = bf16[128,8,4096]{2,1,0:T(8,128)(2,1)S(1)} fusion(bf16[1,768,4096]{2,1,0:T(8,128)(2,1)} %param.15, f32[1024,1536]{1,0:T(8,128)} %fusion), kind=kOutput, calls=%fused_computation.7 | convolution fusion | flops 6451363840 | bytes 20971520 | tf_op jit(solution)/shard_map/dot_general | solution.py:165
  291.3 0.0 copy-start.7
  291.3 102.9 %all_to_all.22 = bf16[128,8,4096]{2,1,0:T(8,128)(2,1)S(1)} all-to-all(bf16[128,8,4096]{2,1,0:T(8,128)(2,1)S(1)} %convert_bitcast_fusion), channel_id=1, replica_groups=mesh['grp'=8,'sa'=4,'sb'=4] {'grp','sa','sb'}, dimensions={0} | all-to-all | bytes 16777216 | tf_op jit(solution)/shard_map/all_to_all | solution.py:166
  394.2 5.1 %multiply_reduce_fusion = f32[128,4096]{1,0:T(8,128)S(1)} fusion(bf16[128,8,4096]{2,1,0:T(8,128)(2,1)S(1)} %all_to_all.22, f32[4,128]{1,0:T(4,128)S(1)} %bitcast.48, s32[4,128]{1,0:T(4,128)S(1)} %bitcast.47), kind=kOutput, calls=%fused_computation.6 | convolution fusion | flops 4299161600 | bytes 10489856 | tf_op jit(solution)/shard_map/dot_general | solution.py:171
  399.4 1.4 add_convert_fusion.1
  (21 shorter events, 0.1 us)
Async XLA Ops:
  6.5 1.6 copy-start
  6.5 5.0 %copy-start.4 = (bf16[128,4096]{1,0:T(8,128)(2,1)S(1)}, bf16[128,4096]{1,0:T(8,128)(2,1)}, u32[]{:S(2)}) copy-start(bf16[128,4096]{1,0:T(8,128)(2,1)} %param.9) | copy-start | bytes 3145732
  6.5 84.7 %all-gather.2.cloned.1.call-start = ((), (), s32[]{:S(2)}) async-start(), calls=%async_computation.5 | async-start | bytes 5242880 | tf_op jit(solution)/shard_map/all_gather | solution.py:95
  33.6 5.6 %copy-start.3 = (bf16[4,128,1280]{2,1,0:T(8,128)(2,1)}, bf16[4,128,1280]{2,1,0:T(8,128)(2,1)S(1)}, u32[]{:S(2)}) copy-start(bf16[4,128,1280]{2,1,0:T(8,128)(2,1)S(1)} %all_to_all.20) | copy-start | bytes 3932164
  34.8 30.6 %all-to-all-start.1 = ((bf16[4,4,128,256]{3,2,1,0:T(8,128)(2,1)}), bf16[4,4,128,256]{3,2,1,0:T(8,128)(2,1)}, u32[]{:S(2)}, u32[]{:S(2)}) async-start(bf16[4,4,128,256]{3,2,1,0:T(8,128)(2,1)} %broadcast_in_dim.14), calls=%async_computation.1 | async-start | bytes 2097152 | tf_op jit(solution)/shard_map/all_to_all | solution.py:108
  39.1 114.1 %reduce-scatter.2.cloned.1.call-start = ((), (), s32[]{:S(2)}) async-start(), calls=%async_computation.6 | async-start | bytes 5242880 | tf_op jit(solution)/shard_map/reduce_scatter | solution.py:127
  91.2 9.9 %collective-permute-start = (bf16[1024,2048]{1,0:T(8,128)(2,1)}, bf16[1024,2048]{1,0:T(8,128)(2,1)S(1)}, u32[]{:S(2)}, u32[]{:S(2)}) collective-permute-start(bf16[1024,2048]{1,0:T(8,128)(2,1)} %all-gather.2.cloned.1.call-done), channel_id=1, source_target_pairs={{0,16},{16,0},{32,48},{48,32},{64,80},{80,64},{96,112},{112,96},{1... | collective-permute-start | bytes 12582920 | tf_op jit(solution)/shard_map/ppermute | solution.py:117
  108.8 0.7 copy-start.6
  108.8 1.4 copy-start.5
  108.8 44.4 %copy-start.2 = (bf16[128,4096]{1,0:T(8,128)(2,1)S(1)}, bf16[128,4096]{1,0:T(8,128)(2,1)}, u32[]{:S(2)}) copy-start(bf16[128,4096]{1,0:T(8,128)(2,1)} %param.11) | copy-start | bytes 3145732
  291.3 102.9 %copy-start.7 = (f32[128,4]{0,1:T(4,128)S(1)}, f32[128,4]{0,1:T(4,128)}, u32[]{:S(2)}) copy-start(f32[128,4]{0,1:T(4,128)} %param.17) | copy-start | bytes 6148
  394.2 6.5 %copy-start.1 = (bf16[256,4096]{1,0:T(8,128)(2,1)S(1)}, bf16[256,4096]{1,0:T(8,128)(2,1)}, u32[]{:S(2)}) copy-start(bf16[256,4096]{1,0:T(8,128)(2,1)} %param.13) | copy-start | bytes 6291460
Sparse Core Ops, SparseCore 0:
  9.4 61.6 all-gather.1
  108.9 44.2 reduce-scatter.1

commit v14 on v11

--- a/solution.py
+++ b/solution.py
@@ -167,14 +167,19 @@
         produced.reshape(arrived.shape), ("grp", "sa", "sb"), split_axis=0, concat_axis=0, tiled=True
     )
     returned = returned.reshape(slots, width)
-    picks_by_choice = picks.reshape(tok_dev, top_count, slots).transpose(1, 0, 2)
-    picked = jnp.dot(
-        picks_by_choice.reshape(n_flat, slots).astype(jnp.bfloat16),
-        returned,
-        preferred_element_type=jnp.float32,
-    ).reshape(top_count, tok_dev, width)
-    weights_by_choice = route_weights.T.reshape(top_count, tok_dev, 1)
-    combined = jnp.sum(picked * weights_by_choice, axis=0)
+    placed = jnp.sum(
+        jnp.where(picks, flat_weights[:, None], jnp.float32(0.0)).reshape(tok_dev, top_count, slots),
+        axis=1,
+    )
+    high = placed.astype(jnp.bfloat16)
+    rest = placed - high.astype(jnp.float32)
+    middle = rest.astype(jnp.bfloat16)
+    low = (rest - middle.astype(jnp.float32)).astype(jnp.bfloat16)
+    parts = jnp.concatenate([high, middle, low], axis=0)
+    combined = jnp.sum(
+        jnp.dot(parts, returned, preferred_element_type=jnp.float32).reshape(3, tok_dev, width),
+        axis=0,
+    )
     return (mixed + combined).astype(jnp.bfloat16)
 
 

time: 403 us -> 410 us (1.017)
  blocking collectives: 231 us -> 128 us
  waiting for transfers between devices: 71.6 us -> 174 us
  starting transfers between devices: 7.36 us -> 12.9 us
    all_to_all x1 -> x0, blocking collectives: 103 us -> none  [shards(): lax.all_to_all(produced.reshape(arrived.shape), ('grp', 'sa', 'sb'), spli...]
    all_to_all x0 -> x1, waiting for transfers between devices: none -> 103 us  [shards(): lax.all_to_all(produced.reshape(arrived.shape), ('grp', 'sa', 'sb'), spli...]
    all_to_all x0 -> x1, starting transfers between devices: none -> 5.59 us  [shards(): lax.all_to_all(produced.reshape(arrived.shape), ('grp', 'sa', 'sb'), spli...]
  transfers between devices with their start and end apart: 4 -> 5, of which waited for: 3 -> 4; matrix products, arithmetic and copies ran while one was open for 3% -> 3% of each run, Pallas kernels for 5% -> 5%
where the time goes in v14:
time: 410 us; the launch traced here: 408 us
  waiting for transfers between devices  174 us (42%)
  blocking collectives  128 us (31%)
  matrix products  42 us (10%)
  Pallas kernels  19.3 us (5%)
  between operations  13.7 us (3%)
  starting transfers between devices  12.9 us (3%)
  local copies, waits for them, and re-layouts  12.8 us (3%)
  other arithmetic  5.33 us (1%)
    all_to_all x1, blocking collectives, shards(): lax.all_to_all(outgoing_rows, ('grp', 'sa', 'sb'), split_axis=0, concat_a...  106 us
    all_to_all x1, waiting for transfers between devices, shards(): lax.all_to_all(produced.reshape(arrived.shape), ('grp', 'sa', 'sb'), spli...  103 us
    reduce_scatter x1, waiting for transfers between devices, shards(): lax.psum_scatter(partial_sum.astype(jnp.bfloat16), 'sa', scatter_dimensio...  42.5 us
    all_to_all x1, waiting for transfers between devices, shards(): lax.all_to_all(jnp.broadcast_to(kv_col[None], (n_sb,) + kv_col.shape), 's...  24.8 us
    all_to_all x1, blocking collectives, shards(): lax.all_to_all(jnp.concatenate([q_send, kv_send], axis=2), 'sa', split_ax...  21.9 us
    pallas_call x1, Pallas kernels, attention(): pl.pallas_call(kernel, out_shape=jax.ShapeDtypeStruct((rows, heads * head...  19.3 us
    dot_general x1, matrix products, shards(): projected = jnp.dot(flat_rows, w_in[0], preferred_element_type=jnp.float32)  15.8 us
    dot_general x1, matrix products, shards(): jnp.dot(hidden, w_down[0], preferred_element_type=jnp.float32)  8.85 us
  transfers between devices with their start and end apart: 5, of which 4 were waited for; matrix products, arithmetic and copies ran while one was open for 3% of the time, Pallas kernels for 5%

profile of v14, /device:TPU:7, one launch (start us, length us, event | category | flops | bytes accessed | tf_op | source)
XLA Modules:
  0.0 408.0 jit_solution(2923385929785021049)
XLA Ops:
  6.5 1.6 copy-done
  8.1 1.1 constant_dynamic-slice_fusion
  9.2 1.0 copy.49
  10.3 0.1 copy.50
  10.4 0.6 gather_fusion
  11.1 0.1 select_bitcast_fusion
  11.2 0.2 copy.51
  11.3 0.1 copy.52
  11.5 0.1 copy.58
  11.6 0.1 pad_maximum_fusion
  11.7 21.9 %all_to_all.20 = bf16[4,128,1280]{2,1,0:T(8,128)(2,1)S(1)} all-to-all(bf16[4,128,1280]{2,1,0:T(8,128)(2,1)S(1)} %pad_maximum_fusion), channel_id=1, replica_groups=mesh['grp'=8,'sa'=4,'sb'=4] {'sa'}, dimensions={0} | all-to-all | bytes 2621440 | tf_op jit(solution)/shard_map/all_to_all | solution.py:103
  33.6 1.2 broadcast_in_dim.35
  34.8 4.2 %all-to-all-start.1 = ((bf16[4,4,128,256]{3,2,1,0:T(8,128)(2,1)}), bf16[4,4,128,256]{3,2,1,0:T(8,128)(2,1)}, u32[]{:S(2)}, u32[]{:S(2)}) async-start(bf16[4,4,128,256]{3,2,1,0:T(8,128)(2,1)} %broadcast_in_dim.35), calls=%async_computation.1 | async-start | bytes 2097152 | tf_op jit(solution)/shard_map/all_to_all | solution.py:108
  39.0 0.0 reduce-scatter.2.cloned.1.call-start
  39.1 0.1 pad_add_fusion.meta_ref
  39.2 1.3 slice.50
  40.5 24.8 %all-to-all-done.1 = bf16[4,4,128,256]{3,2,1,0:T(8,128)(2,1)} async-done(((bf16[4,4,128,256]{3,2,1,0:T(8,128)(2,1)}), bf16[4,4,128,256]{3,2,1,0:T(8,128)(2,1)}, u32[]{:S(2)}, u32[]{:S(2)}) %all-to-all-start.1) | async-done | bytes 1048608 | tf_op jit(solution)/shard_map/all_to_all | solution.py:108
  65.3 1.3 copy.53
  66.6 19.3 %shard_map.91 = bf16[512,1024]{1,0:T(8,128)(2,1)S(1)} custom-call(s32[2]{0:T(128)S(1)} %pad_add_fusion.meta_ref, bf16[512,1024]{1,0:T(8,128)(2,1)S(1)} %bitcast.42, bf16[2048,256]{1,0:T(8,128)(2,1)S(1)} %bitcast.40, bf16[2048,256]{1,0:T(8,128)(2,1)S(1)} %bitcast.41), custom_call_target="tpu_custom_call" | custom-call | tf_op jit(solution)/shard_map/pallas_call | solution.py:53
  85.9 0.0 all-gather.2.cloned.1.call-done
  85.9 3.1 collective-permute-start
  89.0 2.8 constant_dynamic-update-slice_fusion.1
  91.8 4.2 %collective-permute-done = bf16[1024,2048]{1,0:T(8,128)(2,1)S(1)} collective-permute-done((bf16[1024,2048]{1,0:T(8,128)(2,1)}, bf16[1024,2048]{1,0:T(8,128)(2,1)S(1)}, u32[]{:S(2)}, u32[]{:S(2)}) %collective-permute-start) | collective-permute-done | bytes 4194336 | tf_op jit(solution)/shard_map/ppermute | solution.py:117
  96.0 0.3 constant_dynamic-update-slice_fusion
  96.3 1.3 convolution_convert_fusion.3
  97.6 1.3 convolution_convert_fusion.2
  98.8 1.3 convolution_convert_fusion.1
  100.1 3.5 add_convert_fusion
  103.7 0.6 copy-done.8
  104.3 0.1 copy.54
  104.4 0.1 eq.32
  104.5 0.3 fusion.17
  104.9 0.1 convert_element_type.98
  105.0 0.1 copy.55
  105.1 0.4 fusion.14
  105.4 42.5 %reduce-scatter.2.cloned.1.call-done = bf16[128,4096]{1,0:T(8,128)(2,1)} async-done(((bf16[512,4096]{1,0:T(8,128)(2,1)}), bf16[128,4096]{1,0:T(8,128)(2,1)}) %reduce-scatter.2.cloned.1.call-update) | async-done | bytes 1048592 | tf_op jit(solution)/shard_map/reduce_scatter | solution.py:127
  147.9 1.9 multiply_reduce_fusion
  149.9 2.4 convert_bitcast_fusion.1
  152.3 105.9 %all_to_all.21 = bf16[128,8,4096]{2,1,0:T(8,128)(2,1)S(1)} all-to-all(bf16[128,8,4096]{2,1,0:T(8,128)(2,1)S(1)} %convert_bitcast_fusion.1), channel_id=1, replica_groups=mesh['grp'=8,'sa'=4,'sb'=4] {'grp','sa','sb'}, dimensions={0} | all-to-all | bytes 16777216 | tf_op jit(solution)/shard_map/all_to_all | solution.py:161
  258.2 15.8 %fusion = f32[1024,1536]{1,0:T(8,128)S(1)} fusion(bf16[1,4096,1536]{2,1,0:T(8,128)(2,1)} %param.14, bf16[128,8,4096]{2,1,0:T(8,128)(2,1)S(1)} %all_to_all.21), kind=kOutput, calls=%fused_computation.1 | convolution fusion | flops 12884901888 | bytes 27262976 | tf_op jit(solution)/shard_map/dot_general | solution.py:163
  274.1 8.9 %convert_bitcast_fusion = bf16[128,8,4096]{2,1,0:T(8,128)(2,1)} fusion(bf16[1,768,4096]{2,1,0:T(8,128)(2,1)S(1)} %bitcast.49, f32[1024,1536]{1,0:T(8,128)S(1)} %fusion), kind=kOutput, calls=%fused_computation.6 | convolution fusion | flops 6451363840 | bytes 20971520 | tf_op jit(solution)/shard_map/dot_general | solution.py:165
  282.9 5.6 %all-to-all-start.3 = ((bf16[128,8,4096]{2,1,0:T(8,128)(2,1)}), bf16[128,8,4096]{2,1,0:T(8,128)(2,1)}, u32[]{:S(2)}, u32[]{:S(2)}) async-start(bf16[128,8,4096]{2,1,0:T(8,128)(2,1)} %convert_bitcast_fusion), calls=%async_computation.4 | async-start | bytes 16777216 | tf_op jit(solution)/shard_map/all_to_all | solution.py:166
  288.5 0.3 select_reduce_fusion
  288.8 0.1 fusion.31
  288.9 0.9 pad_maximum_fusion.1
  289.9 102.6 %all-to-all-done.3 = bf16[128,8,4096]{2,1,0:T(8,128)(2,1)} async-done(((bf16[128,8,4096]{2,1,0:T(8,128)(2,1)}), bf16[128,8,4096]{2,1,0:T(8,128)(2,1)}, u32[]{:S(2)}, u32[]{:S(2)}) %all-to-all-start.3) | async-done | bytes 8388640 | tf_op jit(solution)/shard_map/all_to_all | solution.py:166
  392.5 7.3 %fusion.7 = f32[128,4096]{1,0:T(8,128)S(1)} fusion(bf16[3,128,1024]{2,1,0:T(8,128)(2,1)} %bitcast.46, bf16[128,8,4096]{2,1,0:T(8,128)(2,1)} %all-to-all-done.3), kind=kOutput, calls=%fused_computation.16 | convolution fusion | flops 3222274048 | bytes 11272192 | tf_op jit(solution)/shard_map/dot_general | solution.py:180
  399.8 1.4 add_convert_fusion.1
  (34 shorter events, 0.2 us)
Async XLA Ops:
  6.5 1.6 copy-start
  6.5 5.0 %copy-start.6 = (bf16[128,4096]{1,0:T(8,128)(2,1)S(1)}, bf16[128,4096]{1,0:T(8,128)(2,1)}, u32[]{:S(2)}) copy-start(bf16[128,4096]{1,0:T(8,128)(2,1)} %param.9) | copy-start | bytes 3145732
  6.5 79.4 %all-gather.2.cloned.1.call-start = ((), (), s32[]{:S(2)}) async-start(), calls=%async_computation.5 | async-start | bytes 5242880 | tf_op jit(solution)/shard_map/all_gather | solution.py:95
  33.6 5.5 %copy-start.5 = (bf16[4,128,1280]{2,1,0:T(8,128)(2,1)}, bf16[4,128,1280]{2,1,0:T(8,128)(2,1)S(1)}, u32[]{:S(2)}) copy-start(bf16[4,128,1280]{2,1,0:T(8,128)(2,1)S(1)} %all_to_all.20) | copy-start | bytes 3932164
  34.8 30.5 %all-to-all-start.1 = ((bf16[4,4,128,256]{3,2,1,0:T(8,128)(2,1)}), bf16[4,4,128,256]{3,2,1,0:T(8,128)(2,1)}, u32[]{:S(2)}, u32[]{:S(2)}) async-start(bf16[4,4,128,256]{3,2,1,0:T(8,128)(2,1)} %broadcast_in_dim.35), calls=%async_computation.1 | async-start | bytes 2097152 | tf_op jit(solution)/shard_map/all_to_all | solution.py:108
  39.0 108.9 %reduce-scatter.2.cloned.1.call-start = ((), (), s32[]{:S(2)}) async-start(), calls=%async_computation.6 | async-start | bytes 5242880 | tf_op jit(solution)/shard_map/reduce_scatter | solution.py:127
  85.9 10.1 %collective-permute-start = (bf16[1024,2048]{1,0:T(8,128)(2,1)}, bf16[1024,2048]{1,0:T(8,128)(2,1)S(1)}, u32[]{:S(2)}, u32[]{:S(2)}) collective-permute-start(bf16[1024,2048]{1,0:T(8,128)(2,1)} %all-gather.2.cloned.1.call-done), channel_id=1, source_target_pairs={{0,16},{16,0},{32,48},{48,32},{64,80},{80,64},{96,112},{112,96},{1... | collective-permute-start | bytes 12582920 | tf_op jit(solution)/shard_map/ppermute | solution.py:117
  103.6 0.7 copy-start.8
  103.6 1.4 copy-start.7
  103.6 44.3 %copy-start.2 = (bf16[128,4096]{1,0:T(8,128)(2,1)S(1)}, bf16[128,4096]{1,0:T(8,128)(2,1)}, u32[]{:S(2)}) copy-start(bf16[128,4096]{1,0:T(8,128)(2,1)} %param.11) | copy-start | bytes 3145732
  149.9 2.4 copy-start.3
  152.3 121.7 %slice-start = ((s8[6291456]{0:T(1024)(128)(4,1)}), s8[4194304]{0:T(1024)(128)(4,1)S(1)}, s32[]{:S(2)}) async-start(s8[6291456]{0:T(1024)(128)(4,1)} %bitcast.48), calls=%async_computation.7 | async-start | bytes 8388608
  258.2 15.8 %slice-start.1 = ((s8[6291456]{0:T(1024)(128)(4,1)}), s8[2097152]{0:T(1024)(128)(4,1)S(1)}, s32[]{:S(2)}) async-start(s8[6291456]{0:T(1024)(128)(4,1)} %bitcast.48), calls=%async_computation.8 | async-start | bytes 4194304
  282.9 5.6 %copy-start.9 = (f32[128,4]{0,1:T(4,128)S(1)}, f32[128,4]{0,1:T(4,128)}, u32[]{:S(2)}) copy-start(f32[128,4]{0,1:T(4,128)} %param.17) | copy-start | bytes 6148
  282.9 109.6 %all-to-all-start.3 = ((bf16[128,8,4096]{2,1,0:T(8,128)(2,1)}), bf16[128,8,4096]{2,1,0:T(8,128)(2,1)}, u32[]{:S(2)}, u32[]{:S(2)}) async-start(bf16[128,8,4096]{2,1,0:T(8,128)(2,1)} %convert_bitcast_fusion), calls=%async_computation.4 | async-start | bytes 16777216 | tf_op jit(solution)/shard_map/all_to_all | solution.py:166
  392.5 7.4 %copy-start.4 = (bf16[128,4096]{1,0:T(8,128)(2,1)S(1)}, bf16[128,4096]{1,0:T(8,128)(2,1)}, u32[]{:S(2)}) copy-start(bf16[128,4096]{1,0:T(8,128)(2,1)} %copy-done.3) | copy-start | bytes 3145732
  392.5 8.7 %copy-start.1 = (bf16[256,4096]{1,0:T(8,128)(2,1)S(1)}, bf16[256,4096]{1,0:T(8,128)(2,1)}, u32[]{:S(2)}) copy-start(bf16[256,4096]{1,0:T(8,128)(2,1)} %param.13) | copy-start | bytes 6291460
Sparse Core Ops, SparseCore 0:
  9.4 61.5 all-gather.1
  103.8 44.1 reduce-scatter.1
